TPU v7x, 32 devices: a whole 2x2x4 slice. The times are simulated.
32 devices in a mesh: groups: 2 (over y), patch: 4 (over z), chan: 2 (over x), col: 2 (over core).
Axes of the slice: x: 2, y: 2, z: 4, core: 2. Of those that a mesh axis runs over, the one named last changes fastest.
Arguments:
- features: bfloat16 [1280, 48, 256], P('chan', ('groups', 'patch'), 'col'), parts along dimension 1, may hold values from -16 to 16
- cache_codes: bfloat16 [1280, 16, 256], P('chan', ('groups', 'patch'), 'col'), parts along dimension 1, may hold values from -127 to 127
- cache_scale: float32 [16, 256], P(('groups', 'patch'), 'col'), parts along dimension 0, may hold values from 0.001 to 0.01
- step_index: int32 [2], P('groups'), parts along dimension 0, may hold values from 0 to 999
- gn1_gain: float32 [1280], P('chan'), may hold values from 0.1 to 1.9
- gn1_shift: float32 [1280], P('chan'), may hold values from -3 to 3
- conv1_weight: bfloat16 [3, 3, 1280, 1280], P(None, None, 'patch', 'chan'), may hold values from -0.0546875 to 0.0546875
- conv1_bias: float32 [1280], P('chan'), may hold values from -3 to 3
- temb_weight: bfloat16 [1280, 1280], P(None, 'chan'), may hold values from -0.15625 to 0.15625
- gn2_gain: float32 [1280], P('chan'), may hold values from 0.1 to 1.9
- gn2_shift: float32 [1280], P('chan'), may hold values from -3 to 3
- conv2_weight: bfloat16 [3, 3, 1280, 1280], P(None, None, 'patch', 'chan'), may hold values from -0.0546875 to 0.0546875
- conv2_bias: float32 [1280], P('chan'), may hold values from -3 to 3
Outputs:
- block_out: bfloat16 [1280, 48, 256], P('chan', ('groups', 'patch'), 'col'), parts along dimension 1
There are 2 independent parts, one for each index of `groups`. A program takes and returns all parts, laid end to end along the dimension named above; an argument that names none is the same for every part. Nothing has to cross between parts.
All inputs are finite; a program needn't handle non-finite values.
Results may differ from a plain program's by a relative error of at most 0.009.
Values may be sent and summed in bfloat16 or wider, within the bound.
No kernel may reach another device: no remote copies, remote signals or barrier semaphores. Data moves between devices by JAX's collectives and lax.ppermute only.
A program may use at most 128 MiB of HBM per device.

v0:
```python
import math

import jax
import jax.numpy as jnp
from jax import lax
from jax.sharding import PartitionSpec as P

GROUPS = 32


norm_epsilon = 1e-05


def extended(value, sides, width):
    for axis, dim in sides:
        count, length = (lax.axis_size(axis), value.shape[dim])
        up = [(i, (i + 1) % count) for i in range(count - 1)]
        down = [(j, i) for i, j in up]
        last = lax.slice_in_dim(value, length - width, length, axis=dim)
        leading = lax.slice_in_dim(value, 0, width, axis=dim)
        before = lax.ppermute(last, axis, up)
        after = lax.ppermute(leading, axis, down)
        value = jnp.concatenate([before, value, after], axis=dim)
    return value


def group_moments(values, group_count, cell_total):
    grouped = values.reshape(group_count, -1)
    local_sums = (jnp.sum(grouped, axis=1), jnp.sum(grouped * grouped, axis=1))
    summed = jnp.stack(local_sums)
    if lax.axis_size("col") == 2:
        summed = summed + swap(summed, "col")
    else:
        summed = lax.psum(summed, "col")
    n_p = lax.axis_size("patch")
    if n_p & (n_p - 1) == 0:
        step = 1
        while step < n_p:
            summed = summed + lax.ppermute(summed, "patch", [(i, i ^ step) for i in range(n_p)])
            step *= 2
    else:
        summed = lax.psum(summed, "patch")
    totals = (summed[0], summed[1])
    group_mean = totals[0] / cell_total
    group_var = totals[1] / cell_total - group_mean * group_mean
    return (group_mean, lax.rsqrt(group_var + norm_epsilon))


def activate(values, group_mean, inv_std, gain_vec, shift_vec):
    channels = values.shape[0]
    width = channels // group_mean.shape[0]
    shape_tail = (channels,) + (1,) * (values.ndim - 1)
    mean_chan = jnp.repeat(group_mean, width).reshape(shape_tail)
    inv_chan = jnp.repeat(inv_std, width).reshape(shape_tail)
    normed = (values - mean_chan) * inv_chan * gain_vec.reshape(shape_tail) + shift_vec.reshape(
        shape_tail
    )
    return jax.nn.silu(normed)


def swap(value, axis):
    return lax.ppermute(value, axis, [(0, 1), (1, 0)])


def fetch_weights(weights):
    taps = weights.shape[0] * weights.shape[1]
    out_block, in_block = weights.shape[2], weights.shape[3]
    flat = weights.reshape(taps, out_block, in_block)
    share_y = lax.axis_size("groups") == 2
    n_y = 2 if share_y else 1
    n_c = lax.axis_size("col")
    y_id = lax.axis_index("groups") if share_y else 0
    c_id = lax.axis_index("col")
    piece = out_block // (n_y * n_c)
    own = y_id * n_c + c_id
    mine = lax.dynamic_slice_in_dim(flat, own * piece, piece, axis=1)
    got = lax.all_gather(mine, "patch", axis=0, tiled=False)
    slots, ids = [got], [own]
    if share_y:
        slots.append(swap(got, "groups"))
        ids.append((1 - y_id) * n_c + c_id)
    if n_c == 2:
        for i in range(len(slots)):
            slots.append(swap(slots[i], "col"))
            ids.append(ids[i] - c_id + (1 - c_id))
    return slots, ids


def conv_slots(padded, slots):
    in_chans, height_pad, width_pad = padded.shape
    height = height_pad - 2
    width = width_pad - 2
    windows = [
        [padded[:, a : a + height, b : b + width] for b in range(3)] for a in range(3)
    ]
    outs = []
    for got in slots:
        total = None
        for a in range(3):
            for b in range(3):
                term = jnp.einsum(
                    "poc,chw->pohw",
                    got[:, a * 3 + b],
                    windows[a][b],
                    preferred_element_type=jnp.float32,
                )
                total = term if total is None else total + term
        outs.append(total.astype(jnp.bfloat16))
    return jnp.stack(outs)


def reduce_chan(parts, ids):
    n_slots, blocks, piece, height, width = parts.shape
    n_k = lax.axis_size("chan")
    k = lax.axis_index("chan")
    per = blocks // n_k
    if n_k == 2:
        mine = lax.dynamic_slice_in_dim(parts, k * per, per, axis=1)
        other = lax.dynamic_slice_in_dim(parts, (1 - k) * per, per, axis=1)
        total = mine.astype(jnp.float32) + swap(other, "chan").astype(jnp.float32)
    else:
        split = parts.reshape(n_slots, n_k, per, piece, height, width)
        split = jnp.moveaxis(split, 1, 0)
        got = lax.all_to_all(split, "chan", 0, 0, tiled=False)
        total = jnp.sum(got.astype(jnp.float32), axis=0)
    where = jnp.zeros((n_slots,), jnp.int32)
    for slot, ident in enumerate(ids):
        where = where.at[ident].set(slot)
    ordered = jnp.take(total, where, axis=0)
    ordered = jnp.moveaxis(ordered, 0, 1)
    return ordered.reshape(per * n_slots * piece, height, width)


def line_weights(weights, after=None):
    taps = weights.shape[0] * weights.shape[1]
    out_block, in_block = weights.shape[2], weights.shape[3]
    flat = weights.reshape(taps, out_block, in_block)
    if after is not None:
        flat, _ = lax.optimization_barrier((flat, after))
    n_p, n_c = lax.axis_size("patch"), lax.axis_size("col")
    p, c, y = lax.axis_index("patch"), lax.axis_index("col"), lax.axis_index("groups")
    half = out_block // 2
    own_half = lax.dynamic_slice_in_dim(flat, y * half, half, axis=1)
    own_other = lax.dynamic_slice_in_dim(flat, (1 - y) * half, half, axis=1)
    per_core = n_p // n_c
    needs = lambda z, cc, s: cc * per_core <= s < (cc + 1) * per_core
    bufs = {"own": own_half, "own_o": own_other}
    last = {1: own_half, -1: own_half}
    lines = []
    for t in range(1, n_p):
        for d in (1, -1):
            pairs = [((z - d) * n_c + cc, z * n_c + cc)
                     for z in range(n_p) for cc in range(n_c)
                     if 0 <= z - d < n_p and needs(z, cc, z - d * t)]
            if not pairs:
                continue
            got = lax.ppermute(last[d], ("patch", "col"), pairs)
            last[d] = got
            bufs[(t, d)] = got
            lines.append(got)
            trade = [((g * n_p + z) * n_c + cc, ((1 - g) * n_p + z) * n_c + cc)
                     for g in range(2) for z in range(n_p) for cc in range(n_c)
                     if 0 <= z - d < n_p and needs(z, cc, z - d * t)]
            bufs[(t, d, "o")] = lax.ppermute(got, ("groups", "patch", "col"), trade)
    names = sorted(bufs, key=str)
    operands = [bufs[n] for n in names]

    def branch(z, cc, g):
        def run(*ops):
            table = dict(zip(names, ops))
            pieces = []
            for r in range(per_core):
                s = cc * per_core + r
                if s == z:
                    mine, other = table["own"], table["own_o"]
                else:
                    d = 1 if s < z else -1
                    t = abs(z - s)
                    mine, other = table[(t, d)], table[(t, d, "o")]
                pieces += [mine, other] if g == 0 else [other, mine]
            return jnp.concatenate(pieces, axis=1)
        return run

    cases = [branch(z, cc, g) for g in range(2) for z in range(n_p) for cc in range(n_c)]
    index = (y * n_p + p) * n_c + c
    return lax.switch(index, cases, *operands), lines


def full_width(block):
    other = swap(block, "col")
    c = lax.axis_index("col")
    left = jnp.where(c == 0, block, other)
    right = jnp.where(c == 0, other, block)
    return jnp.pad(jnp.concatenate([left, right], axis=2), ((0, 0), (0, 0), (1, 1)))


def conv_full(padded, weight):
    kernel = weight.reshape(3, 3, weight.shape[1], weight.shape[2])
    total = lax.conv_general_dilated(
        padded[None],
        kernel,
        window_strides=(1, 1),
        padding="VALID",
        dimension_numbers=("NCHW", "HWOI", "NCHW"),
        preferred_element_type=jnp.float32,
    )[0]
    return total.astype(jnp.bfloat16)


def reduce_cores(part):
    k, c = lax.axis_index("chan"), lax.axis_index("col")
    width = part.shape[2] // 2
    piece = lambda j: lax.dynamic_slice_in_dim(part, j * width, width, axis=2)
    send_a = piece(jnp.where(k == c, 1 - c, c))
    got_a = lax.ppermute(send_a, ("chan", "col"), [(0, 1), (3, 2), (1, 3), (2, 0)])
    got_b = lax.ppermute(piece(1 - c), ("chan", "col"), [(1, 2), (2, 1)])
    first = jnp.where(k == c, piece(c), got_b)
    return first.astype(jnp.float32) + got_a.astype(jnp.float32)


def fast_path():
    return (
        lax.axis_size("chan") == 2
        and lax.axis_size("col") == 2
        and lax.axis_size("groups") == 2
        and lax.axis_size("patch") % 2 == 0
    )


def time_bias(step_index, temb_weight):
    half_width = temb_weight.shape[0] // 2
    freqs = jnp.exp(-math.log(10000.0) * jnp.arange(half_width).astype(jnp.float32) / half_width)
    angles = step_index[0].astype(jnp.float32) * freqs
    embed = jnp.concatenate([jnp.cos(angles), jnp.sin(angles)])
    gated = jax.nn.silu(embed).astype(jnp.bfloat16)
    return jnp.dot(gated[None, :], temb_weight, preferred_element_type=jnp.float32)[0]


def on_device(
    features,
    cache_codes,
    cache_scale,
    step_index,
    gn1_gain,
    gn1_shift,
    conv1_weight,
    conv1_bias,
    temb_weight,
    gn2_gain,
    gn2_shift,
    conv2_weight,
    conv2_bias,
):
    channels, rows_here, cols_here = features.shape
    patches = lax.axis_size("patch")
    group_count = GROUPS // lax.axis_size("chan")
    cell_total = channels // group_count * rows_here * patches * cols_here * lax.axis_size("col")
    fast = fast_path()
    feat32 = features.astype(jnp.float32)
    mean_one, inv_one = group_moments(feat32, group_count, cell_total)
    if fast:
        weight_one, lines_one = line_weights(conv1_weight)
        weight_two, _ = line_weights(conv2_weight)
    else:
        slots_one, ids_one = fetch_weights(conv1_weight)
        slots_two, ids_two = fetch_weights(conv2_weight)
    own_act = activate(feat32, mean_one, inv_one, gn1_gain, gn1_shift)
    stale = cache_codes.astype(jnp.float32) * cache_scale[None, :, :]
    rim_act = activate(stale, mean_one, inv_one, gn1_gain, gn1_shift)
    where_patch = lax.axis_index("patch")
    upper_rim = rim_act[:, 0:1, :] * (where_patch > 0).astype(jnp.float32)
    lower_rim = rim_act[:, 1:2, :] * (where_patch < patches - 1).astype(jnp.float32)
    block_one = jnp.concatenate([upper_rim, own_act, lower_rim], axis=1).astype(jnp.bfloat16)
    if fast:
        sum_one = reduce_cores(conv_full(full_width(block_one), weight_one))
    else:
        padded_one = extended(block_one, (("col", 2),), 1)
        sum_one = reduce_chan(conv_slots(padded_one, slots_one), ids_one)
    temb_bias = time_bias(step_index, temb_weight)
    hidden = (sum_one + conv1_bias[:, None, None] + temb_bias[:, None, None]).astype(jnp.bfloat16)
    hidden32 = hidden.astype(jnp.float32)
    mean_two, inv_two = group_moments(hidden32, group_count, cell_total)
    act_two = activate(hidden32, mean_two, inv_two, gn2_gain, gn2_shift).astype(jnp.bfloat16)
    if fast:
        rows_two = extended(act_two, (("patch", 1),), 1)
        sum_two = reduce_cores(conv_full(full_width(rows_two), weight_two))
    else:
        padded_two = extended(act_two, (("patch", 1), ("col", 2)), 1)
        sum_two = reduce_chan(conv_slots(padded_two, slots_two), ids_two)
    return (sum_two + conv2_bias[:, None, None] + feat32).astype(jnp.bfloat16)


def solution(mesh):
    return jax.shard_map(
        on_device,
        mesh=mesh,
        in_specs=(
            P("chan", ("groups", "patch"), "col"),
            P("chan", ("groups", "patch"), "col"),
            P(("groups", "patch"), "col"),
            P("groups"),
            P("chan"),
            P("chan"),
            P(None, None, "patch", "chan"),
            P("chan"),
            P(None, "chan"),
            P("chan"),
            P("chan"),
            P(None, None, "patch", "chan"),
            P("chan"),
        ),
        out_specs=P("chan", ("groups", "patch"), "col"),
        check_vma=False,
    )
```

profile of v0, /device:TPU:0, one launch (start us, length us, event | category | flops | bytes accessed | tf_op | source)
XLA Modules:
  0.0 337.6 jit_solution(1178170251067071927)
XLA Ops:
  5.1 7.5 %collective-permute-start.10 = (bf16[9,160,640]{2,1,0:T(8,128)(2,1)S(1)}, bf16[9,160,640]{2,1,0:T(8,128)(2,1)}, u32[]{:S(2)}, u32[]{:S(2)}) collective-permute-start(bf16[9,160,640]{2,1,0:T(8,128)(2,1)S(1)} %get-tuple-element.431), channel_id=1, source_target_pairs={{0,4},{4,8},{9,13},{2,6},{6,10},{11,15},{16,20},{20,24},{25,29},{1... | collective-permute-start | bytes 5529608 | tf_op jit(solution)/shard_map/ppermute | solution.py:157
  14.7 17.4 %collective-permute-done.1 = f32[2,16]{1,0:T(2,128)S(1)} collective-permute-done((f32[2,16]{1,0:T(2,128)S(1)}, f32[2,16]{1,0:T(2,128)S(1)}, u32[]{:S(2)}, u32[]{:S(2)}) %collective-permute-start.1) | collective-permute-done | bytes 160 | tf_op jit(solution)/shard_map/ppermute | solution.py:39
  32.2 4.5 %collective-permute-done.2 = f32[2,16]{1,0:T(2,128)S(1)} collective-permute-done((f32[2,16]{1,0:T(2,128)S(1)}, f32[2,16]{1,0:T(2,128)S(1)}, u32[]{:S(2)}, u32[]{:S(2)}) %collective-permute-start.2) | collective-permute-done | bytes 160 | tf_op jit(solution)/shard_map/ppermute | solution.py:39
  47.3 6.4 %collective-permute-start.30 = (bf16[9,160,640]{2,1,0:T(8,128)(2,1)}, bf16[9,160,640]{2,1,0:T(8,128)(2,1)}, u32[]{:S(2)}, u32[]{:S(2)}) collective-permute-start(bf16[9,160,640]{2,1,0:T(8,128)(2,1)} %get-tuple-element.433), channel_id=1, source_target_pairs={{0,4},{4,8},{9,13},{2,6},{6,10},{11,15},{16,20},{20,24},{25,29},{1... | collective-permute-start | bytes 5529608 | tf_op jit(solution)/shard_map/ppermute | solution.py:157
  53.6 4.5 %collective-permute-start.5 = (bf16[9,160,640]{2,1,0:T(8,128)(2,1)}, bf16[9,160,640]{2,1,0:T(8,128)(2,1)}, u32[]{:S(2)}, u32[]{:S(2)}) collective-permute-start(bf16[9,160,640]{2,1,0:T(8,128)(2,1)} %collective-permute-done.4), channel_id=1, source_target_pairs={{0,16},{5,21},{9,25},{16,0},{21,5},{25,9},{2,18},{7,23},{11,27},{1... | collective-permute-start | bytes 5529608 | tf_op jit(solution)/shard_map/ppermute | solution.py:164
  65.0 8.5 %collective-permute-done.30 = bf16[9,160,640]{2,1,0:T(8,128)(2,1)} collective-permute-done((bf16[9,160,640]{2,1,0:T(8,128)(2,1)}, bf16[9,160,640]{2,1,0:T(8,128)(2,1)}, u32[]{:S(2)}, u32[]{:S(2)}) %collective-permute-start.30) | collective-permute-done | bytes 1843232 | tf_op jit(solution)/shard_map/ppermute | solution.py:157
  74.8 12.2 %collective-permute-done.5 = bf16[9,160,640]{2,1,0:T(8,128)(2,1)} collective-permute-done((bf16[9,160,640]{2,1,0:T(8,128)(2,1)}, bf16[9,160,640]{2,1,0:T(8,128)(2,1)}, u32[]{:S(2)}, u32[]{:S(2)}) %collective-permute-start.5) | collective-permute-done | bytes 1843232 | tf_op jit(solution)/shard_map/ppermute | solution.py:164
  96.6 4.0 %fusion.7 = bf16[640,8,1,258]{3,0,1,2:T(8,128)(2,1)} fusion(bf16[640,8,128]{2,0,1:T(8,128)(2,1)S(1)} %get-tuple-element.437, bf16[640,8,128]{2,0,1:T(8,128)(2,1)S(1)} %get-tuple-element.436), kind=kLoop, calls=%fused_computation.45 | loop fusion | flops 11888640 | bytes 5263360 | tf_op jit(solution)/shard_map/broadcast_in_dim | solution.py:200
  100.6 5.9 %copy.86 = bf16[640,8,1,258]{0,1,3,2:T(8,128)(2,1)} copy(bf16[640,8,1,258]{3,0,1,2:T(8,128)(2,1)} %fusion.7) | data formatting | bytes 5283840
  113.7 6.5 %conditional.2 = (bf16[3,3,640,640]{3,2,1,0:T(8,128)(2,1)}) conditional(s32[]{:T(128)} %clamp.4, (bf16[9,160,640]{2,1,0:T(8,128)(2,1)S(1)}, bf16[9,160,640]{2,1,0:T(8,128)(2,1)S(1)}, bf16[9,160,640]{2,1,0:T(8,128)(2,1)}, bf16[9,160,640]{2,1,0:T(8,128)(2,1)}) %tuple.211, (bf16[9,160,640]{2,1,0:T(8,128)(2,1)}, ...), branch_computations={%region_4.0_spmd, %region_5.0_spmd, %region_6.0_spmd, %region_7.0_... | conditional | flops 29491200 | bytes 14745608 | solution.py:186
  113.7 6.5 %pad_maximum_fusion = bf16[9,640,640]{2,1,0:T(8,128)(2,1)} fusion(bf16[9,160,640]{2,1,0:T(8,128)(2,1)} %get-tuple-element.273, bf16[9,160,640]{2,1,0:T(8,128)(2,1)} %get-tuple-element.272, bf16[9,160,640]{2,1,0:T(8,128)(2,1)S(1)} %get-tuple-element.271, bf16[9,160,640]{2,1,0:T(8,128)(2,1)S(1)} %get-tuple-element.270), kind=kLoop, calls=%fused_computation | loop fusion | flops 29491200 | bytes 14745600 | tf_op jit(solution)/shard_map/cond/branch_0_fun/concatenate | solution.py:181
  120.2 18.2 %select_convert_fusion.1 = bf16[6,8,33,640]{3,1,2,0:T(8,128)(2,1)S(1)} fusion(pred[8,33]{0,1:T(8,128)(4,1)S(1)} %copy-done.22, bf16[3,3,640,640]{3,2,1,0:T(8,128)(2,1)} %get-tuple-element.450, bf16[640,8,1,7,2]{0,3,4,1,2:T(8,128)(2,1)} %slice.38, bf16[640,8,1,8,33]{0,3,4,1,2:T(8,128)(2,1)} %copy-done.9), kind=kOutput, calls=%fused_computation.39 | convolution fusion | flops 11689144320 | bytes 12247304 | tf_op jit(solution)/shard_map/conv_general_dilated | solution.py:199
  140.3 4.1 %reshape.162 = bf16[6,1,264,640]{3,2,0,1:T(8,128)(2,1)} reshape(bf16[6,8,33,640]{3,2,1,0:T(8,128)(2,1)} %copy.71) | data formatting | bytes 4055040 | tf_op jit(solution)/shard_map/convert_element_type | solution.py:207
  154.0 7.2 %collective-permute-start.17 = (bf16[640,6,128]{2,0,1:T(8,128)(2,1)}, bf16[640,6,128]{2,0,1:T(8,128)(2,1)}, u32[]{:S(2)}, u32[]{:S(2)}) collective-permute-start(bf16[640,6,128]{2,0,1:T(8,128)(2,1)} %bitcast.141), channel_id=1, source_target_pairs={{0,1},{3,2},{1,3},{2,0},{4,5},{7,6},{5,7},{6,4},{8,9},{11,10},{9,1... | collective-permute-start | bytes 2949128 | tf_op jit(solution)/shard_map/ppermute | solution.py:215
  169.6 13.7 %collective-permute-done.17 = bf16[640,6,128]{2,0,1:T(8,128)(2,1)} collective-permute-done((bf16[640,6,128]{2,0,1:T(8,128)(2,1)}, bf16[640,6,128]{2,0,1:T(8,128)(2,1)}, u32[]{:S(2)}, u32[]{:S(2)}) %collective-permute-start.17) | collective-permute-done | bytes 983072 | tf_op jit(solution)/shard_map/ppermute | solution.py:215
  187.8 7.8 %collective-permute-start.19 = (f32[2,16]{1,0:T(2,128)S(1)}, f32[2,16]{1,0:T(2,128)S(1)}, u32[]{:S(2)}, u32[]{:S(2)}) collective-permute-start(f32[2,16]{1,0:T(2,128)S(1)} %fusion.63), channel_id=1, source_target_pairs={{0,4},{4,0},{8,12},{12,8},{1,5},{5,1},{9,13},{13,9},{2,6},{6,2},{1... | collective-permute-start | bytes 392 | tf_op jit(solution)/shard_map/ppermute | solution.py:39
  199.1 6.5 %collective-permute-start.20 = (f32[2,16]{1,0:T(2,128)S(1)}, f32[2,16]{1,0:T(2,128)S(1)}, u32[]{:S(2)}, u32[]{:S(2)}) collective-permute-start(f32[2,16]{1,0:T(2,128)S(1)} %fusion.70), channel_id=1, source_target_pairs={{0,8},{4,12},{8,0},{12,4},{1,9},{5,13},{9,1},{13,5},{2,10},{6,14},... | collective-permute-start | bytes 392 | tf_op jit(solution)/shard_map/ppermute | solution.py:39
  224.2 7.4 %conditional.3 = (bf16[3,3,640,640]{3,2,1,0:T(8,128)(2,1)}) conditional(s32[]{:T(128)} %clamp.4, (bf16[9,160,640]{2,1,0:T(8,128)(2,1)}, bf16[9,160,640]{2,1,0:T(8,128)(2,1)S(1)}, bf16[9,160,640]{2,1,0:T(8,128)(2,1)}, bf16[9,160,640]{2,1,0:T(8,128)(2,1)}) %tuple.145, (bf16[9,160,640]{2,1,0:T(8,128)(2,1)}, ...), branch_computations={%region_24.0_spmd, %region_25.0_spmd, %region_26.0_spmd, %region_2... | conditional | flops 29491200 | bytes 14745608 | solution.py:186
  224.2 7.4 %pad_maximum_fusion.16 = bf16[9,640,640]{2,1,0:T(8,128)(2,1)} fusion(bf16[9,160,640]{2,1,0:T(8,128)(2,1)} %get-tuple-element.364, bf16[9,160,640]{2,1,0:T(8,128)(2,1)} %get-tuple-element.363, bf16[9,160,640]{2,1,0:T(8,128)(2,1)S(1)} %get-tuple-element.362, bf16[9,160,640]{2,1,0:T(8,128)(2,1)} %get-tuple-element.361), kind=kLoop, calls=%fused_computation.16 | loop fusion | flops 29491200 | bytes 14745600 | tf_op jit(solution)/shard_map/cond/branch_0_fun/concatenate | solution.py:181
  233.3 4.0 %fusion.3 = bf16[640,8,1,258]{3,0,1,2:T(8,128)(2,1)} fusion(bf16[640,8,128]{2,0,1:T(8,128)(2,1)S(1)} %get-tuple-element.435, bf16[640,8,128]{2,0,1:T(8,128)(2,1)S(1)} %get-tuple-element.434), kind=kLoop, calls=%fused_computation.41 | loop fusion | flops 11888640 | bytes 5263360 | tf_op jit(solution)/shard_map/broadcast_in_dim | solution.py:200
  237.2 5.9 %copy.87 = bf16[640,8,1,258]{0,1,3,2:T(8,128)(2,1)} copy(bf16[640,8,1,258]{3,0,1,2:T(8,128)(2,1)} %fusion.3) | data formatting | bytes 5283840
  245.5 17.4 %select_convert_fusion = bf16[6,8,33,640]{3,1,2,0:T(8,128)(2,1)S(1)} fusion(pred[8,33]{0,1:T(8,128)(4,1)S(1)} %copy-done.22, bf16[3,3,640,640]{3,2,1,0:T(8,128)(2,1)} %get-tuple-element.451, bf16[640,8,1,7,2]{0,3,4,1,2:T(8,128)(2,1)S(1)} %slice.42, bf16[640,8,1,8,33]{0,3,4,1,2:T(8,128)(2,1)S(1)} %copy.75), kind=kOutput, calls=%fused_computation.38 | convolution fusion | flops 11689144320 | bytes 12247304 | tf_op jit(solution)/shard_map/conv_general_dilated | solution.py:199
  275.2 37.1 %collective-permute-start.37 = (bf16[640,6,128]{2,0,1:T(8,128)(2,1)}, bf16[640,6,128]{2,0,1:T(8,128)(2,1)}, u32[]{:S(2)}, u32[]{:S(2)}) collective-permute-start(bf16[640,6,128]{2,0,1:T(8,128)(2,1)} %bitcast.143), channel_id=1, source_target_pairs={{0,1},{3,2},{1,3},{2,0},{4,5},{7,6},{5,7},{6,4},{8,9},{11,10},{9,1... | collective-permute-start | bytes 2949128 | tf_op jit(solution)/shard_map/ppermute | solution.py:215
  314.5 20.0 %collective-permute-done.37 = bf16[640,6,128]{2,0,1:T(8,128)(2,1)} collective-permute-done((bf16[640,6,128]{2,0,1:T(8,128)(2,1)}, bf16[640,6,128]{2,0,1:T(8,128)(2,1)}, u32[]{:S(2)}, u32[]{:S(2)}) %collective-permute-start.37) | collective-permute-done | bytes 983072 | tf_op jit(solution)/shard_map/ppermute | solution.py:215
  (174 shorter events, 109.7 us)
Async XLA Ops:
  3.8 34.9 %collective-permute-start.4 = (bf16[9,160,640]{2,1,0:T(8,128)(2,1)S(1)}, bf16[9,160,640]{2,1,0:T(8,128)(2,1)}, u32[]{:S(2)}, u32[]{:S(2)}) collective-permute-start(bf16[9,160,640]{2,1,0:T(8,128)(2,1)S(1)} %get-tuple-element.431), channel_id=1, source_target_pairs={{4,0},{9,5},{13,9},{6,2},{11,7},{15,11},{20,16},{25,21},{29,25},{2... | collective-permute-start | bytes 5529608 | tf_op jit(solution)/shard_map/ppermute | solution.py:157
  5.1 35.6 %collective-permute-start.10 = (bf16[9,160,640]{2,1,0:T(8,128)(2,1)S(1)}, bf16[9,160,640]{2,1,0:T(8,128)(2,1)}, u32[]{:S(2)}, u32[]{:S(2)}) collective-permute-start(bf16[9,160,640]{2,1,0:T(8,128)(2,1)S(1)} %get-tuple-element.431), channel_id=1, source_target_pairs={{0,4},{4,8},{9,13},{2,6},{6,10},{11,15},{16,20},{20,24},{25,29},{1... | collective-permute-start | bytes 5529608 | tf_op jit(solution)/shard_map/ppermute | solution.py:157
  38.7 22.4 %collective-permute-start.6 = (bf16[9,160,640]{2,1,0:T(8,128)(2,1)}, bf16[9,160,640]{2,1,0:T(8,128)(2,1)}, u32[]{:S(2)}, u32[]{:S(2)}) collective-permute-start(bf16[9,160,640]{2,1,0:T(8,128)(2,1)} %collective-permute-done.4), channel_id=1, source_target_pairs={{5,1},{9,5},{7,3},{11,7},{21,17},{25,21},{23,19},{27,23}} | collective-permute-start | bytes 5529608 | tf_op jit(solution)/shard_map/ppermute | solution.py:157
  40.6 22.4 %collective-permute-start.12 = (bf16[9,160,640]{2,1,0:T(8,128)(2,1)}, bf16[9,160,640]{2,1,0:T(8,128)(2,1)}, u32[]{:S(2)}, u32[]{:S(2)}) collective-permute-start(bf16[9,160,640]{2,1,0:T(8,128)(2,1)} %collective-permute-done.10), channel_id=1, source_target_pairs={{4,8},{8,12},{6,10},{10,14},{20,24},{24,28},{22,26},{26,30}} | collective-permute-start | bytes 5529608 | tf_op jit(solution)/shard_map/ppermute | solution.py:157
  47.3 26.2 %collective-permute-start.30 = (bf16[9,160,640]{2,1,0:T(8,128)(2,1)}, bf16[9,160,640]{2,1,0:T(8,128)(2,1)}, u32[]{:S(2)}, u32[]{:S(2)}) collective-permute-start(bf16[9,160,640]{2,1,0:T(8,128)(2,1)} %get-tuple-element.433), channel_id=1, source_target_pairs={{0,4},{4,8},{9,13},{2,6},{6,10},{11,15},{16,20},{20,24},{25,29},{1... | collective-permute-start | bytes 5529608 | tf_op jit(solution)/shard_map/ppermute | solution.py:157
  53.6 33.4 %collective-permute-start.5 = (bf16[9,160,640]{2,1,0:T(8,128)(2,1)}, bf16[9,160,640]{2,1,0:T(8,128)(2,1)}, u32[]{:S(2)}, u32[]{:S(2)}) collective-permute-start(bf16[9,160,640]{2,1,0:T(8,128)(2,1)} %collective-permute-done.4), channel_id=1, source_target_pairs={{0,16},{5,21},{9,25},{16,0},{21,5},{25,9},{2,18},{7,23},{11,27},{1... | collective-permute-start | bytes 5529608 | tf_op jit(solution)/shard_map/ppermute | solution.py:164
  59.2 29.8 %collective-permute-start.11 = (bf16[9,160,640]{2,1,0:T(8,128)(2,1)}, bf16[9,160,640]{2,1,0:T(8,128)(2,1)}, u32[]{:S(2)}, u32[]{:S(2)}) collective-permute-start(bf16[9,160,640]{2,1,0:T(8,128)(2,1)} %collective-permute-done.10), channel_id=1, source_target_pairs={{4,20},{8,24},{13,29},{20,4},{24,8},{29,13},{6,22},{10,26},{15,31}... | collective-permute-start | bytes 5529608 | tf_op jit(solution)/shard_map/ppermute | solution.py:164
  61.1 29.8 %collective-permute-start.8 = (bf16[9,160,640]{2,1,0:T(8,128)(2,1)}, bf16[9,160,640]{2,1,0:T(8,128)(2,1)}, u32[]{:S(2)}, u32[]{:S(2)}) collective-permute-start(bf16[9,160,640]{2,1,0:T(8,128)(2,1)} %collective-permute-done.6), channel_id=1, source_target_pairs={{5,1},{7,3},{21,17},{23,19}} | collective-permute-start | bytes 5529608 | tf_op jit(solution)/shard_map/ppermute | solution.py:157
  63.1 29.8 %collective-permute-start.14 = (bf16[9,160,640]{2,1,0:T(8,128)(2,1)}, bf16[9,160,640]{2,1,0:T(8,128)(2,1)}, u32[]{:S(2)}, u32[]{:S(2)}) collective-permute-start(bf16[9,160,640]{2,1,0:T(8,128)(2,1)} %collective-permute-done.12), channel_id=1, source_target_pairs={{8,12},{10,14},{24,28},{26,30}} | collective-permute-start | bytes 5529608 | tf_op jit(solution)/shard_map/ppermute | solution.py:157
  73.5 36.3 %collective-permute-start.24 = (bf16[9,160,640]{2,1,0:T(8,128)(2,1)}, bf16[9,160,640]{2,1,0:T(8,128)(2,1)}, u32[]{:S(2)}, u32[]{:S(2)}) collective-permute-start(bf16[9,160,640]{2,1,0:T(8,128)(2,1)} %get-tuple-element.433), channel_id=1, source_target_pairs={{4,0},{9,5},{13,9},{6,2},{11,7},{15,11},{20,16},{25,21},{29,25},{2... | collective-permute-start | bytes 5529608 | tf_op jit(solution)/shard_map/ppermute | solution.py:157
  87.0 24.7 %collective-permute-start.7 = (bf16[9,160,640]{2,1,0:T(8,128)(2,1)}, bf16[9,160,640]{2,1,0:T(8,128)(2,1)}, u32[]{:S(2)}, u32[]{:S(2)}) collective-permute-start(bf16[9,160,640]{2,1,0:T(8,128)(2,1)} %collective-permute-done.6), channel_id=1, source_target_pairs={{1,17},{5,21},{17,1},{21,5},{3,19},{7,23},{19,3},{23,7}} | collective-permute-start | bytes 5529608 | tf_op jit(solution)/shard_map/ppermute | solution.py:164
  89.0 24.7 %collective-permute-start.13 = (bf16[9,160,640]{2,1,0:T(8,128)(2,1)}, bf16[9,160,640]{2,1,0:T(8,128)(2,1)}, u32[]{:S(2)}, u32[]{:S(2)}) collective-permute-start(bf16[9,160,640]{2,1,0:T(8,128)(2,1)} %collective-permute-done.12), channel_id=1, source_target_pairs={{8,24},{12,28},{24,8},{28,12},{10,26},{14,30},{26,10},{30,14}} | collective-permute-start | bytes 5529608 | tf_op jit(solution)/shard_map/ppermute | solution.py:164
  91.0 22.7 %collective-permute-start.9 = (bf16[9,160,640]{2,1,0:T(8,128)(2,1)}, bf16[9,160,640]{2,1,0:T(8,128)(2,1)}, u32[]{:S(2)}, u32[]{:S(2)}) collective-permute-start(bf16[9,160,640]{2,1,0:T(8,128)(2,1)} %collective-permute-done.8), channel_id=1, source_target_pairs={{1,17},{17,1},{3,19},{19,3}} | collective-permute-start | bytes 5529608 | tf_op jit(solution)/shard_map/ppermute | solution.py:164
  92.9 20.8 %collective-permute-start.15 = (bf16[9,160,640]{2,1,0:T(8,128)(2,1)}, bf16[9,160,640]{2,1,0:T(8,128)(2,1)}, u32[]{:S(2)}, u32[]{:S(2)}) collective-permute-start(bf16[9,160,640]{2,1,0:T(8,128)(2,1)} %collective-permute-done.14), channel_id=1, source_target_pairs={{12,28},{28,12},{14,30},{30,14}} | collective-permute-start | bytes 5529608 | tf_op jit(solution)/shard_map/ppermute | solution.py:164
  109.8 54.4 %collective-permute-start.32 = (bf16[9,160,640]{2,1,0:T(8,128)(2,1)}, bf16[9,160,640]{2,1,0:T(8,128)(2,1)}, u32[]{:S(2)}, u32[]{:S(2)}) collective-permute-start(bf16[9,160,640]{2,1,0:T(8,128)(2,1)} %collective-permute-done.30), channel_id=1, source_target_pairs={{4,8},{8,12},{6,10},{10,14},{20,24},{24,28},{22,26},{26,30}} | collective-permute-start | bytes 5529608 | tf_op jit(solution)/shard_map/ppermute | solution.py:157
  111.7 54.4 %collective-permute-start.26 = (bf16[9,160,640]{2,1,0:T(8,128)(2,1)}, bf16[9,160,640]{2,1,0:T(8,128)(2,1)}, u32[]{:S(2)}, u32[]{:S(2)}) collective-permute-start(bf16[9,160,640]{2,1,0:T(8,128)(2,1)} %collective-permute-done.24), channel_id=1, source_target_pairs={{5,1},{9,5},{7,3},{11,7},{21,17},{25,21},{23,19},{27,23}} | collective-permute-start | bytes 5529608 | tf_op jit(solution)/shard_map/ppermute | solution.py:157
  150.1 19.5 %collective-permute-start.16 = (bf16[640,6,128]{2,0,1:T(8,128)(2,1)}, bf16[640,6,128]{2,0,1:T(8,128)(2,1)}, u32[]{:S(2)}, u32[]{:S(2)}) collective-permute-start(bf16[640,6,128]{2,0,1:T(8,128)(2,1)} %bitcast.140), channel_id=1, source_target_pairs={{1,2},{2,1},{5,6},{6,5},{9,10},{10,9},{13,14},{14,13},{17,18},{18,... | collective-permute-start | bytes 2949128 | tf_op jit(solution)/shard_map/ppermute | solution.py:216
  154.0 29.4 %collective-permute-start.17 = (bf16[640,6,128]{2,0,1:T(8,128)(2,1)}, bf16[640,6,128]{2,0,1:T(8,128)(2,1)}, u32[]{:S(2)}, u32[]{:S(2)}) collective-permute-start(bf16[640,6,128]{2,0,1:T(8,128)(2,1)} %bitcast.141), channel_id=1, source_target_pairs={{0,1},{3,2},{1,3},{2,0},{4,5},{7,6},{5,7},{6,4},{8,9},{11,10},{9,1... | collective-permute-start | bytes 2949128 | tf_op jit(solution)/shard_map/ppermute | solution.py:215
  162.2 50.9 %collective-permute-start.31 = (bf16[9,160,640]{2,1,0:T(8,128)(2,1)}, bf16[9,160,640]{2,1,0:T(8,128)(2,1)}, u32[]{:S(2)}, u32[]{:S(2)}) collective-permute-start(bf16[9,160,640]{2,1,0:T(8,128)(2,1)} %collective-permute-done.30), channel_id=1, source_target_pairs={{4,20},{8,24},{13,29},{20,4},{24,8},{29,13},{6,22},{10,26},{15,31}... | collective-permute-start | bytes 5529608 | tf_op jit(solution)/shard_map/ppermute | solution.py:164
  164.2 50.2 %collective-permute-start.34 = (bf16[9,160,640]{2,1,0:T(8,128)(2,1)}, bf16[9,160,640]{2,1,0:T(8,128)(2,1)}, u32[]{:S(2)}, u32[]{:S(2)}) collective-permute-start(bf16[9,160,640]{2,1,0:T(8,128)(2,1)} %collective-permute-done.32), channel_id=1, source_target_pairs={{8,12},{10,14},{24,28},{26,30}} | collective-permute-start | bytes 5529608 | tf_op jit(solution)/shard_map/ppermute | solution.py:157
  166.1 50.3 %collective-permute-start.28 = (bf16[9,160,640]{2,1,0:T(8,128)(2,1)}, bf16[9,160,640]{2,1,0:T(8,128)(2,1)}, u32[]{:S(2)}, u32[]{:S(2)}) collective-permute-start(bf16[9,160,640]{2,1,0:T(8,128)(2,1)} %collective-permute-done.26), channel_id=1, source_target_pairs={{5,1},{7,3},{21,17},{23,19}} | collective-permute-start | bytes 5529608 | tf_op jit(solution)/shard_map/ppermute | solution.py:157
  195.6 28.5 %collective-permute-start.25 = (bf16[9,160,640]{2,1,0:T(8,128)(2,1)}, bf16[9,160,640]{2,1,0:T(8,128)(2,1)}, u32[]{:S(2)}, u32[]{:S(2)}) collective-permute-start(bf16[9,160,640]{2,1,0:T(8,128)(2,1)} %collective-permute-done.24), channel_id=1, source_target_pairs={{0,16},{5,21},{9,25},{16,0},{21,5},{25,9},{2,18},{7,23},{11,27},{1... | collective-permute-start | bytes 5529608 | tf_op jit(solution)/shard_map/ppermute | solution.py:164
  271.3 43.2 %collective-permute-start.36 = (bf16[640,6,128]{2,0,1:T(8,128)(2,1)}, bf16[640,6,128]{2,0,1:T(8,128)(2,1)}, u32[]{:S(2)}, u32[]{:S(2)}) collective-permute-start(bf16[640,6,128]{2,0,1:T(8,128)(2,1)} %bitcast.142), channel_id=1, source_target_pairs={{1,2},{2,1},{5,6},{6,5},{9,10},{10,9},{13,14},{14,13},{17,18},{18,... | collective-permute-start | bytes 2949128 | tf_op jit(solution)/shard_map/ppermute | solution.py:216
  275.2 59.3 %collective-permute-start.37 = (bf16[640,6,128]{2,0,1:T(8,128)(2,1)}, bf16[640,6,128]{2,0,1:T(8,128)(2,1)}, u32[]{:S(2)}, u32[]{:S(2)}) collective-permute-start(bf16[640,6,128]{2,0,1:T(8,128)(2,1)} %bitcast.143), channel_id=1, source_target_pairs={{0,1},{3,2},{1,3},{2,0},{4,5},{7,6},{5,7},{6,4},{8,9},{11,10},{9,1... | collective-permute-start | bytes 2949128 | tf_op jit(solution)/shard_map/ppermute | solution.py:215
  (37 other events, 861.8 us)
where the time goes:
time: 339 us; the launch traced here: 338 us
  starting transfers between devices  126 us (37%)
  waiting for transfers between devices  81.2 us (24%)
  local copies, waits for them, and re-layouts  54.1 us (16%)
  other arithmetic  39.2 us (12%)
  matrix products  35.9 us (11%)
    ppermute x2, starting transfers between devices, reduce_cores(): lax.ppermute(send_a, ('chan', 'col'), [(0, 1), (3, 2), (1, 3), (2, 0)])  44.2 us
    conv_general_dilated x2, matrix products, conv_full(): lax.conv_general_dilated(padded[None], kernel, window_strides=(1, 1), pad...  35.6 us
    ppermute x2, waiting for transfers between devices, reduce_cores(): lax.ppermute(send_a, ('chan', 'col'), [(0, 1), (3, 2), (1, 3), (2, 0)])  33.8 us
    ppermute x12, starting transfers between devices, line_weights(): got = lax.ppermute(last[d], ('patch', 'col'), pairs)  31.8 us
    unnamed x56, local copies, waits for them, and re-layouts  29.9 us
    ppermute x12, starting transfers between devices, line_weights(): bufs[t, d, 'o'] = lax.ppermute(got, ('groups', 'patch', 'col'), trade)  27.1 us
    ppermute x4, waiting for transfers between devices, group_moments(): lax.ppermute(summed, 'patch', [(i, i ^ step) for i in range(n_p)])  23.4 us
    ppermute x4, starting transfers between devices, group_moments(): lax.ppermute(summed, 'patch', [(i, i ^ step) for i in range(n_p)])  14.4 us
  transfers between devices with their start and end apart: 38, of which 10 were waited for; matrix products, arithmetic and copies ran while one was open for 24% of the time, Pallas kernels for 0%

commit v1 on v0

--- a/solution.py
+++ b/solution.py
@@ -148,6 +148,7 @@
     last = {1: own_half, -1: own_half}
     lines = []
     for t in range(1, n_p):
+        step_got = []
         for d in (1, -1):
             pairs = [((z - d) * n_c + cc, z * n_c + cc)
                      for z in range(n_p) for cc in range(n_c)
@@ -158,10 +159,13 @@
             last[d] = got
             bufs[(t, d)] = got
             lines.append(got)
+            step_got.append(got)
             trade = [((g * n_p + z) * n_c + cc, ((1 - g) * n_p + z) * n_c + cc)
                      for g in range(2) for z in range(n_p) for cc in range(n_c)
                      if 0 <= z - d < n_p and needs(z, cc, z - d * t)]
             bufs[(t, d, "o")] = lax.ppermute(got, ("groups", "patch", "col"), trade)
+        if step_got:
+            yield step_got
     names = sorted(bufs, key=str)
     operands = [bufs[n] for n in names]
 
@@ -183,7 +187,21 @@
 
     cases = [branch(z, cc, g) for g in range(2) for z in range(n_p) for cc in range(n_c)]
     index = (y * n_p + p) * n_c + c
-    return lax.switch(index, cases, *operands), lines
+    yield lax.switch(index, cases, *operands), lines
+
+
+def tie(steps, value):
+    got = next(steps)
+    if isinstance(got, tuple):
+        return got, value
+    _, value = lax.optimization_barrier((tuple(got), value))
+    return None, value
+
+
+def finish(steps):
+    for got in steps:
+        if isinstance(got, tuple):
+            return got
 
 
 def full_width(block):
@@ -259,8 +277,8 @@
     feat32 = features.astype(jnp.float32)
     mean_one, inv_one = group_moments(feat32, group_count, cell_total)
     if fast:
-        weight_one, lines_one = line_weights(conv1_weight)
-        weight_two, _ = line_weights(conv2_weight)
+        weight_one, lines_one = finish(line_weights(conv1_weight))
+        steps_two = line_weights(conv2_weight)
     else:
         slots_one, ids_one = fetch_weights(conv1_weight)
         slots_two, ids_two = fetch_weights(conv2_weight)
@@ -272,7 +290,12 @@
     lower_rim = rim_act[:, 1:2, :] * (where_patch < patches - 1).astype(jnp.float32)
     block_one = jnp.concatenate([upper_rim, own_act, lower_rim], axis=1).astype(jnp.bfloat16)
     if fast:
-        sum_one = reduce_cores(conv_full(full_width(block_one), weight_one))
+        _, block_one = tie(steps_two, block_one)
+        part_one = conv_full(full_width(block_one), weight_one)
+        _, part_one = tie(steps_two, part_one)
+        sum_one = reduce_cores(part_one)
+        _, sum_one = tie(steps_two, sum_one)
+        weight_two, _ = finish(steps_two)
     else:
         padded_one = extended(block_one, (("col", 2),), 1)
         sum_one = reduce_chan(conv_slots(padded_one, slots_one), ids_one)

time: 339 us -> 363 us (1.071)
  the two profiles are of different devices: /device:TPU:0 before, /device:TPU:25 now
where the time goes in v1:
time: 363 us; the launch traced here: 362 us
  starting transfers between devices  143 us (39%)
  waiting for transfers between devices  84.3 us (23%)
  local copies, waits for them, and re-layouts  55.6 us (15%)
  other arithmetic  41 us (11%)
  matrix products  35.9 us (10%)
    ppermute x2, starting transfers between devices, reduce_cores(): got_b = lax.ppermute(piece(1 - c), ('chan', 'col'), [(1, 2), (2, 1)])  65.4 us
    conv_general_dilated x2, matrix products, conv_full(): lax.conv_general_dilated(padded[None], kernel, window_strides=(1, 1), pad...  35.6 us
    ppermute x4, waiting for transfers between devices, group_moments(): lax.ppermute(summed, 'patch', [(i, i ^ step) for i in range(n_p)])  32.3 us
    ppermute x2, waiting for transfers between devices, reduce_cores(): got_b = lax.ppermute(piece(1 - c), ('chan', 'col'), [(1, 2), (2, 1)])  27.5 us
    ppermute x12, starting transfers between devices, line_weights(): got = lax.ppermute(last[d], ('patch', 'col'), pairs)  27 us
    unnamed x45, local copies, waits for them, and re-layouts  26.5 us
    ppermute x12, starting transfers between devices, line_weights(): bufs[t, d, 'o'] = lax.ppermute(got, ('groups', 'patch', 'col'), trade)  25.5 us
    concatenate x2, other arithmetic, run(): return jnp.concatenate(pieces, axis=1)  14.8 us
  transfers between devices with their start and end apart: 38, of which 9 were waited for; matrix products, arithmetic and copies ran while one was open for 22% of the time, Pallas kernels for 0%

profile of v1, /device:TPU:25, one launch (start us, length us, event | category | flops | bytes accessed | tf_op | source)
XLA Modules:
  0.0 361.5 jit_solution(14876276402992024022)
XLA Ops:
  0.0 4.4 %constant_dynamic-slice_fusion.6 = (bf16[9,160,640]{2,1,0:T(8,128)(2,1)}, bf16[9,160,640]{2,1,0:T(8,128)(2,1)}) fusion(bf16[9,320,640]{2,1,0:T(8,128)(2,1)} %bitcast.130, s32[]{:T(128)S(6)} %select_n.62, s32[]{:T(128)S(6)} %select_n.59), kind=kLoop, calls=%fused_computation.114 | loop fusion | bytes 7372808 | tf_op jit(solution)/shard_map/dynamic_slice | solution.py:144
  5.7 6.5 %collective-permute-start.10 = (bf16[9,160,640]{2,1,0:T(8,128)(2,1)}, bf16[9,160,640]{2,1,0:T(8,128)(2,1)}, u32[]{:S(2)}, u32[]{:S(2)}) collective-permute-start(bf16[9,160,640]{2,1,0:T(8,128)(2,1)} %get-tuple-element.437), channel_id=1, source_target_pairs={{4,0},{9,5},{13,9},{6,2},{11,7},{15,11},{20,16},{25,21},{29,25},{2... | collective-permute-start | bytes 5529608 | tf_op jit(solution)/shard_map/ppermute | solution.py:158
  23.3 28.0 %collective-permute-done.7 = f32[2,16]{1,0:T(2,128)S(1)} collective-permute-done((f32[2,16]{1,0:T(2,128)S(1)}, f32[2,16]{1,0:T(2,128)S(1)}, u32[]{:S(2)}, u32[]{:S(2)}) %collective-permute-start.7) | collective-permute-done | bytes 160 | tf_op jit(solution)/shard_map/ppermute | solution.py:39
  75.7 12.7 %collective-permute-done.17 = bf16[9,160,640]{2,1,0:T(8,128)(2,1)} collective-permute-done((bf16[9,160,640]{2,1,0:T(8,128)(2,1)}, bf16[9,160,640]{2,1,0:T(8,128)(2,1)}, u32[]{:S(2)}, u32[]{:S(2)}) %collective-permute-start.17) | collective-permute-done | bytes 1843232 | tf_op jit(solution)/shard_map/ppermute | solution.py:166
  99.8 3.9 %fusion.7 = bf16[640,8,1,258]{3,0,1,2:T(8,128)(2,1)} fusion(bf16[640,8,128]{2,0,1:T(8,128)(2,1)S(1)} %get-tuple-element.443, bf16[640,8,128]{2,0,1:T(8,128)(2,1)S(1)} %get-tuple-element.442), kind=kLoop, calls=%fused_computation.45 | loop fusion | flops 11888640 | bytes 5263360 | tf_op jit(solution)/shard_map/broadcast_in_dim | solution.py:218
  103.8 5.9 %copy.83 = bf16[640,8,1,258]{0,1,3,2:T(8,128)(2,1)} copy(bf16[640,8,1,258]{3,0,1,2:T(8,128)(2,1)} %fusion.7) | data formatting | bytes 5283840
  116.8 7.4 %conditional.2 = (bf16[3,3,640,640]{3,2,1,0:T(8,128)(2,1)}) conditional(s32[]{:T(128)} %clamp.4, (bf16[9,160,640]{2,1,0:T(8,128)(2,1)}, bf16[9,160,640]{2,1,0:T(8,128)(2,1)S(1)}, bf16[9,160,640]{2,1,0:T(8,128)(2,1)}, bf16[9,160,640]{2,1,0:T(8,128)(2,1)}) %tuple.208, (bf16[9,160,640]{2,1,0:T(8,128)(2,1)}, ...), branch_computations={%region_4.0_spmd, %region_5.0_spmd, %region_6.0_spmd, %region_7.0_... | conditional | flops 29491200 | bytes 14745608 | solution.py:190
  116.8 7.4 %pad_maximum_fusion.7 = bf16[9,640,640]{2,1,0:T(8,128)(2,1)} fusion(bf16[9,160,640]{2,1,0:T(8,128)(2,1)S(1)} %get-tuple-element.328, bf16[9,160,640]{2,1,0:T(8,128)(2,1)} %get-tuple-element.327, bf16[9,160,640]{2,1,0:T(8,128)(2,1)} %get-tuple-element.326, bf16[9,160,640]{2,1,0:T(8,128)(2,1)} %get-tuple-element.325), kind=kLoop, calls=%fused_computation.7 | loop fusion | flops 29491200 | bytes 14745600 | tf_op jit(solution)/shard_map/cond/branch_7_fun/concatenate | solution.py:185
  124.2 18.2 %select_convert_fusion.1 = bf16[6,8,33,640]{3,1,2,0:T(8,128)(2,1)S(1)} fusion(pred[8,33]{0,1:T(8,128)(4,1)S(1)} %copy-done.18, bf16[3,3,640,640]{3,2,1,0:T(8,128)(2,1)} %get-tuple-element.455, bf16[640,8,1,7,2]{0,3,4,1,2:T(8,128)(2,1)} %slice.38, bf16[640,8,1,8,33]{0,3,4,1,2:T(8,128)(2,1)} %copy-done.7), kind=kOutput, calls=%fused_computation.39 | convolution fusion | flops 11689144320 | bytes 12247304 | tf_op jit(solution)/shard_map/conv_general_dilated | solution.py:217
  144.3 4.1 %reshape.159 = bf16[6,1,264,640]{3,2,0,1:T(8,128)(2,1)} reshape(bf16[6,8,33,640]{3,2,1,0:T(8,128)(2,1)} %copy.71) | data formatting | bytes 4055040 | tf_op jit(solution)/shard_map/convert_element_type | solution.py:225
  151.4 4.0 %copy.78 = bf16[6,1,256,640]{2,3,0,1:T(8,128)(2,1)} copy(bf16[6,1,256,640]{3,2,0,1:T(8,128)(2,1)} %slice.39) | data formatting | bytes 3932160
  158.3 25.1 %collective-permute-start.22 = (bf16[640,6,128]{2,0,1:T(8,128)(2,1)}, bf16[640,6,128]{2,0,1:T(8,128)(2,1)}, u32[]{:S(2)}, u32[]{:S(2)}) collective-permute-start(bf16[640,6,128]{2,0,1:T(8,128)(2,1)} %get-tuple-element.447), channel_id=1, source_target_pairs={{1,2},{2,1},{5,6},{6,5},{9,10},{10,9},{13,14},{14,13},{17,18},{18,... | collective-permute-start | bytes 2949128 | tf_op jit(solution)/shard_map/ppermute | solution.py:234
  186.5 9.0 %collective-permute-done.22 = bf16[640,6,128]{2,0,1:T(8,128)(2,1)} collective-permute-done((bf16[640,6,128]{2,0,1:T(8,128)(2,1)}, bf16[640,6,128]{2,0,1:T(8,128)(2,1)}, u32[]{:S(2)}, u32[]{:S(2)}) %collective-permute-start.22) | collective-permute-done | bytes 983072 | tf_op jit(solution)/shard_map/ppermute | solution.py:234
  195.5 9.8 %collective-permute-done.23 = bf16[640,6,128]{2,0,1:T(8,128)(2,1)} collective-permute-done((bf16[640,6,128]{2,0,1:T(8,128)(2,1)}, bf16[640,6,128]{2,0,1:T(8,128)(2,1)}, u32[]{:S(2)}, u32[]{:S(2)}) %collective-permute-start.23) | collective-permute-done | bytes 983072 | tf_op jit(solution)/shard_map/ppermute | solution.py:233
  218.2 6.1 %collective-permute-start.26 = (f32[2,16]{1,0:T(2,128)S(1)}, f32[2,16]{1,0:T(2,128)S(1)}, u32[]{:S(2)}, u32[]{:S(2)}) collective-permute-start(f32[2,16]{1,0:T(2,128)S(1)} %fusion.70), channel_id=1, source_target_pairs={{0,8},{4,12},{8,0},{12,4},{1,9},{5,13},{9,1},{13,5},{2,10},{6,14},... | collective-permute-start | bytes 392 | tf_op jit(solution)/shard_map/ppermute | solution.py:39
  229.0 4.0 %collective-permute-start.28 = (bf16[640,1,128]{2,0,1:T(8,128)(2,1)S(1)}, bf16[640,1,128]{2,0,1:T(8,128)(2,1)S(1)}, u32[]{:S(2)}, u32[]{:S(2)}) collective-permute-start(bf16[640,1,128]{2,0,1:T(8,128)(2,1)S(1)} %get-tuple-element.450), channel_id=1, source_target_pairs={{4,0},{8,4},{12,8},{5,1},{9,5},{13,9},{6,2},{10,6},{14,10},{7,3},{... | collective-permute-start | bytes 491528 | tf_op jit(solution)/shard_map/ppermute | solution.py:22
  242.0 5.6 %collective-permute-start.29 = (bf16[640,8,128]{2,0,1:T(8,128)(2,1)}, bf16[640,8,128]{2,0,1:T(8,128)(2,1)}, u32[]{:S(2)}, u32[]{:S(2)}) collective-permute-start(bf16[640,8,128]{2,0,1:T(8,128)(2,1)} %pad_maximum_fusion.33), channel_id=1, source_target_pairs={{0,1},{1,0},{2,3},{3,2},{4,5},{5,4},{6,7},{7,6},{8,9},{9,8},{10,11... | collective-permute-start | bytes 3932168 | tf_op jit(solution)/shard_map/ppermute | solution.py:62
  247.6 7.5 %conditional.3 = (bf16[3,3,640,640]{3,2,1,0:T(8,128)(2,1)}) conditional(s32[]{:T(128)} %clamp.4, (bf16[9,160,640]{2,1,0:T(8,128)(2,1)}, bf16[9,160,640]{2,1,0:T(8,128)(2,1)S(1)}, bf16[9,160,640]{2,1,0:T(8,128)(2,1)}, bf16[9,160,640]{2,1,0:T(8,128)(2,1)}) %tuple.151, (bf16[9,160,640]{2,1,0:T(8,128)(2,1)}, ...), branch_computations={%region_24.25_spmd, %region_25.26_spmd, %region_26.27_spmd, %regio... | conditional | flops 29491200 | bytes 14745608 | solution.py:190
  247.7 7.5 %pad_maximum_fusion.23 = bf16[9,640,640]{2,1,0:T(8,128)(2,1)} fusion(bf16[9,160,640]{2,1,0:T(8,128)(2,1)S(1)} %get-tuple-element.392, bf16[9,160,640]{2,1,0:T(8,128)(2,1)} %get-tuple-element.391, bf16[9,160,640]{2,1,0:T(8,128)(2,1)} %get-tuple-element.390, bf16[9,160,640]{2,1,0:T(8,128)(2,1)} %get-tuple-element.389), kind=kLoop, calls=%fused_computation.23 | loop fusion | flops 29491200 | bytes 14745600 | tf_op jit(solution)/shard_map/cond/branch_7_fun/concatenate | solution.py:185
  256.8 3.9 %fusion.3 = bf16[640,8,1,258]{3,0,1,2:T(8,128)(2,1)} fusion(bf16[640,8,128]{2,0,1:T(8,128)(2,1)S(1)} %get-tuple-element.441, bf16[640,8,128]{2,0,1:T(8,128)(2,1)S(1)} %get-tuple-element.440), kind=kLoop, calls=%fused_computation.41 | loop fusion | flops 11888640 | bytes 5263360 | tf_op jit(solution)/shard_map/broadcast_in_dim | solution.py:218
  260.7 6.0 %copy.84 = bf16[640,8,1,258]{0,1,3,2:T(8,128)(2,1)} copy(bf16[640,8,1,258]{3,0,1,2:T(8,128)(2,1)} %fusion.3) | data formatting | bytes 5283840
  269.1 17.4 %select_convert_fusion = bf16[6,8,33,640]{3,1,2,0:T(8,128)(2,1)S(1)} fusion(pred[8,33]{0,1:T(8,128)(4,1)S(1)} %copy-done.18, bf16[3,3,640,640]{3,2,1,0:T(8,128)(2,1)} %get-tuple-element.456, bf16[640,8,1,7,2]{0,3,4,1,2:T(8,128)(2,1)S(1)} %slice.42, bf16[640,8,1,8,33]{0,3,4,1,2:T(8,128)(2,1)S(1)} %copy.75), kind=kOutput, calls=%fused_computation.38 | convolution fusion | flops 11689144320 | bytes 12247304 | tf_op jit(solution)/shard_map/conv_general_dilated | solution.py:217
  297.2 40.3 %collective-permute-start.36 = (bf16[640,6,128]{2,0,1:T(8,128)(2,1)}, bf16[640,6,128]{2,0,1:T(8,128)(2,1)}, u32[]{:S(2)}, u32[]{:S(2)}) collective-permute-start(bf16[640,6,128]{2,0,1:T(8,128)(2,1)} %bitcast.132), channel_id=1, source_target_pairs={{1,2},{2,1},{5,6},{6,5},{9,10},{10,9},{13,14},{14,13},{17,18},{18,... | collective-permute-start | bytes 2949128 | tf_op jit(solution)/shard_map/ppermute | solution.py:234
  339.7 18.4 %collective-permute-done.36 = bf16[640,6,128]{2,0,1:T(8,128)(2,1)} collective-permute-done((bf16[640,6,128]{2,0,1:T(8,128)(2,1)}, bf16[640,6,128]{2,0,1:T(8,128)(2,1)}, u32[]{:S(2)}, u32[]{:S(2)}) %collective-permute-start.36) | collective-permute-done | bytes 983072 | tf_op jit(solution)/shard_map/ppermute | solution.py:234
  (165 shorter events, 112.0 us)
Async XLA Ops:
  4.4 52.1 %collective-permute-start.16 = (bf16[9,160,640]{2,1,0:T(8,128)(2,1)}, bf16[9,160,640]{2,1,0:T(8,128)(2,1)}, u32[]{:S(2)}, u32[]{:S(2)}) collective-permute-start(bf16[9,160,640]{2,1,0:T(8,128)(2,1)} %get-tuple-element.437), channel_id=1, source_target_pairs={{0,4},{4,8},{9,13},{2,6},{6,10},{11,15},{16,20},{20,24},{25,29},{1... | collective-permute-start | bytes 5529608 | tf_op jit(solution)/shard_map/ppermute | solution.py:158
  5.7 52.8 %collective-permute-start.10 = (bf16[9,160,640]{2,1,0:T(8,128)(2,1)}, bf16[9,160,640]{2,1,0:T(8,128)(2,1)}, u32[]{:S(2)}, u32[]{:S(2)}) collective-permute-start(bf16[9,160,640]{2,1,0:T(8,128)(2,1)} %get-tuple-element.437), channel_id=1, source_target_pairs={{4,0},{9,5},{13,9},{6,2},{11,7},{15,11},{20,16},{25,21},{29,25},{2... | collective-permute-start | bytes 5529608 | tf_op jit(solution)/shard_map/ppermute | solution.py:158
  14.0 48.7 %collective-permute-start.3 = (bf16[9,160,640]{2,1,0:T(8,128)(2,1)}, bf16[9,160,640]{2,1,0:T(8,128)(2,1)}, u32[]{:S(2)}, u32[]{:S(2)}) collective-permute-start(bf16[9,160,640]{2,1,0:T(8,128)(2,1)} %get-tuple-element.439), channel_id=1, source_target_pairs={{4,0},{9,5},{13,9},{6,2},{11,7},{15,11},{20,16},{25,21},{29,25},{2... | collective-permute-start | bytes 5529608 | tf_op jit(solution)/shard_map/ppermute | solution.py:158
  16.5 46.1 %collective-permute-start = (bf16[9,160,640]{2,1,0:T(8,128)(2,1)}, bf16[9,160,640]{2,1,0:T(8,128)(2,1)}, u32[]{:S(2)}, u32[]{:S(2)}) collective-permute-start(bf16[9,160,640]{2,1,0:T(8,128)(2,1)} %get-tuple-element.439), channel_id=1, source_target_pairs={{0,4},{4,8},{9,13},{2,6},{6,10},{11,15},{16,20},{20,24},{25,29},{1... | collective-permute-start | bytes 5529608 | tf_op jit(solution)/shard_map/ppermute | solution.py:158
  19.8 31.4 %collective-permute-start.7 = (f32[2,16]{1,0:T(2,128)S(1)}, f32[2,16]{1,0:T(2,128)S(1)}, u32[]{:S(2)}, u32[]{:S(2)}) collective-permute-start(f32[2,16]{1,0:T(2,128)S(1)} %fusion.64), channel_id=1, source_target_pairs={{0,4},{4,0},{8,12},{12,8},{1,5},{5,1},{9,13},{13,9},{2,6},{6,2},{1... | collective-permute-start | bytes 392 | tf_op jit(solution)/shard_map/ppermute | solution.py:39
  58.5 15.3 %collective-permute-start.12 = (bf16[9,160,640]{2,1,0:T(8,128)(2,1)}, bf16[9,160,640]{2,1,0:T(8,128)(2,1)}, u32[]{:S(2)}, u32[]{:S(2)}) collective-permute-start(bf16[9,160,640]{2,1,0:T(8,128)(2,1)} %collective-permute-done.10), channel_id=1, source_target_pairs={{5,1},{9,5},{7,3},{11,7},{21,17},{25,21},{23,19},{27,23}} | collective-permute-start | bytes 5529608 | tf_op jit(solution)/shard_map/ppermute | solution.py:158
  63.7 24.7 %collective-permute-start.17 = (bf16[9,160,640]{2,1,0:T(8,128)(2,1)}, bf16[9,160,640]{2,1,0:T(8,128)(2,1)}, u32[]{:S(2)}, u32[]{:S(2)}) collective-permute-start(bf16[9,160,640]{2,1,0:T(8,128)(2,1)} %collective-permute-done.16), channel_id=1, source_target_pairs={{4,20},{8,24},{13,29},{20,4},{24,8},{29,13},{6,22},{10,26},{15,31}... | collective-permute-start | bytes 5529608 | tf_op jit(solution)/shard_map/ppermute | solution.py:166
  66.9 23.5 %collective-permute-start.11 = (bf16[9,160,640]{2,1,0:T(8,128)(2,1)}, bf16[9,160,640]{2,1,0:T(8,128)(2,1)}, u32[]{:S(2)}, u32[]{:S(2)}) collective-permute-start(bf16[9,160,640]{2,1,0:T(8,128)(2,1)} %collective-permute-done.10), channel_id=1, source_target_pairs={{0,16},{5,21},{9,25},{16,0},{21,5},{25,9},{2,18},{7,23},{11,27},{1... | collective-permute-start | bytes 5529608 | tf_op jit(solution)/shard_map/ppermute | solution.py:166
  69.9 22.3 %collective-permute-start.4 = (bf16[9,160,640]{2,1,0:T(8,128)(2,1)}, bf16[9,160,640]{2,1,0:T(8,128)(2,1)}, u32[]{:S(2)}, u32[]{:S(2)}) collective-permute-start(bf16[9,160,640]{2,1,0:T(8,128)(2,1)} %collective-permute-done.3), channel_id=1, source_target_pairs={{5,1},{9,5},{7,3},{11,7},{21,17},{25,21},{23,19},{27,23}} | collective-permute-start | bytes 5529608 | tf_op jit(solution)/shard_map/ppermute | solution.py:158
  71.8 22.3 %collective-permute-start.20 = (bf16[9,160,640]{2,1,0:T(8,128)(2,1)}, bf16[9,160,640]{2,1,0:T(8,128)(2,1)}, u32[]{:S(2)}, u32[]{:S(2)}) collective-permute-start(bf16[9,160,640]{2,1,0:T(8,128)(2,1)} %collective-permute-done.18), channel_id=1, source_target_pairs={{8,12},{10,14},{24,28},{26,30}} | collective-permute-start | bytes 5529608 | tf_op jit(solution)/shard_map/ppermute | solution.py:158
  73.8 22.3 %collective-permute-start.14 = (bf16[9,160,640]{2,1,0:T(8,128)(2,1)}, bf16[9,160,640]{2,1,0:T(8,128)(2,1)}, u32[]{:S(2)}, u32[]{:S(2)}) collective-permute-start(bf16[9,160,640]{2,1,0:T(8,128)(2,1)} %collective-permute-done.12), channel_id=1, source_target_pairs={{5,1},{7,3},{21,17},{23,19}} | collective-permute-start | bytes 5529608 | tf_op jit(solution)/shard_map/ppermute | solution.py:158
  88.4 24.5 %collective-permute-start.1 = (bf16[9,160,640]{2,1,0:T(8,128)(2,1)}, bf16[9,160,640]{2,1,0:T(8,128)(2,1)}, u32[]{:S(2)}, u32[]{:S(2)}) collective-permute-start(bf16[9,160,640]{2,1,0:T(8,128)(2,1)} %collective-permute-done), channel_id=1, source_target_pairs={{4,8},{8,12},{6,10},{10,14},{20,24},{24,28},{22,26},{26,30}} | collective-permute-start | bytes 5529608 | tf_op jit(solution)/shard_map/ppermute | solution.py:158
  90.3 24.5 %collective-permute-start.19 = (bf16[9,160,640]{2,1,0:T(8,128)(2,1)}, bf16[9,160,640]{2,1,0:T(8,128)(2,1)}, u32[]{:S(2)}, u32[]{:S(2)}) collective-permute-start(bf16[9,160,640]{2,1,0:T(8,128)(2,1)} %collective-permute-done.18), channel_id=1, source_target_pairs={{8,24},{12,28},{24,8},{28,12},{10,26},{14,30},{26,10},{30,14}} | collective-permute-start | bytes 5529608 | tf_op jit(solution)/shard_map/ppermute | solution.py:166
  92.2 24.5 %collective-permute-start.13 = (bf16[9,160,640]{2,1,0:T(8,128)(2,1)}, bf16[9,160,640]{2,1,0:T(8,128)(2,1)}, u32[]{:S(2)}, u32[]{:S(2)}) collective-permute-start(bf16[9,160,640]{2,1,0:T(8,128)(2,1)} %collective-permute-done.12), channel_id=1, source_target_pairs={{1,17},{5,21},{17,1},{21,5},{3,19},{7,23},{19,3},{23,7}} | collective-permute-start | bytes 5529608 | tf_op jit(solution)/shard_map/ppermute | solution.py:166
  94.1 22.6 %collective-permute-start.21 = (bf16[9,160,640]{2,1,0:T(8,128)(2,1)}, bf16[9,160,640]{2,1,0:T(8,128)(2,1)}, u32[]{:S(2)}, u32[]{:S(2)}) collective-permute-start(bf16[9,160,640]{2,1,0:T(8,128)(2,1)} %collective-permute-done.20), channel_id=1, source_target_pairs={{12,28},{28,12},{14,30},{30,14}} | collective-permute-start | bytes 5529608 | tf_op jit(solution)/shard_map/ppermute | solution.py:166
  96.0 20.7 %collective-permute-start.15 = (bf16[9,160,640]{2,1,0:T(8,128)(2,1)}, bf16[9,160,640]{2,1,0:T(8,128)(2,1)}, u32[]{:S(2)}, u32[]{:S(2)}) collective-permute-start(bf16[9,160,640]{2,1,0:T(8,128)(2,1)} %collective-permute-done.14), channel_id=1, source_target_pairs={{1,17},{17,1},{3,19},{19,3}} | collective-permute-start | bytes 5529608 | tf_op jit(solution)/shard_map/ppermute | solution.py:166
  112.9 94.5 %collective-permute-start.5 = (bf16[9,160,640]{2,1,0:T(8,128)(2,1)}, bf16[9,160,640]{2,1,0:T(8,128)(2,1)}, u32[]{:S(2)}, u32[]{:S(2)}) collective-permute-start(bf16[9,160,640]{2,1,0:T(8,128)(2,1)} %collective-permute-done.4), channel_id=1, source_target_pairs={{5,1},{7,3},{21,17},{23,19}} | collective-permute-start | bytes 5529608 | tf_op jit(solution)/shard_map/ppermute | solution.py:158
  114.8 92.6 %collective-permute-start.2 = (bf16[9,160,640]{2,1,0:T(8,128)(2,1)}, bf16[9,160,640]{2,1,0:T(8,128)(2,1)}, u32[]{:S(2)}, u32[]{:S(2)}) collective-permute-start(bf16[9,160,640]{2,1,0:T(8,128)(2,1)} %collective-permute-done.1), channel_id=1, source_target_pairs={{8,12},{10,14},{24,28},{26,30}} | collective-permute-start | bytes 5529608 | tf_op jit(solution)/shard_map/ppermute | solution.py:158
  158.3 37.2 %collective-permute-start.22 = (bf16[640,6,128]{2,0,1:T(8,128)(2,1)}, bf16[640,6,128]{2,0,1:T(8,128)(2,1)}, u32[]{:S(2)}, u32[]{:S(2)}) collective-permute-start(bf16[640,6,128]{2,0,1:T(8,128)(2,1)} %get-tuple-element.447), channel_id=1, source_target_pairs={{1,2},{2,1},{5,6},{6,5},{9,10},{10,9},{13,14},{14,13},{17,18},{18,... | collective-permute-start | bytes 2949128 | tf_op jit(solution)/shard_map/ppermute | solution.py:234
  183.4 21.9 %collective-permute-start.23 = (bf16[640,6,128]{2,0,1:T(8,128)(2,1)}, bf16[640,6,128]{2,0,1:T(8,128)(2,1)}, u32[]{:S(2)}, u32[]{:S(2)}) collective-permute-start(bf16[640,6,128]{2,0,1:T(8,128)(2,1)} %get-tuple-element.448), channel_id=1, source_target_pairs={{0,1},{3,2},{1,3},{2,0},{4,5},{7,6},{5,7},{6,4},{8,9},{11,10},{9,1... | collective-permute-start | bytes 2949128 | tf_op jit(solution)/shard_map/ppermute | solution.py:233
  184.5 50.4 %collective-permute-start.30 = (bf16[9,160,640]{2,1,0:T(8,128)(2,1)}, bf16[9,160,640]{2,1,0:T(8,128)(2,1)}, u32[]{:S(2)}, u32[]{:S(2)}) collective-permute-start(bf16[9,160,640]{2,1,0:T(8,128)(2,1)} %collective-permute-done.3), channel_id=1, source_target_pairs={{0,16},{5,21},{9,25},{16,0},{21,5},{25,9},{2,18},{7,23},{11,27},{1... | collective-permute-start | bytes 5529608 | tf_op jit(solution)/shard_map/ppermute | solution.py:166
  215.0 27.0 %collective-permute-start.33 = (bf16[9,160,640]{2,1,0:T(8,128)(2,1)}, bf16[9,160,640]{2,1,0:T(8,128)(2,1)}, u32[]{:S(2)}, u32[]{:S(2)}) collective-permute-start(bf16[9,160,640]{2,1,0:T(8,128)(2,1)} %collective-permute-done), channel_id=1, source_target_pairs={{4,20},{8,24},{13,29},{20,4},{24,8},{29,13},{6,22},{10,26},{15,31}... | collective-permute-start | bytes 5529608 | tf_op jit(solution)/shard_map/ppermute | solution.py:166
  297.2 42.6 %collective-permute-start.37 = (bf16[640,6,128]{2,0,1:T(8,128)(2,1)}, bf16[640,6,128]{2,0,1:T(8,128)(2,1)}, u32[]{:S(2)}, u32[]{:S(2)}) collective-permute-start(bf16[640,6,128]{2,0,1:T(8,128)(2,1)} %bitcast.133), channel_id=1, source_target_pairs={{0,1},{3,2},{1,3},{2,0},{4,5},{7,6},{5,7},{6,4},{8,9},{11,10},{9,1... | collective-permute-start | bytes 2949128 | tf_op jit(solution)/shard_map/ppermute | solution.py:233
  297.2 61.0 %collective-permute-start.36 = (bf16[640,6,128]{2,0,1:T(8,128)(2,1)}, bf16[640,6,128]{2,0,1:T(8,128)(2,1)}, u32[]{:S(2)}, u32[]{:S(2)}) collective-permute-start(bf16[640,6,128]{2,0,1:T(8,128)(2,1)} %bitcast.132), channel_id=1, source_target_pairs={{1,2},{2,1},{5,6},{6,5},{9,10},{10,9},{13,14},{14,13},{17,18},{18,... | collective-permute-start | bytes 2949128 | tf_op jit(solution)/shard_map/ppermute | solution.py:234
  (33 other events, 947.0 us)

commit v2 on v0

--- a/solution.py
+++ b/solution.py
@@ -260,7 +260,7 @@
     mean_one, inv_one = group_moments(feat32, group_count, cell_total)
     if fast:
         weight_one, lines_one = line_weights(conv1_weight)
-        weight_two, _ = line_weights(conv2_weight)
+        weight_two, _ = line_weights(conv2_weight, after=lines_one[:2])
     else:
         slots_one, ids_one = fetch_weights(conv1_weight)
         slots_two, ids_two = fetch_weights(conv2_weight)

time: 339 us -> 339 us (level)
    ppermute x2, starting transfers between devices: 44.2 us -> 50 us  [reduce_cores(): lax.ppermute(send_a, ('chan', 'col'), [(0, 1), (3, 2), (1, 3), (2, 0)])]
    ppermute x12, waiting for transfers between devices: 12.3 us -> 6.69 us  [line_weights(): bufs[t, d, 'o'] = lax.ppermute(got, ('groups', 'patch', 'col'), trade)]
  transfers between devices with their start and end apart: 38 -> 38, of which waited for: 10 -> 11; matrix products, arithmetic and copies ran while one was open for 24% -> 24% of each run, Pallas kernels for 0% -> 0%
where the time goes in v2:
time: 339 us; the launch traced here: 338 us
  starting transfers between devices  129 us (38%)
  waiting for transfers between devices  78.9 us (23%)
  local copies, waits for them, and re-layouts  53.5 us (16%)
  other arithmetic  39.2 us (12%)
  matrix products  35.9 us (11%)
    ppermute x2, starting transfers between devices, reduce_cores(): lax.ppermute(send_a, ('chan', 'col'), [(0, 1), (3, 2), (1, 3), (2, 0)])  50 us
    conv_general_dilated x2, matrix products, conv_full(): lax.conv_general_dilated(padded[None], kernel, window_strides=(1, 1), pad...  35.6 us
    ppermute x2, waiting for transfers between devices, reduce_cores(): lax.ppermute(send_a, ('chan', 'col'), [(0, 1), (3, 2), (1, 3), (2, 0)])  33.8 us
    ppermute x12, starting transfers between devices, line_weights(): got = lax.ppermute(last[d], ('patch', 'col'), pairs)  31.7 us
    unnamed x56, local copies, waits for them, and re-layouts  29.2 us
    ppermute x12, starting transfers between devices, line_weights(): bufs[t, d, 'o'] = lax.ppermute(got, ('groups', 'patch', 'col'), trade)  27.2 us
    ppermute x4, waiting for transfers between devices, group_moments(): lax.ppermute(summed, 'patch', [(i, i ^ step) for i in range(n_p)])  23.4 us
    concatenate x2, other arithmetic, run(): return jnp.concatenate(pieces, axis=1)  13.9 us
  transfers between devices with their start and end apart: 38, of which 11 were waited for; matrix products, arithmetic and copies ran while one was open for 24% of the time, Pallas kernels for 0%

profile of v2, /device:TPU:0, one launch (start us, length us, event | category | flops | bytes accessed | tf_op | source)
XLA Modules:
  0.0 337.6 jit_solution(1988542010415991231)
XLA Ops:
  5.1 7.5 %collective-permute-start.10 = (bf16[9,160,640]{2,1,0:T(8,128)(2,1)S(1)}, bf16[9,160,640]{2,1,0:T(8,128)(2,1)}, u32[]{:S(2)}, u32[]{:S(2)}) collective-permute-start(bf16[9,160,640]{2,1,0:T(8,128)(2,1)S(1)} %get-tuple-element.433), channel_id=1, source_target_pairs={{0,4},{4,8},{9,13},{2,6},{6,10},{11,15},{16,20},{20,24},{25,29},{1... | collective-permute-start | bytes 5529608 | tf_op jit(solution)/shard_map/ppermute | solution.py:157
  14.7 17.4 %collective-permute-done.1 = f32[2,16]{1,0:T(2,128)S(1)} collective-permute-done((f32[2,16]{1,0:T(2,128)S(1)}, f32[2,16]{1,0:T(2,128)S(1)}, u32[]{:S(2)}, u32[]{:S(2)}) %collective-permute-start.1) | collective-permute-done | bytes 160 | tf_op jit(solution)/shard_map/ppermute | solution.py:39
  32.2 4.5 %collective-permute-done.2 = f32[2,16]{1,0:T(2,128)S(1)} collective-permute-done((f32[2,16]{1,0:T(2,128)S(1)}, f32[2,16]{1,0:T(2,128)S(1)}, u32[]{:S(2)}, u32[]{:S(2)}) %collective-permute-start.2) | collective-permute-done | bytes 160 | tf_op jit(solution)/shard_map/ppermute | solution.py:39
  44.8 4.5 %collective-permute-start.5 = (bf16[9,160,640]{2,1,0:T(8,128)(2,1)}, bf16[9,160,640]{2,1,0:T(8,128)(2,1)}, u32[]{:S(2)}, u32[]{:S(2)}) collective-permute-start(bf16[9,160,640]{2,1,0:T(8,128)(2,1)} %collective-permute-done.4), channel_id=1, source_target_pairs={{0,16},{5,21},{9,25},{16,0},{21,5},{25,9},{2,18},{7,23},{11,27},{1... | collective-permute-start | bytes 5529608 | tf_op jit(solution)/shard_map/ppermute | solution.py:164
  54.2 6.3 %collective-permute-start.30 = (bf16[9,160,640]{2,1,0:T(8,128)(2,1)}, bf16[9,160,640]{2,1,0:T(8,128)(2,1)}, u32[]{:S(2)}, u32[]{:S(2)}) collective-permute-start(bf16[9,160,640]{2,1,0:T(8,128)(2,1)} %get-tuple-element.435), channel_id=1, source_target_pairs={{0,4},{4,8},{9,13},{2,6},{6,10},{11,15},{16,20},{20,24},{25,29},{1... | collective-permute-start | bytes 5529608 | tf_op jit(solution)/shard_map/ppermute | solution.py:157
  64.3 6.7 %collective-permute-done.5 = bf16[9,160,640]{2,1,0:T(8,128)(2,1)} collective-permute-done((bf16[9,160,640]{2,1,0:T(8,128)(2,1)}, bf16[9,160,640]{2,1,0:T(8,128)(2,1)}, u32[]{:S(2)}, u32[]{:S(2)}) %collective-permute-start.5) | collective-permute-done | bytes 1843232 | tf_op jit(solution)/shard_map/ppermute | solution.py:164
  74.2 6.1 %collective-permute-done.30 = bf16[9,160,640]{2,1,0:T(8,128)(2,1)} collective-permute-done((bf16[9,160,640]{2,1,0:T(8,128)(2,1)}, bf16[9,160,640]{2,1,0:T(8,128)(2,1)}, u32[]{:S(2)}, u32[]{:S(2)}) %collective-permute-start.30) | collective-permute-done | bytes 1843232 | tf_op jit(solution)/shard_map/ppermute | solution.py:157
  91.9 5.9 %copy.86 = bf16[640,8,1,258]{0,1,3,2:T(8,128)(2,1)} copy(bf16[640,8,1,258]{3,0,1,2:T(8,128)(2,1)} %fusion.7) | data formatting | bytes 5283840
  101.1 5.7 %collective-permute-done.24 = bf16[9,160,640]{2,1,0:T(8,128)(2,1)} collective-permute-done((bf16[9,160,640]{2,1,0:T(8,128)(2,1)}, bf16[9,160,640]{2,1,0:T(8,128)(2,1)}, u32[]{:S(2)}, u32[]{:S(2)}) %collective-permute-start.24) | collective-permute-done | bytes 1843232 | tf_op jit(solution)/shard_map/ppermute | solution.py:157
  110.7 6.5 %conditional.2 = (bf16[3,3,640,640]{3,2,1,0:T(8,128)(2,1)}) conditional(s32[]{:T(128)} %clamp.4, (bf16[9,160,640]{2,1,0:T(8,128)(2,1)S(1)}, bf16[9,160,640]{2,1,0:T(8,128)(2,1)S(1)}, bf16[9,160,640]{2,1,0:T(8,128)(2,1)}, bf16[9,160,640]{2,1,0:T(8,128)(2,1)}) %tuple.213, (bf16[9,160,640]{2,1,0:T(8,128)(2,1)}, ...), branch_computations={%region_4.0_spmd, %region_5.0_spmd, %region_6.0_spmd, %region_7.0_... | conditional | flops 29491200 | bytes 14745608 | solution.py:186
  110.7 6.5 %pad_maximum_fusion = bf16[9,640,640]{2,1,0:T(8,128)(2,1)} fusion(bf16[9,160,640]{2,1,0:T(8,128)(2,1)} %get-tuple-element.273, bf16[9,160,640]{2,1,0:T(8,128)(2,1)} %get-tuple-element.272, bf16[9,160,640]{2,1,0:T(8,128)(2,1)S(1)} %get-tuple-element.271, bf16[9,160,640]{2,1,0:T(8,128)(2,1)S(1)} %get-tuple-element.270), kind=kLoop, calls=%fused_computation | loop fusion | flops 29491200 | bytes 14745600 | tf_op jit(solution)/shard_map/cond/branch_0_fun/concatenate | solution.py:181
  117.2 18.2 %select_convert_fusion.1 = bf16[6,8,33,640]{3,1,2,0:T(8,128)(2,1)S(1)} fusion(pred[8,33]{0,1:T(8,128)(4,1)S(1)} %copy-done.22, bf16[3,3,640,640]{3,2,1,0:T(8,128)(2,1)} %get-tuple-element.452, bf16[640,8,1,7,2]{0,3,4,1,2:T(8,128)(2,1)} %slice.38, bf16[640,8,1,8,33]{0,3,4,1,2:T(8,128)(2,1)} %copy-done.9), kind=kOutput, calls=%fused_computation.39 | convolution fusion | flops 11689144320 | bytes 12247304 | tf_op jit(solution)/shard_map/conv_general_dilated | solution.py:199
  137.3 4.1 %reshape.162 = bf16[6,1,264,640]{3,2,0,1:T(8,128)(2,1)} reshape(bf16[6,8,33,640]{3,2,1,0:T(8,128)(2,1)} %copy.71) | data formatting | bytes 4055040 | tf_op jit(solution)/shard_map/convert_element_type | solution.py:207
  151.0 12.9 %collective-permute-start.17 = (bf16[640,6,128]{2,0,1:T(8,128)(2,1)}, bf16[640,6,128]{2,0,1:T(8,128)(2,1)}, u32[]{:S(2)}, u32[]{:S(2)}) collective-permute-start(bf16[640,6,128]{2,0,1:T(8,128)(2,1)} %bitcast.141), channel_id=1, source_target_pairs={{0,1},{3,2},{1,3},{2,0},{4,5},{7,6},{5,7},{6,4},{8,9},{11,10},{9,1... | collective-permute-start | bytes 2949128 | tf_op jit(solution)/shard_map/ppermute | solution.py:215
  172.4 13.7 %collective-permute-done.17 = bf16[640,6,128]{2,0,1:T(8,128)(2,1)} collective-permute-done((bf16[640,6,128]{2,0,1:T(8,128)(2,1)}, bf16[640,6,128]{2,0,1:T(8,128)(2,1)}, u32[]{:S(2)}, u32[]{:S(2)}) %collective-permute-start.17) | collective-permute-done | bytes 983072 | tf_op jit(solution)/shard_map/ppermute | solution.py:215
  190.6 5.0 %collective-permute-start.19 = (f32[2,16]{1,0:T(2,128)S(1)}, f32[2,16]{1,0:T(2,128)S(1)}, u32[]{:S(2)}, u32[]{:S(2)}) collective-permute-start(f32[2,16]{1,0:T(2,128)S(1)} %fusion.63), channel_id=1, source_target_pairs={{0,4},{4,0},{8,12},{12,8},{1,5},{5,1},{9,13},{13,9},{2,6},{6,2},{1... | collective-permute-start | bytes 392 | tf_op jit(solution)/shard_map/ppermute | solution.py:39
  199.0 6.5 %collective-permute-start.20 = (f32[2,16]{1,0:T(2,128)S(1)}, f32[2,16]{1,0:T(2,128)S(1)}, u32[]{:S(2)}, u32[]{:S(2)}) collective-permute-start(f32[2,16]{1,0:T(2,128)S(1)} %fusion.70), channel_id=1, source_target_pairs={{0,8},{4,12},{8,0},{12,4},{1,9},{5,13},{9,1},{13,5},{2,10},{6,14},... | collective-permute-start | bytes 392 | tf_op jit(solution)/shard_map/ppermute | solution.py:39
  224.2 7.4 %conditional.3 = (bf16[3,3,640,640]{3,2,1,0:T(8,128)(2,1)}) conditional(s32[]{:T(128)} %clamp.4, (bf16[9,160,640]{2,1,0:T(8,128)(2,1)}, bf16[9,160,640]{2,1,0:T(8,128)(2,1)S(1)}, bf16[9,160,640]{2,1,0:T(8,128)(2,1)}, bf16[9,160,640]{2,1,0:T(8,128)(2,1)}) %tuple.147, (bf16[9,160,640]{2,1,0:T(8,128)(2,1)}, ...), branch_computations={%region_24.0_spmd, %region_25.0_spmd, %region_26.0_spmd, %region_2... | conditional | flops 29491200 | bytes 14745608 | solution.py:186
  224.2 7.4 %pad_maximum_fusion.16 = bf16[9,640,640]{2,1,0:T(8,128)(2,1)} fusion(bf16[9,160,640]{2,1,0:T(8,128)(2,1)} %get-tuple-element.364, bf16[9,160,640]{2,1,0:T(8,128)(2,1)} %get-tuple-element.363, bf16[9,160,640]{2,1,0:T(8,128)(2,1)S(1)} %get-tuple-element.362, bf16[9,160,640]{2,1,0:T(8,128)(2,1)} %get-tuple-element.361), kind=kLoop, calls=%fused_computation.16 | loop fusion | flops 29491200 | bytes 14745600 | tf_op jit(solution)/shard_map/cond/branch_0_fun/concatenate | solution.py:181
  233.2 4.0 %fusion.3 = bf16[640,8,1,258]{3,0,1,2:T(8,128)(2,1)} fusion(bf16[640,8,128]{2,0,1:T(8,128)(2,1)S(1)} %get-tuple-element.437, bf16[640,8,128]{2,0,1:T(8,128)(2,1)S(1)} %get-tuple-element.436), kind=kLoop, calls=%fused_computation.41 | loop fusion | flops 11888640 | bytes 5263360 | tf_op jit(solution)/shard_map/broadcast_in_dim | solution.py:200
  237.2 5.9 %copy.87 = bf16[640,8,1,258]{0,1,3,2:T(8,128)(2,1)} copy(bf16[640,8,1,258]{3,0,1,2:T(8,128)(2,1)} %fusion.3) | data formatting | bytes 5283840
  245.5 17.4 %select_convert_fusion = bf16[6,8,33,640]{3,1,2,0:T(8,128)(2,1)S(1)} fusion(pred[8,33]{0,1:T(8,128)(4,1)S(1)} %copy-done.22, bf16[3,3,640,640]{3,2,1,0:T(8,128)(2,1)} %get-tuple-element.453, bf16[640,8,1,7,2]{0,3,4,1,2:T(8,128)(2,1)S(1)} %slice.42, bf16[640,8,1,8,33]{0,3,4,1,2:T(8,128)(2,1)S(1)} %copy.75), kind=kOutput, calls=%fused_computation.38 | convolution fusion | flops 11689144320 | bytes 12247304 | tf_op jit(solution)/shard_map/conv_general_dilated | solution.py:199
  275.2 37.1 %collective-permute-start.37 = (bf16[640,6,128]{2,0,1:T(8,128)(2,1)}, bf16[640,6,128]{2,0,1:T(8,128)(2,1)}, u32[]{:S(2)}, u32[]{:S(2)}) collective-permute-start(bf16[640,6,128]{2,0,1:T(8,128)(2,1)} %bitcast.143), channel_id=1, source_target_pairs={{0,1},{3,2},{1,3},{2,0},{4,5},{7,6},{5,7},{6,4},{8,9},{11,10},{9,1... | collective-permute-start | bytes 2949128 | tf_op jit(solution)/shard_map/ppermute | solution.py:215
  314.5 20.0 %collective-permute-done.37 = bf16[640,6,128]{2,0,1:T(8,128)(2,1)} collective-permute-done((bf16[640,6,128]{2,0,1:T(8,128)(2,1)}, bf16[640,6,128]{2,0,1:T(8,128)(2,1)}, u32[]{:S(2)}, u32[]{:S(2)}) %collective-permute-start.37) | collective-permute-done | bytes 983072 | tf_op jit(solution)/shard_map/ppermute | solution.py:215
  (174 shorter events, 113.0 us)
Async XLA Ops:
  3.8 34.9 %collective-permute-start.4 = (bf16[9,160,640]{2,1,0:T(8,128)(2,1)S(1)}, bf16[9,160,640]{2,1,0:T(8,128)(2,1)}, u32[]{:S(2)}, u32[]{:S(2)}) collective-permute-start(bf16[9,160,640]{2,1,0:T(8,128)(2,1)S(1)} %get-tuple-element.433), channel_id=1, source_target_pairs={{4,0},{9,5},{13,9},{6,2},{11,7},{15,11},{20,16},{25,21},{29,25},{2... | collective-permute-start | bytes 5529608 | tf_op jit(solution)/shard_map/ppermute | solution.py:157
  5.1 35.5 %collective-permute-start.10 = (bf16[9,160,640]{2,1,0:T(8,128)(2,1)S(1)}, bf16[9,160,640]{2,1,0:T(8,128)(2,1)}, u32[]{:S(2)}, u32[]{:S(2)}) collective-permute-start(bf16[9,160,640]{2,1,0:T(8,128)(2,1)S(1)} %get-tuple-element.433), channel_id=1, source_target_pairs={{0,4},{4,8},{9,13},{2,6},{6,10},{11,15},{16,20},{20,24},{25,29},{1... | collective-permute-start | bytes 5529608 | tf_op jit(solution)/shard_map/ppermute | solution.py:157
  38.7 21.7 %collective-permute-start.6 = (bf16[9,160,640]{2,1,0:T(8,128)(2,1)}, bf16[9,160,640]{2,1,0:T(8,128)(2,1)}, u32[]{:S(2)}, u32[]{:S(2)}) collective-permute-start(bf16[9,160,640]{2,1,0:T(8,128)(2,1)} %collective-permute-done.4), channel_id=1, source_target_pairs={{5,1},{9,5},{7,3},{11,7},{21,17},{25,21},{23,19},{27,23}} | collective-permute-start | bytes 5529608 | tf_op jit(solution)/shard_map/ppermute | solution.py:157
  40.6 21.8 %collective-permute-start.12 = (bf16[9,160,640]{2,1,0:T(8,128)(2,1)}, bf16[9,160,640]{2,1,0:T(8,128)(2,1)}, u32[]{:S(2)}, u32[]{:S(2)}) collective-permute-start(bf16[9,160,640]{2,1,0:T(8,128)(2,1)} %collective-permute-done.10), channel_id=1, source_target_pairs={{4,8},{8,12},{6,10},{10,14},{20,24},{24,28},{22,26},{26,30}} | collective-permute-start | bytes 5529608 | tf_op jit(solution)/shard_map/ppermute | solution.py:157
  44.8 26.1 %collective-permute-start.5 = (bf16[9,160,640]{2,1,0:T(8,128)(2,1)}, bf16[9,160,640]{2,1,0:T(8,128)(2,1)}, u32[]{:S(2)}, u32[]{:S(2)}) collective-permute-start(bf16[9,160,640]{2,1,0:T(8,128)(2,1)} %collective-permute-done.4), channel_id=1, source_target_pairs={{0,16},{5,21},{9,25},{16,0},{21,5},{25,9},{2,18},{7,23},{11,27},{1... | collective-permute-start | bytes 5529608 | tf_op jit(solution)/shard_map/ppermute | solution.py:164
  49.4 22.8 %collective-permute-start.11 = (bf16[9,160,640]{2,1,0:T(8,128)(2,1)}, bf16[9,160,640]{2,1,0:T(8,128)(2,1)}, u32[]{:S(2)}, u32[]{:S(2)}) collective-permute-start(bf16[9,160,640]{2,1,0:T(8,128)(2,1)} %collective-permute-done.10), channel_id=1, source_target_pairs={{4,20},{8,24},{13,29},{20,4},{24,8},{29,13},{6,22},{10,26},{15,31}... | collective-permute-start | bytes 5529608 | tf_op jit(solution)/shard_map/ppermute | solution.py:164
  54.2 26.1 %collective-permute-start.30 = (bf16[9,160,640]{2,1,0:T(8,128)(2,1)}, bf16[9,160,640]{2,1,0:T(8,128)(2,1)}, u32[]{:S(2)}, u32[]{:S(2)}) collective-permute-start(bf16[9,160,640]{2,1,0:T(8,128)(2,1)} %get-tuple-element.435), channel_id=1, source_target_pairs={{0,4},{4,8},{9,13},{2,6},{6,10},{11,15},{16,20},{20,24},{25,29},{1... | collective-permute-start | bytes 5529608 | tf_op jit(solution)/shard_map/ppermute | solution.py:157
  60.5 21.8 %collective-permute-start.8 = (bf16[9,160,640]{2,1,0:T(8,128)(2,1)}, bf16[9,160,640]{2,1,0:T(8,128)(2,1)}, u32[]{:S(2)}, u32[]{:S(2)}) collective-permute-start(bf16[9,160,640]{2,1,0:T(8,128)(2,1)} %collective-permute-done.6), channel_id=1, source_target_pairs={{5,1},{7,3},{21,17},{23,19}} | collective-permute-start | bytes 5529608 | tf_op jit(solution)/shard_map/ppermute | solution.py:157
  62.4 21.8 %collective-permute-start.14 = (bf16[9,160,640]{2,1,0:T(8,128)(2,1)}, bf16[9,160,640]{2,1,0:T(8,128)(2,1)}, u32[]{:S(2)}, u32[]{:S(2)}) collective-permute-start(bf16[9,160,640]{2,1,0:T(8,128)(2,1)} %collective-permute-done.12), channel_id=1, source_target_pairs={{8,12},{10,14},{24,28},{26,30}} | collective-permute-start | bytes 5529608 | tf_op jit(solution)/shard_map/ppermute | solution.py:157
  70.9 35.8 %collective-permute-start.24 = (bf16[9,160,640]{2,1,0:T(8,128)(2,1)}, bf16[9,160,640]{2,1,0:T(8,128)(2,1)}, u32[]{:S(2)}, u32[]{:S(2)}) collective-permute-start(bf16[9,160,640]{2,1,0:T(8,128)(2,1)} %get-tuple-element.435), channel_id=1, source_target_pairs={{4,0},{9,5},{13,9},{6,2},{11,7},{15,11},{20,16},{25,21},{29,25},{2... | collective-permute-start | bytes 5529608 | tf_op jit(solution)/shard_map/ppermute | solution.py:157
  72.2 36.5 %collective-permute-start.7 = (bf16[9,160,640]{2,1,0:T(8,128)(2,1)}, bf16[9,160,640]{2,1,0:T(8,128)(2,1)}, u32[]{:S(2)}, u32[]{:S(2)}) collective-permute-start(bf16[9,160,640]{2,1,0:T(8,128)(2,1)} %collective-permute-done.6), channel_id=1, source_target_pairs={{1,17},{5,21},{17,1},{21,5},{3,19},{7,23},{19,3},{23,7}} | collective-permute-start | bytes 5529608 | tf_op jit(solution)/shard_map/ppermute | solution.py:164
  80.3 30.3 %collective-permute-start.13 = (bf16[9,160,640]{2,1,0:T(8,128)(2,1)}, bf16[9,160,640]{2,1,0:T(8,128)(2,1)}, u32[]{:S(2)}, u32[]{:S(2)}) collective-permute-start(bf16[9,160,640]{2,1,0:T(8,128)(2,1)} %collective-permute-done.12), channel_id=1, source_target_pairs={{8,24},{12,28},{24,8},{28,12},{10,26},{14,30},{26,10},{30,14}} | collective-permute-start | bytes 5529608 | tf_op jit(solution)/shard_map/ppermute | solution.py:164
  82.3 28.4 %collective-permute-start.9 = (bf16[9,160,640]{2,1,0:T(8,128)(2,1)}, bf16[9,160,640]{2,1,0:T(8,128)(2,1)}, u32[]{:S(2)}, u32[]{:S(2)}) collective-permute-start(bf16[9,160,640]{2,1,0:T(8,128)(2,1)} %collective-permute-done.8), channel_id=1, source_target_pairs={{1,17},{17,1},{3,19},{19,3}} | collective-permute-start | bytes 5529608 | tf_op jit(solution)/shard_map/ppermute | solution.py:164
  84.2 26.5 %collective-permute-start.15 = (bf16[9,160,640]{2,1,0:T(8,128)(2,1)}, bf16[9,160,640]{2,1,0:T(8,128)(2,1)}, u32[]{:S(2)}, u32[]{:S(2)}) collective-permute-start(bf16[9,160,640]{2,1,0:T(8,128)(2,1)} %collective-permute-done.14), channel_id=1, source_target_pairs={{12,28},{28,12},{14,30},{30,14}} | collective-permute-start | bytes 5529608 | tf_op jit(solution)/shard_map/ppermute | solution.py:164
  106.8 60.2 %collective-permute-start.32 = (bf16[9,160,640]{2,1,0:T(8,128)(2,1)}, bf16[9,160,640]{2,1,0:T(8,128)(2,1)}, u32[]{:S(2)}, u32[]{:S(2)}) collective-permute-start(bf16[9,160,640]{2,1,0:T(8,128)(2,1)} %collective-permute-done.30), channel_id=1, source_target_pairs={{4,8},{8,12},{6,10},{10,14},{20,24},{24,28},{22,26},{26,30}} | collective-permute-start | bytes 5529608 | tf_op jit(solution)/shard_map/ppermute | solution.py:157
  108.7 60.2 %collective-permute-start.26 = (bf16[9,160,640]{2,1,0:T(8,128)(2,1)}, bf16[9,160,640]{2,1,0:T(8,128)(2,1)}, u32[]{:S(2)}, u32[]{:S(2)}) collective-permute-start(bf16[9,160,640]{2,1,0:T(8,128)(2,1)} %collective-permute-done.24), channel_id=1, source_target_pairs={{5,1},{9,5},{7,3},{11,7},{21,17},{25,21},{23,19},{27,23}} | collective-permute-start | bytes 5529608 | tf_op jit(solution)/shard_map/ppermute | solution.py:157
  147.1 25.3 %collective-permute-start.16 = (bf16[640,6,128]{2,0,1:T(8,128)(2,1)}, bf16[640,6,128]{2,0,1:T(8,128)(2,1)}, u32[]{:S(2)}, u32[]{:S(2)}) collective-permute-start(bf16[640,6,128]{2,0,1:T(8,128)(2,1)} %bitcast.140), channel_id=1, source_target_pairs={{1,2},{2,1},{5,6},{6,5},{9,10},{10,9},{13,14},{14,13},{17,18},{18,... | collective-permute-start | bytes 2949128 | tf_op jit(solution)/shard_map/ppermute | solution.py:216
  151.0 35.1 %collective-permute-start.17 = (bf16[640,6,128]{2,0,1:T(8,128)(2,1)}, bf16[640,6,128]{2,0,1:T(8,128)(2,1)}, u32[]{:S(2)}, u32[]{:S(2)}) collective-permute-start(bf16[640,6,128]{2,0,1:T(8,128)(2,1)} %bitcast.141), channel_id=1, source_target_pairs={{0,1},{3,2},{1,3},{2,0},{4,5},{7,6},{5,7},{6,4},{8,9},{11,10},{9,1... | collective-permute-start | bytes 2949128 | tf_op jit(solution)/shard_map/ppermute | solution.py:215
  165.0 48.1 %collective-permute-start.31 = (bf16[9,160,640]{2,1,0:T(8,128)(2,1)}, bf16[9,160,640]{2,1,0:T(8,128)(2,1)}, u32[]{:S(2)}, u32[]{:S(2)}) collective-permute-start(bf16[9,160,640]{2,1,0:T(8,128)(2,1)} %collective-permute-done.30), channel_id=1, source_target_pairs={{4,20},{8,24},{13,29},{20,4},{24,8},{29,13},{6,22},{10,26},{15,31}... | collective-permute-start | bytes 5529608 | tf_op jit(solution)/shard_map/ppermute | solution.py:164
  167.0 47.4 %collective-permute-start.34 = (bf16[9,160,640]{2,1,0:T(8,128)(2,1)}, bf16[9,160,640]{2,1,0:T(8,128)(2,1)}, u32[]{:S(2)}, u32[]{:S(2)}) collective-permute-start(bf16[9,160,640]{2,1,0:T(8,128)(2,1)} %collective-permute-done.32), channel_id=1, source_target_pairs={{8,12},{10,14},{24,28},{26,30}} | collective-permute-start | bytes 5529608 | tf_op jit(solution)/shard_map/ppermute | solution.py:157
  168.9 47.5 %collective-permute-start.28 = (bf16[9,160,640]{2,1,0:T(8,128)(2,1)}, bf16[9,160,640]{2,1,0:T(8,128)(2,1)}, u32[]{:S(2)}, u32[]{:S(2)}) collective-permute-start(bf16[9,160,640]{2,1,0:T(8,128)(2,1)} %collective-permute-done.26), channel_id=1, source_target_pairs={{5,1},{7,3},{21,17},{23,19}} | collective-permute-start | bytes 5529608 | tf_op jit(solution)/shard_map/ppermute | solution.py:157
  195.6 28.5 %collective-permute-start.25 = (bf16[9,160,640]{2,1,0:T(8,128)(2,1)}, bf16[9,160,640]{2,1,0:T(8,128)(2,1)}, u32[]{:S(2)}, u32[]{:S(2)}) collective-permute-start(bf16[9,160,640]{2,1,0:T(8,128)(2,1)} %collective-permute-done.24), channel_id=1, source_target_pairs={{0,16},{5,21},{9,25},{16,0},{21,5},{25,9},{2,18},{7,23},{11,27},{1... | collective-permute-start | bytes 5529608 | tf_op jit(solution)/shard_map/ppermute | solution.py:164
  271.3 43.2 %collective-permute-start.36 = (bf16[640,6,128]{2,0,1:T(8,128)(2,1)}, bf16[640,6,128]{2,0,1:T(8,128)(2,1)}, u32[]{:S(2)}, u32[]{:S(2)}) collective-permute-start(bf16[640,6,128]{2,0,1:T(8,128)(2,1)} %bitcast.142), channel_id=1, source_target_pairs={{1,2},{2,1},{5,6},{6,5},{9,10},{10,9},{13,14},{14,13},{17,18},{18,... | collective-permute-start | bytes 2949128 | tf_op jit(solution)/shard_map/ppermute | solution.py:216
  275.2 59.3 %collective-permute-start.37 = (bf16[640,6,128]{2,0,1:T(8,128)(2,1)}, bf16[640,6,128]{2,0,1:T(8,128)(2,1)}, u32[]{:S(2)}, u32[]{:S(2)}) collective-permute-start(bf16[640,6,128]{2,0,1:T(8,128)(2,1)} %bitcast.143), channel_id=1, source_target_pairs={{0,1},{3,2},{1,3},{2,0},{4,5},{7,6},{5,7},{6,4},{8,9},{11,10},{9,1... | collective-permute-start | bytes 2949128 | tf_op jit(solution)/shard_map/ppermute | solution.py:215
  (37 other events, 908.7 us)

commit v3 on v0

--- a/solution.py
+++ b/solution.py
@@ -177,12 +177,12 @@
                     d = 1 if s < z else -1
                     t = abs(z - s)
                     mine, other = table[(t, d)], table[(t, d, "o")]
-                pieces += [mine, other] if g == 0 else [other, mine]
+                pieces += [mine, other]
             return jnp.concatenate(pieces, axis=1)
         return run
 
-    cases = [branch(z, cc, g) for g in range(2) for z in range(n_p) for cc in range(n_c)]
-    index = (y * n_p + p) * n_c + c
+    cases = [branch(z, cc, 0) for z in range(n_p) for cc in range(n_c)]
+    index = p * n_c + c
     return lax.switch(index, cases, *operands), lines
 
 
@@ -216,6 +216,14 @@
     got_b = lax.ppermute(piece(1 - c), ("chan", "col"), [(1, 2), (2, 1)])
     first = jnp.where(k == c, piece(c), got_b)
     return first.astype(jnp.float32) + got_a.astype(jnp.float32)
+
+
+def unswap_halves(total):
+    roles = lax.axis_size("patch") // lax.axis_size("col")
+    blocks = total.reshape(roles, 2, -1, *total.shape[1:])
+    swapped = blocks[:, ::-1]
+    y = lax.axis_index("groups")
+    return jnp.where(y == 0, blocks, swapped).reshape(total.shape)
 
 
 def fast_path():
@@ -272,7 +280,7 @@
     lower_rim = rim_act[:, 1:2, :] * (where_patch < patches - 1).astype(jnp.float32)
     block_one = jnp.concatenate([upper_rim, own_act, lower_rim], axis=1).astype(jnp.bfloat16)
     if fast:
-        sum_one = reduce_cores(conv_full(full_width(block_one), weight_one))
+        sum_one = unswap_halves(reduce_cores(conv_full(full_width(block_one), weight_one)))
     else:
         padded_one = extended(block_one, (("col", 2),), 1)
         sum_one = reduce_chan(conv_slots(padded_one, slots_one), ids_one)
@@ -283,7 +291,7 @@
     act_two = activate(hidden32, mean_two, inv_two, gn2_gain, gn2_shift).astype(jnp.bfloat16)
     if fast:
         rows_two = extended(act_two, (("patch", 1),), 1)
-        sum_two = reduce_cores(conv_full(full_width(rows_two), weight_two))
+        sum_two = unswap_halves(reduce_cores(conv_full(full_width(rows_two), weight_two)))
     else:
         padded_two = extended(act_two, (("patch", 1), ("col", 2)), 1)
         sum_two = reduce_chan(conv_slots(padded_two, slots_two), ids_two)

time: 339 us -> 346 us (1.021)
  local copies, waits for them, and re-layouts: 54.1 us -> 46.3 us
  waiting for transfers between devices: 81.2 us -> 89 us
  other arithmetic: 39.2 us -> 46.1 us
    unnamed x56 -> x50, local copies, waits for them, and re-layouts: 29.9 us -> 14.9 us
    ppermute x2, waiting for transfers between devices: 33.8 us -> 41.6 us  [reduce_cores(): lax.ppermute(send_a, ('chan', 'col'), [(0, 1), (3, 2), (1, 3), (2, 0)])]
    add x0 -> x4, local copies, waits for them, and re-layouts: none -> 5.97 us  [the longest x2 5.81 us: reduce_cores(): return first.astype(jnp.float32) + got_a.astype(jnp.float32)]
    add x0 -> x2, other arithmetic: none -> 4.75 us  [reduce_cores(): return first.astype(jnp.float32) + got_a.astype(jnp.float32)]
  transfers between devices with their start and end apart: 38 -> 38, of which waited for: 10 -> 10; matrix products, arithmetic and copies ran while one was open for 24% -> 22% of each run, Pallas kernels for 0% -> 0%
where the time goes in v3:
time: 346 us; the launch traced here: 345 us
  starting transfers between devices  126 us (36%)
  waiting for transfers between devices  89 us (26%)
  local copies, waits for them, and re-layouts  46.3 us (13%)
  other arithmetic  46.1 us (13%)
  matrix products  35.9 us (10%)
    ppermute x2, starting transfers between devices, reduce_cores(): lax.ppermute(send_a, ('chan', 'col'), [(0, 1), (3, 2), (1, 3), (2, 0)])  45.1 us
    ppermute x2, waiting for transfers between devices, reduce_cores(): lax.ppermute(send_a, ('chan', 'col'), [(0, 1), (3, 2), (1, 3), (2, 0)])  41.6 us
    conv_general_dilated x2, matrix products, conv_full(): lax.conv_general_dilated(padded[None], kernel, window_strides=(1, 1), pad...  35.6 us
    ppermute x12, starting transfers between devices, line_weights(): got = lax.ppermute(last[d], ('patch', 'col'), pairs)  31.7 us
    ppermute x12, starting transfers between devices, line_weights(): bufs[t, d, 'o'] = lax.ppermute(got, ('groups', 'patch', 'col'), trade)  27.2 us
    ppermute x4, waiting for transfers between devices, group_moments(): lax.ppermute(summed, 'patch', [(i, i ^ step) for i in range(n_p)])  23.4 us
    unnamed x50, local copies, waits for them, and re-layouts  14.9 us
    ppermute x4, starting transfers between devices, group_moments(): lax.ppermute(summed, 'patch', [(i, i ^ step) for i in range(n_p)])  14.4 us
  transfers between devices with their start and end apart: 38, of which 10 were waited for; matrix products, arithmetic and copies ran while one was open for 22% of the time, Pallas kernels for 0%

profile of v3, /device:TPU:0, one launch (start us, length us, event | category | flops | bytes accessed | tf_op | source)
XLA Modules:
  0.0 344.6 jit_solution(4014858043113958636)
XLA Ops:
  5.1 7.5 %collective-permute-start.10 = (bf16[9,160,640]{2,1,0:T(8,128)(2,1)S(1)}, bf16[9,160,640]{2,1,0:T(8,128)(2,1)}, u32[]{:S(2)}, u32[]{:S(2)}) collective-permute-start(bf16[9,160,640]{2,1,0:T(8,128)(2,1)S(1)} %get-tuple-element.223), channel_id=1, source_target_pairs={{0,4},{4,8},{9,13},{2,6},{6,10},{11,15},{16,20},{20,24},{25,29},{1... | collective-permute-start | bytes 5529608 | tf_op jit(solution)/shard_map/ppermute | solution.py:157
  14.7 17.4 %collective-permute-done.1 = f32[2,16]{1,0:T(2,128)S(1)} collective-permute-done((f32[2,16]{1,0:T(2,128)S(1)}, f32[2,16]{1,0:T(2,128)S(1)}, u32[]{:S(2)}, u32[]{:S(2)}) %collective-permute-start.1) | collective-permute-done | bytes 160 | tf_op jit(solution)/shard_map/ppermute | solution.py:39
  32.2 4.5 %collective-permute-done.2 = f32[2,16]{1,0:T(2,128)S(1)} collective-permute-done((f32[2,16]{1,0:T(2,128)S(1)}, f32[2,16]{1,0:T(2,128)S(1)}, u32[]{:S(2)}, u32[]{:S(2)}) %collective-permute-start.2) | collective-permute-done | bytes 160 | tf_op jit(solution)/shard_map/ppermute | solution.py:39
  47.3 6.3 %collective-permute-start.30 = (bf16[9,160,640]{2,1,0:T(8,128)(2,1)}, bf16[9,160,640]{2,1,0:T(8,128)(2,1)}, u32[]{:S(2)}, u32[]{:S(2)}) collective-permute-start(bf16[9,160,640]{2,1,0:T(8,128)(2,1)} %get-tuple-element.225), channel_id=1, source_target_pairs={{0,4},{4,8},{9,13},{2,6},{6,10},{11,15},{16,20},{20,24},{25,29},{1... | collective-permute-start | bytes 5529608 | tf_op jit(solution)/shard_map/ppermute | solution.py:157
  53.6 4.5 %collective-permute-start.5 = (bf16[9,160,640]{2,1,0:T(8,128)(2,1)}, bf16[9,160,640]{2,1,0:T(8,128)(2,1)}, u32[]{:S(2)}, u32[]{:S(2)}) collective-permute-start(bf16[9,160,640]{2,1,0:T(8,128)(2,1)} %collective-permute-done.4), channel_id=1, source_target_pairs={{0,16},{5,21},{9,25},{16,0},{21,5},{25,9},{2,18},{7,23},{11,27},{1... | collective-permute-start | bytes 5529608 | tf_op jit(solution)/shard_map/ppermute | solution.py:164
  64.9 8.6 %collective-permute-done.30 = bf16[9,160,640]{2,1,0:T(8,128)(2,1)} collective-permute-done((bf16[9,160,640]{2,1,0:T(8,128)(2,1)}, bf16[9,160,640]{2,1,0:T(8,128)(2,1)}, u32[]{:S(2)}, u32[]{:S(2)}) %collective-permute-start.30) | collective-permute-done | bytes 1843232 | tf_op jit(solution)/shard_map/ppermute | solution.py:157
  74.8 12.2 %collective-permute-done.5 = bf16[9,160,640]{2,1,0:T(8,128)(2,1)} collective-permute-done((bf16[9,160,640]{2,1,0:T(8,128)(2,1)}, bf16[9,160,640]{2,1,0:T(8,128)(2,1)}, u32[]{:S(2)}, u32[]{:S(2)}) %collective-permute-start.5) | collective-permute-done | bytes 1843232 | tf_op jit(solution)/shard_map/ppermute | solution.py:164
  96.6 4.0 %fusion.7 = bf16[640,8,1,258]{3,0,1,2:T(8,128)(2,1)} fusion(bf16[640,8,128]{2,0,1:T(8,128)(2,1)S(1)} %get-tuple-element.229, bf16[640,8,128]{2,0,1:T(8,128)(2,1)S(1)} %get-tuple-element.228), kind=kLoop, calls=%fused_computation.29 | loop fusion | flops 11888640 | bytes 5263360 | tf_op jit(solution)/shard_map/broadcast_in_dim | solution.py:200
  100.6 5.9 %copy.68 = bf16[640,8,1,258]{0,1,3,2:T(8,128)(2,1)} copy(bf16[640,8,1,258]{3,0,1,2:T(8,128)(2,1)} %fusion.7) | data formatting | bytes 5283840
  113.6 6.5 %conditional.2 = (bf16[3,3,640,640]{3,2,1,0:T(8,128)(2,1)}) conditional(s32[]{:T(128)} %clamp.4, (bf16[9,160,640]{2,1,0:T(8,128)(2,1)S(1)}, bf16[9,160,640]{2,1,0:T(8,128)(2,1)S(1)}, bf16[9,160,640]{2,1,0:T(8,128)(2,1)}, bf16[9,160,640]{2,1,0:T(8,128)(2,1)}) %tuple.113, (bf16[9,160,640]{2,1,0:T(8,128)(2,1)}, ...), branch_computations={%region_4.0_spmd, %region_5.0_spmd, %region_6.0_spmd, %region_7.0_... | conditional | flops 29491200 | bytes 14745608 | solution.py:186
  113.6 6.5 %pad_maximum_fusion = bf16[9,640,640]{2,1,0:T(8,128)(2,1)} fusion(bf16[9,160,640]{2,1,0:T(8,128)(2,1)} %get-tuple-element.144, bf16[9,160,640]{2,1,0:T(8,128)(2,1)} %get-tuple-element.143, bf16[9,160,640]{2,1,0:T(8,128)(2,1)S(1)} %get-tuple-element.142, bf16[9,160,640]{2,1,0:T(8,128)(2,1)S(1)} %get-tuple-element.141), kind=kLoop, calls=%fused_computation | loop fusion | flops 29491200 | bytes 14745600 | tf_op jit(solution)/shard_map/cond/branch_0_fun/concatenate | solution.py:181
  120.1 18.2 %select_convert_fusion.1 = bf16[6,8,33,640]{3,1,2,0:T(8,128)(2,1)S(1)} fusion(pred[8,33]{0,1:T(8,128)(4,1)S(1)} %copy-done.23, bf16[3,3,640,640]{3,2,1,0:T(8,128)(2,1)} %get-tuple-element.240, bf16[640,8,1,7,2]{0,3,4,1,2:T(8,128)(2,1)} %slice.38, bf16[640,8,1,8,33]{0,3,4,1,2:T(8,128)(2,1)} %copy-done.10), kind=kOutput, calls=%fused_computation.23 | convolution fusion | flops 11689144320 | bytes 12247304 | tf_op jit(solution)/shard_map/conv_general_dilated | solution.py:199
  140.1 4.1 %reshape.143 = bf16[6,1,264,640]{3,2,0,1:T(8,128)(2,1)} reshape(bf16[6,8,33,640]{3,2,1,0:T(8,128)(2,1)} %copy.61) | data formatting | bytes 4055040 | tf_op jit(solution)/shard_map/convert_element_type | solution.py:207
  150.3 7.3 %collective-permute-start.17 = (bf16[640,6,128]{0,2,1:T(8,128)(2,1)}, bf16[640,6,128]{0,2,1:T(8,128)(2,1)}, u32[]{:S(2)}, u32[]{:S(2)}) collective-permute-start(bf16[640,6,128]{0,2,1:T(8,128)(2,1)} %get-tuple-element.233), channel_id=1, source_target_pairs={{0,1},{3,2},{1,3},{2,0},{4,5},{7,6},{5,7},{6,4},{8,9},{11,10},{9,1... | collective-permute-start | bytes 2949128 | tf_op jit(solution)/shard_map/ppermute | solution.py:215
  164.6 17.4 %collective-permute-done.17 = bf16[640,6,128]{0,2,1:T(8,128)(2,1)} collective-permute-done((bf16[640,6,128]{0,2,1:T(8,128)(2,1)}, bf16[640,6,128]{0,2,1:T(8,128)(2,1)}, u32[]{:S(2)}, u32[]{:S(2)}) %collective-permute-start.17) | collective-permute-done | bytes 983072 | tf_op jit(solution)/shard_map/ppermute | solution.py:215
  188.0 4.0 %convert_reduce_fusion.1 = (f32[2,2,160]{2,1,0:T(2,128)S(1)}, f32[2,2,160]{2,1,0:T(2,128)S(1)}, f32[2,2,160,6,128]{4,2,1,0,3:T(8,128)}) fusion(f32[2,2,160]{2,1,0:T(2,128)S(1)} %add.173, f32[2,2,160]{2,1,0:T(2,128)S(1)} %add.170, f32[2,2,160,6,128]{4,2,1,0,3:T(8,128)} %bitcast.107, pred[]{:T(512)S(6)} %eq.6), kind=kLoop, calls=%fused_computation.49 | loop fusion | flops 3930880 | bytes 3942401 | tf_op jit(solution)/shard_map/reduce_sum | solution.py:29
  193.7 7.9 %collective-permute-start.19 = (f32[2,16]{1,0:T(2,128)S(1)}, f32[2,16]{1,0:T(2,128)S(1)}, u32[]{:S(2)}, u32[]{:S(2)}) collective-permute-start(f32[2,16]{1,0:T(2,128)S(1)} %fusion.56), channel_id=1, source_target_pairs={{0,4},{4,0},{8,12},{12,8},{1,5},{5,1},{9,13},{13,9},{2,6},{6,2},{1... | collective-permute-start | bytes 392 | tf_op jit(solution)/shard_map/ppermute | solution.py:39
  205.0 6.3 %collective-permute-start.20 = (f32[2,16]{1,0:T(2,128)S(1)}, f32[2,16]{1,0:T(2,128)S(1)}, u32[]{:S(2)}, u32[]{:S(2)}) collective-permute-start(f32[2,16]{1,0:T(2,128)S(1)} %fusion.63), channel_id=1, source_target_pairs={{0,8},{4,12},{8,0},{12,4},{1,9},{5,13},{9,1},{13,5},{2,10},{6,14},... | collective-permute-start | bytes 392 | tf_op jit(solution)/shard_map/ppermute | solution.py:39
  230.3 7.4 %conditional.3 = (bf16[3,3,640,640]{3,2,1,0:T(8,128)(2,1)}) conditional(s32[]{:T(128)} %clamp.4, (bf16[9,160,640]{2,1,0:T(8,128)(2,1)}, bf16[9,160,640]{2,1,0:T(8,128)(2,1)S(1)}, bf16[9,160,640]{2,1,0:T(8,128)(2,1)}, bf16[9,160,640]{2,1,0:T(8,128)(2,1)}) %tuple.75, (bf16[9,160,640]{2,1,0:T(8,128)(2,1)}, ...), branch_computations={%region_16.0_spmd, %region_17.0_spmd, %region_18.19_spmd, %region_... | conditional | flops 29491200 | bytes 14745608 | solution.py:186
  230.3 7.4 %pad_maximum_fusion.8 = bf16[9,640,640]{2,1,0:T(8,128)(2,1)} fusion(bf16[9,160,640]{2,1,0:T(8,128)(2,1)} %get-tuple-element.188, bf16[9,160,640]{2,1,0:T(8,128)(2,1)} %get-tuple-element.187, bf16[9,160,640]{2,1,0:T(8,128)(2,1)S(1)} %get-tuple-element.186, bf16[9,160,640]{2,1,0:T(8,128)(2,1)} %get-tuple-element.185), kind=kLoop, calls=%fused_computation.8 | loop fusion | flops 29491200 | bytes 14745600 | tf_op jit(solution)/shard_map/cond/branch_0_fun/concatenate | solution.py:181
  243.3 5.9 %copy.69 = bf16[640,8,1,258]{0,1,3,2:T(8,128)(2,1)} copy(bf16[640,8,1,258]{3,0,1,2:T(8,128)(2,1)} %fusion.3) | data formatting | bytes 5283840
  251.5 17.4 %select_convert_fusion = bf16[6,8,33,640]{3,1,2,0:T(8,128)(2,1)S(1)} fusion(pred[8,33]{0,1:T(8,128)(4,1)S(1)} %copy-done.23, bf16[3,3,640,640]{3,2,1,0:T(8,128)(2,1)} %get-tuple-element.241, bf16[640,8,1,7,2]{0,3,4,1,2:T(8,128)(2,1)S(1)} %slice.42, bf16[640,8,1,8,33]{0,3,4,1,2:T(8,128)(2,1)S(1)} %copy.65), kind=kOutput, calls=%fused_computation.22 | convolution fusion | flops 11689144320 | bytes 12247304 | tf_op jit(solution)/shard_map/conv_general_dilated | solution.py:199
  274.2 37.9 %collective-permute-start.37 = (bf16[640,6,128]{0,2,1:T(8,128)(2,1)S(1)}, bf16[640,6,128]{0,2,1:T(8,128)(2,1)S(1)}, u32[]{:S(2)}, u32[]{:S(2)}) collective-permute-start(bf16[640,6,128]{0,2,1:T(8,128)(2,1)S(1)} %get-tuple-element.231), channel_id=1, source_target_pairs={{0,1},{3,2},{1,3},{2,0},{4,5},{7,6},{5,7},{6,4},{8,9},{11,10},{9,1... | collective-permute-start | bytes 2949128 | tf_op jit(solution)/shard_map/ppermute | solution.py:215
  312.1 24.2 %collective-permute-done.37 = bf16[640,6,128]{0,2,1:T(8,128)(2,1)S(1)} collective-permute-done((bf16[640,6,128]{0,2,1:T(8,128)(2,1)S(1)}, bf16[640,6,128]{0,2,1:T(8,128)(2,1)S(1)}, u32[]{:S(2)}, u32[]{:S(2)}) %collective-permute-start.37) | collective-permute-done | bytes 983072 | tf_op jit(solution)/shard_map/ppermute | solution.py:215
  (177 shorter events, 107.9 us)
Async XLA Ops:
  3.8 34.9 %collective-permute-start.4 = (bf16[9,160,640]{2,1,0:T(8,128)(2,1)S(1)}, bf16[9,160,640]{2,1,0:T(8,128)(2,1)}, u32[]{:S(2)}, u32[]{:S(2)}) collective-permute-start(bf16[9,160,640]{2,1,0:T(8,128)(2,1)S(1)} %get-tuple-element.223), channel_id=1, source_target_pairs={{4,0},{9,5},{13,9},{6,2},{11,7},{15,11},{20,16},{25,21},{29,25},{2... | collective-permute-start | bytes 5529608 | tf_op jit(solution)/shard_map/ppermute | solution.py:157
  5.1 35.6 %collective-permute-start.10 = (bf16[9,160,640]{2,1,0:T(8,128)(2,1)S(1)}, bf16[9,160,640]{2,1,0:T(8,128)(2,1)}, u32[]{:S(2)}, u32[]{:S(2)}) collective-permute-start(bf16[9,160,640]{2,1,0:T(8,128)(2,1)S(1)} %get-tuple-element.223), channel_id=1, source_target_pairs={{0,4},{4,8},{9,13},{2,6},{6,10},{11,15},{16,20},{20,24},{25,29},{1... | collective-permute-start | bytes 5529608 | tf_op jit(solution)/shard_map/ppermute | solution.py:157
  14.6 17.5 %collective-permute-start.1 = (f32[2,16]{1,0:T(2,128)S(1)}, f32[2,16]{1,0:T(2,128)S(1)}, u32[]{:S(2)}, u32[]{:S(2)}) collective-permute-start(f32[2,16]{1,0:T(2,128)S(1)} %fusion.57), channel_id=1, source_target_pairs={{0,4},{4,0},{8,12},{12,8},{1,5},{5,1},{9,13},{13,9},{2,6},{6,2},{1... | collective-permute-start | bytes 392 | tf_op jit(solution)/shard_map/ppermute | solution.py:39
  38.7 22.4 %collective-permute-start.6 = (bf16[9,160,640]{2,1,0:T(8,128)(2,1)}, bf16[9,160,640]{2,1,0:T(8,128)(2,1)}, u32[]{:S(2)}, u32[]{:S(2)}) collective-permute-start(bf16[9,160,640]{2,1,0:T(8,128)(2,1)} %collective-permute-done.4), channel_id=1, source_target_pairs={{5,1},{9,5},{7,3},{11,7},{21,17},{25,21},{23,19},{27,23}} | collective-permute-start | bytes 5529608 | tf_op jit(solution)/shard_map/ppermute | solution.py:157
  40.6 22.4 %collective-permute-start.12 = (bf16[9,160,640]{2,1,0:T(8,128)(2,1)}, bf16[9,160,640]{2,1,0:T(8,128)(2,1)}, u32[]{:S(2)}, u32[]{:S(2)}) collective-permute-start(bf16[9,160,640]{2,1,0:T(8,128)(2,1)} %collective-permute-done.10), channel_id=1, source_target_pairs={{4,8},{8,12},{6,10},{10,14},{20,24},{24,28},{22,26},{26,30}} | collective-permute-start | bytes 5529608 | tf_op jit(solution)/shard_map/ppermute | solution.py:157
  47.3 26.2 %collective-permute-start.30 = (bf16[9,160,640]{2,1,0:T(8,128)(2,1)}, bf16[9,160,640]{2,1,0:T(8,128)(2,1)}, u32[]{:S(2)}, u32[]{:S(2)}) collective-permute-start(bf16[9,160,640]{2,1,0:T(8,128)(2,1)} %get-tuple-element.225), channel_id=1, source_target_pairs={{0,4},{4,8},{9,13},{2,6},{6,10},{11,15},{16,20},{20,24},{25,29},{1... | collective-permute-start | bytes 5529608 | tf_op jit(solution)/shard_map/ppermute | solution.py:157
  53.6 33.4 %collective-permute-start.5 = (bf16[9,160,640]{2,1,0:T(8,128)(2,1)}, bf16[9,160,640]{2,1,0:T(8,128)(2,1)}, u32[]{:S(2)}, u32[]{:S(2)}) collective-permute-start(bf16[9,160,640]{2,1,0:T(8,128)(2,1)} %collective-permute-done.4), channel_id=1, source_target_pairs={{0,16},{5,21},{9,25},{16,0},{21,5},{25,9},{2,18},{7,23},{11,27},{1... | collective-permute-start | bytes 5529608 | tf_op jit(solution)/shard_map/ppermute | solution.py:164
  59.2 29.7 %collective-permute-start.11 = (bf16[9,160,640]{2,1,0:T(8,128)(2,1)}, bf16[9,160,640]{2,1,0:T(8,128)(2,1)}, u32[]{:S(2)}, u32[]{:S(2)}) collective-permute-start(bf16[9,160,640]{2,1,0:T(8,128)(2,1)} %collective-permute-done.10), channel_id=1, source_target_pairs={{4,20},{8,24},{13,29},{20,4},{24,8},{29,13},{6,22},{10,26},{15,31}... | collective-permute-start | bytes 5529608 | tf_op jit(solution)/shard_map/ppermute | solution.py:164
  61.1 29.8 %collective-permute-start.8 = (bf16[9,160,640]{2,1,0:T(8,128)(2,1)}, bf16[9,160,640]{2,1,0:T(8,128)(2,1)}, u32[]{:S(2)}, u32[]{:S(2)}) collective-permute-start(bf16[9,160,640]{2,1,0:T(8,128)(2,1)} %collective-permute-done.6), channel_id=1, source_target_pairs={{5,1},{7,3},{21,17},{23,19}} | collective-permute-start | bytes 5529608 | tf_op jit(solution)/shard_map/ppermute | solution.py:157
  63.0 29.8 %collective-permute-start.14 = (bf16[9,160,640]{2,1,0:T(8,128)(2,1)}, bf16[9,160,640]{2,1,0:T(8,128)(2,1)}, u32[]{:S(2)}, u32[]{:S(2)}) collective-permute-start(bf16[9,160,640]{2,1,0:T(8,128)(2,1)} %collective-permute-done.12), channel_id=1, source_target_pairs={{8,12},{10,14},{24,28},{26,30}} | collective-permute-start | bytes 5529608 | tf_op jit(solution)/shard_map/ppermute | solution.py:157
  73.5 36.1 %collective-permute-start.24 = (bf16[9,160,640]{2,1,0:T(8,128)(2,1)}, bf16[9,160,640]{2,1,0:T(8,128)(2,1)}, u32[]{:S(2)}, u32[]{:S(2)}) collective-permute-start(bf16[9,160,640]{2,1,0:T(8,128)(2,1)} %get-tuple-element.225), channel_id=1, source_target_pairs={{4,0},{9,5},{13,9},{6,2},{11,7},{15,11},{20,16},{25,21},{29,25},{2... | collective-permute-start | bytes 5529608 | tf_op jit(solution)/shard_map/ppermute | solution.py:157
  87.0 24.6 %collective-permute-start.7 = (bf16[9,160,640]{2,1,0:T(8,128)(2,1)}, bf16[9,160,640]{2,1,0:T(8,128)(2,1)}, u32[]{:S(2)}, u32[]{:S(2)}) collective-permute-start(bf16[9,160,640]{2,1,0:T(8,128)(2,1)} %collective-permute-done.6), channel_id=1, source_target_pairs={{1,17},{5,21},{17,1},{21,5},{3,19},{7,23},{19,3},{23,7}} | collective-permute-start | bytes 5529608 | tf_op jit(solution)/shard_map/ppermute | solution.py:164
  88.9 24.6 %collective-permute-start.13 = (bf16[9,160,640]{2,1,0:T(8,128)(2,1)}, bf16[9,160,640]{2,1,0:T(8,128)(2,1)}, u32[]{:S(2)}, u32[]{:S(2)}) collective-permute-start(bf16[9,160,640]{2,1,0:T(8,128)(2,1)} %collective-permute-done.12), channel_id=1, source_target_pairs={{8,24},{12,28},{24,8},{28,12},{10,26},{14,30},{26,10},{30,14}} | collective-permute-start | bytes 5529608 | tf_op jit(solution)/shard_map/ppermute | solution.py:164
  91.0 22.6 %collective-permute-start.9 = (bf16[9,160,640]{2,1,0:T(8,128)(2,1)}, bf16[9,160,640]{2,1,0:T(8,128)(2,1)}, u32[]{:S(2)}, u32[]{:S(2)}) collective-permute-start(bf16[9,160,640]{2,1,0:T(8,128)(2,1)} %collective-permute-done.8), channel_id=1, source_target_pairs={{1,17},{17,1},{3,19},{19,3}} | collective-permute-start | bytes 5529608 | tf_op jit(solution)/shard_map/ppermute | solution.py:164
  92.9 20.7 %collective-permute-start.15 = (bf16[9,160,640]{2,1,0:T(8,128)(2,1)}, bf16[9,160,640]{2,1,0:T(8,128)(2,1)}, u32[]{:S(2)}, u32[]{:S(2)}) collective-permute-start(bf16[9,160,640]{2,1,0:T(8,128)(2,1)} %collective-permute-done.14), channel_id=1, source_target_pairs={{12,28},{28,12},{14,30},{30,14}} | collective-permute-start | bytes 5529608 | tf_op jit(solution)/shard_map/ppermute | solution.py:164
  109.6 51.2 %collective-permute-start.32 = (bf16[9,160,640]{2,1,0:T(8,128)(2,1)}, bf16[9,160,640]{2,1,0:T(8,128)(2,1)}, u32[]{:S(2)}, u32[]{:S(2)}) collective-permute-start(bf16[9,160,640]{2,1,0:T(8,128)(2,1)} %collective-permute-done.30), channel_id=1, source_target_pairs={{4,8},{8,12},{6,10},{10,14},{20,24},{24,28},{22,26},{26,30}} | collective-permute-start | bytes 5529608 | tf_op jit(solution)/shard_map/ppermute | solution.py:157
  111.6 51.1 %collective-permute-start.26 = (bf16[9,160,640]{2,1,0:T(8,128)(2,1)}, bf16[9,160,640]{2,1,0:T(8,128)(2,1)}, u32[]{:S(2)}, u32[]{:S(2)}) collective-permute-start(bf16[9,160,640]{2,1,0:T(8,128)(2,1)} %collective-permute-done.24), channel_id=1, source_target_pairs={{5,1},{9,5},{7,3},{11,7},{21,17},{25,21},{23,19},{27,23}} | collective-permute-start | bytes 5529608 | tf_op jit(solution)/shard_map/ppermute | solution.py:157
  150.3 31.8 %collective-permute-start.17 = (bf16[640,6,128]{0,2,1:T(8,128)(2,1)}, bf16[640,6,128]{0,2,1:T(8,128)(2,1)}, u32[]{:S(2)}, u32[]{:S(2)}) collective-permute-start(bf16[640,6,128]{0,2,1:T(8,128)(2,1)} %get-tuple-element.233), channel_id=1, source_target_pairs={{0,1},{3,2},{1,3},{2,0},{4,5},{7,6},{5,7},{6,4},{8,9},{11,10},{9,1... | collective-permute-start | bytes 2949128 | tf_op jit(solution)/shard_map/ppermute | solution.py:215
  158.8 60.4 %collective-permute-start.31 = (bf16[9,160,640]{2,1,0:T(8,128)(2,1)}, bf16[9,160,640]{2,1,0:T(8,128)(2,1)}, u32[]{:S(2)}, u32[]{:S(2)}) collective-permute-start(bf16[9,160,640]{2,1,0:T(8,128)(2,1)} %collective-permute-done.30), channel_id=1, source_target_pairs={{4,20},{8,24},{13,29},{20,4},{24,8},{29,13},{6,22},{10,26},{15,31}... | collective-permute-start | bytes 5529608 | tf_op jit(solution)/shard_map/ppermute | solution.py:164
  160.8 59.7 %collective-permute-start.34 = (bf16[9,160,640]{2,1,0:T(8,128)(2,1)}, bf16[9,160,640]{2,1,0:T(8,128)(2,1)}, u32[]{:S(2)}, u32[]{:S(2)}) collective-permute-start(bf16[9,160,640]{2,1,0:T(8,128)(2,1)} %collective-permute-done.32), channel_id=1, source_target_pairs={{8,12},{10,14},{24,28},{26,30}} | collective-permute-start | bytes 5529608 | tf_op jit(solution)/shard_map/ppermute | solution.py:157
  162.7 59.8 %collective-permute-start.28 = (bf16[9,160,640]{2,1,0:T(8,128)(2,1)}, bf16[9,160,640]{2,1,0:T(8,128)(2,1)}, u32[]{:S(2)}, u32[]{:S(2)}) collective-permute-start(bf16[9,160,640]{2,1,0:T(8,128)(2,1)} %collective-permute-done.26), channel_id=1, source_target_pairs={{5,1},{7,3},{21,17},{23,19}} | collective-permute-start | bytes 5529608 | tf_op jit(solution)/shard_map/ppermute | solution.py:157
  201.5 28.7 %collective-permute-start.25 = (bf16[9,160,640]{2,1,0:T(8,128)(2,1)}, bf16[9,160,640]{2,1,0:T(8,128)(2,1)}, u32[]{:S(2)}, u32[]{:S(2)}) collective-permute-start(bf16[9,160,640]{2,1,0:T(8,128)(2,1)} %collective-permute-done.24), channel_id=1, source_target_pairs={{0,16},{5,21},{9,25},{16,0},{21,5},{25,9},{2,18},{7,23},{11,27},{1... | collective-permute-start | bytes 5529608 | tf_op jit(solution)/shard_map/ppermute | solution.py:164
  273.5 38.6 %collective-permute-start.36 = (bf16[640,6,128]{0,2,1:T(8,128)(2,1)S(1)}, bf16[640,6,128]{0,2,1:T(8,128)(2,1)S(1)}, u32[]{:S(2)}, u32[]{:S(2)}) collective-permute-start(bf16[640,6,128]{0,2,1:T(8,128)(2,1)S(1)} %get-tuple-element.230), channel_id=1, source_target_pairs={{1,2},{2,1},{5,6},{6,5},{9,10},{10,9},{13,14},{14,13},{17,18},{18,... | collective-permute-start | bytes 2949128 | tf_op jit(solution)/shard_map/ppermute | solution.py:216
  274.2 62.0 %collective-permute-start.37 = (bf16[640,6,128]{0,2,1:T(8,128)(2,1)S(1)}, bf16[640,6,128]{0,2,1:T(8,128)(2,1)S(1)}, u32[]{:S(2)}, u32[]{:S(2)}) collective-permute-start(bf16[640,6,128]{0,2,1:T(8,128)(2,1)S(1)} %get-tuple-element.231), channel_id=1, source_target_pairs={{0,1},{3,2},{1,3},{2,0},{4,5},{7,6},{5,7},{6,4},{8,9},{11,10},{9,1... | collective-permute-start | bytes 2949128 | tf_op jit(solution)/shard_map/ppermute | solution.py:215
  (38 other events, 568.7 us)

commit v4 on v3

--- a/solution.py
+++ b/solution.py
@@ -194,7 +194,7 @@
     return jnp.pad(jnp.concatenate([left, right], axis=2), ((0, 0), (0, 0), (1, 1)))
 
 
-def conv_full(padded, weight):
+def conv_full(padded, weight, unswap=False):
     kernel = weight.reshape(3, 3, weight.shape[1], weight.shape[2])
     total = lax.conv_general_dilated(
         padded[None],
@@ -204,6 +204,8 @@
         dimension_numbers=("NCHW", "HWOI", "NCHW"),
         preferred_element_type=jnp.float32,
     )[0]
+    if unswap:
+        total = unswap_halves(total)
     return total.astype(jnp.bfloat16)
 
 
@@ -280,7 +282,7 @@
     lower_rim = rim_act[:, 1:2, :] * (where_patch < patches - 1).astype(jnp.float32)
     block_one = jnp.concatenate([upper_rim, own_act, lower_rim], axis=1).astype(jnp.bfloat16)
     if fast:
-        sum_one = unswap_halves(reduce_cores(conv_full(full_width(block_one), weight_one)))
+        sum_one = reduce_cores(conv_full(full_width(block_one), weight_one, unswap=True))
     else:
         padded_one = extended(block_one, (("col", 2),), 1)
         sum_one = reduce_chan(conv_slots(padded_one, slots_one), ids_one)
@@ -291,7 +293,7 @@
     act_two = activate(hidden32, mean_two, inv_two, gn2_gain, gn2_shift).astype(jnp.bfloat16)
     if fast:
         rows_two = extended(act_two, (("patch", 1),), 1)
-        sum_two = unswap_halves(reduce_cores(conv_full(full_width(rows_two), weight_two)))
+        sum_two = reduce_cores(conv_full(full_width(rows_two), weight_two, unswap=True))
     else:
         padded_two = extended(act_two, (("patch", 1), ("col", 2)), 1)
         sum_two = reduce_chan(conv_slots(padded_two, slots_two), ids_two)

time: 346 us -> 352 us (1.017)
  local copies, waits for them, and re-layouts: 46.3 us -> 54.6 us
    conv_general_dilated x4 -> x12, local copies, waits for them, and re-layouts: 1.43 us -> 27.3 us  [conv_full(): lax.conv_general_dilated(padded[None], kernel, window_strides=(1, 1), pad...]
    convert_element_type x6 -> x0, local copies, waits for them, and re-layouts: 11.9 us -> none  [conv_full(): return total.astype(jnp.bfloat16)]
    add x4 -> x0, local copies, waits for them, and re-layouts: 5.97 us -> none  [the longest x2 5.81 us: reduce_cores(): return first.astype(jnp.float32) + got_a.astype(jnp.float32)]
    convert_element_type x0 -> x2, other arithmetic: none -> 5.67 us  [conv_full(): return total.astype(jnp.bfloat16)]
    add x2 -> x0, other arithmetic: 4.75 us -> none  [reduce_cores(): return first.astype(jnp.float32) + got_a.astype(jnp.float32)]
    unnamed x50 -> x46, local copies, waits for them, and re-layouts: 14.9 us -> 14.9 us
where the time goes in v4:
time: 352 us; the launch traced here: 351 us
  starting transfers between devices  126 us (36%)
  waiting for transfers between devices  89.4 us (25%)
  local copies, waits for them, and re-layouts  54.6 us (16%)
  other arithmetic  43.6 us (12%)
  matrix products  36 us (10%)
    ppermute x2, starting transfers between devices, reduce_cores(): lax.ppermute(send_a, ('chan', 'col'), [(0, 1), (3, 2), (1, 3), (2, 0)])  45.3 us
    ppermute x2, waiting for transfers between devices, reduce_cores(): lax.ppermute(send_a, ('chan', 'col'), [(0, 1), (3, 2), (1, 3), (2, 0)])  41.9 us
    conv_general_dilated x2, matrix products, conv_full(): lax.conv_general_dilated(padded[None], kernel, window_strides=(1, 1), pad...  35.6 us
    ppermute x12, starting transfers between devices, line_weights(): got = lax.ppermute(last[d], ('patch', 'col'), pairs)  31.7 us
    conv_general_dilated x12, local copies, waits for them, and re-layouts, conv_full(): lax.conv_general_dilated(padded[None], kernel, window_strides=(1, 1), pad...  27.3 us
    ppermute x12, starting transfers between devices, line_weights(): bufs[t, d, 'o'] = lax.ppermute(got, ('groups', 'patch', 'col'), trade)  27 us
    ppermute x4, waiting for transfers between devices, group_moments(): lax.ppermute(summed, 'patch', [(i, i ^ step) for i in range(n_p)])  23.4 us
    unnamed x46, local copies, waits for them, and re-layouts  14.9 us
  transfers between devices with their start and end apart: 38, of which 10 were waited for; matrix products, arithmetic and copies ran while one was open for 22% of the time, Pallas kernels for 0%

profile of v4, /device:TPU:0, one launch (start us, length us, event | category | flops | bytes accessed | tf_op | source)
XLA Modules:
  0.0 350.8 jit_solution(9724777229873237080)
XLA Ops:
  5.1 7.5 %collective-permute-start.10 = (bf16[9,160,640]{2,1,0:T(8,128)(2,1)S(1)}, bf16[9,160,640]{2,1,0:T(8,128)(2,1)}, u32[]{:S(2)}, u32[]{:S(2)}) collective-permute-start(bf16[9,160,640]{2,1,0:T(8,128)(2,1)S(1)} %get-tuple-element.223), channel_id=1, source_target_pairs={{0,4},{4,8},{9,13},{2,6},{6,10},{11,15},{16,20},{20,24},{25,29},{1... | collective-permute-start | bytes 5529608 | tf_op jit(solution)/shard_map/ppermute | solution.py:157
  14.7 17.4 %collective-permute-done.1 = f32[2,16]{1,0:T(2,128)S(1)} collective-permute-done((f32[2,16]{1,0:T(2,128)S(1)}, f32[2,16]{1,0:T(2,128)S(1)}, u32[]{:S(2)}, u32[]{:S(2)}) %collective-permute-start.1) | collective-permute-done | bytes 160 | tf_op jit(solution)/shard_map/ppermute | solution.py:39
  32.2 4.5 %collective-permute-done.2 = f32[2,16]{1,0:T(2,128)S(1)} collective-permute-done((f32[2,16]{1,0:T(2,128)S(1)}, f32[2,16]{1,0:T(2,128)S(1)}, u32[]{:S(2)}, u32[]{:S(2)}) %collective-permute-start.2) | collective-permute-done | bytes 160 | tf_op jit(solution)/shard_map/ppermute | solution.py:39
  47.3 6.3 %collective-permute-start.30 = (bf16[9,160,640]{2,1,0:T(8,128)(2,1)}, bf16[9,160,640]{2,1,0:T(8,128)(2,1)}, u32[]{:S(2)}, u32[]{:S(2)}) collective-permute-start(bf16[9,160,640]{2,1,0:T(8,128)(2,1)} %get-tuple-element.225), channel_id=1, source_target_pairs={{0,4},{4,8},{9,13},{2,6},{6,10},{11,15},{16,20},{20,24},{25,29},{1... | collective-permute-start | bytes 5529608 | tf_op jit(solution)/shard_map/ppermute | solution.py:157
  53.6 4.5 %collective-permute-start.5 = (bf16[9,160,640]{2,1,0:T(8,128)(2,1)}, bf16[9,160,640]{2,1,0:T(8,128)(2,1)}, u32[]{:S(2)}, u32[]{:S(2)}) collective-permute-start(bf16[9,160,640]{2,1,0:T(8,128)(2,1)} %collective-permute-done.4), channel_id=1, source_target_pairs={{0,16},{5,21},{9,25},{16,0},{21,5},{25,9},{2,18},{7,23},{11,27},{1... | collective-permute-start | bytes 5529608 | tf_op jit(solution)/shard_map/ppermute | solution.py:164
  64.9 8.6 %collective-permute-done.30 = bf16[9,160,640]{2,1,0:T(8,128)(2,1)} collective-permute-done((bf16[9,160,640]{2,1,0:T(8,128)(2,1)}, bf16[9,160,640]{2,1,0:T(8,128)(2,1)}, u32[]{:S(2)}, u32[]{:S(2)}) %collective-permute-start.30) | collective-permute-done | bytes 1843232 | tf_op jit(solution)/shard_map/ppermute | solution.py:157
  74.8 12.2 %collective-permute-done.5 = bf16[9,160,640]{2,1,0:T(8,128)(2,1)} collective-permute-done((bf16[9,160,640]{2,1,0:T(8,128)(2,1)}, bf16[9,160,640]{2,1,0:T(8,128)(2,1)}, u32[]{:S(2)}, u32[]{:S(2)}) %collective-permute-start.5) | collective-permute-done | bytes 1843232 | tf_op jit(solution)/shard_map/ppermute | solution.py:164
  96.6 4.0 %fusion.9 = bf16[640,8,1,258]{3,0,1,2:T(8,128)(2,1)} fusion(bf16[640,8,128]{2,0,1:T(8,128)(2,1)S(1)} %get-tuple-element.229, bf16[640,8,128]{2,0,1:T(8,128)(2,1)S(1)} %get-tuple-element.228), kind=kLoop, calls=%fused_computation.32 | loop fusion | flops 11888640 | bytes 5263360 | tf_op jit(solution)/shard_map/broadcast_in_dim | solution.py:200
  100.6 5.9 %copy.94 = bf16[640,8,1,258]{0,1,3,2:T(8,128)(2,1)} copy(bf16[640,8,1,258]{3,0,1,2:T(8,128)(2,1)} %fusion.9) | data formatting | bytes 5283840
  113.5 6.5 %conditional.2 = (bf16[3,3,640,640]{3,2,1,0:T(8,128)(2,1)}) conditional(s32[]{:T(128)} %clamp.4, (bf16[9,160,640]{2,1,0:T(8,128)(2,1)S(1)}, bf16[9,160,640]{2,1,0:T(8,128)(2,1)S(1)}, bf16[9,160,640]{2,1,0:T(8,128)(2,1)}, bf16[9,160,640]{2,1,0:T(8,128)(2,1)}) %tuple.113, (bf16[9,160,640]{2,1,0:T(8,128)(2,1)}, ...), branch_computations={%region_4.0_spmd, %region_5.0_spmd, %region_6.0_spmd, %region_7.0_... | conditional | flops 29491200 | bytes 14745608 | solution.py:186
  113.5 6.5 %pad_maximum_fusion = bf16[9,640,640]{2,1,0:T(8,128)(2,1)} fusion(bf16[9,160,640]{2,1,0:T(8,128)(2,1)} %get-tuple-element.144, bf16[9,160,640]{2,1,0:T(8,128)(2,1)} %get-tuple-element.143, bf16[9,160,640]{2,1,0:T(8,128)(2,1)S(1)} %get-tuple-element.142, bf16[9,160,640]{2,1,0:T(8,128)(2,1)S(1)} %get-tuple-element.141), kind=kLoop, calls=%fused_computation | loop fusion | flops 29491200 | bytes 14745600 | tf_op jit(solution)/shard_map/cond/branch_0_fun/concatenate | solution.py:181
  120.0 18.2 %broadcast_select_fusion.1 = bf16[6,8,33,640]{3,1,2,0:T(8,128)(2,1)S(1)} fusion(pred[8,33]{0,1:T(8,128)(4,1)S(1)} %copy-done.21, bf16[3,3,640,640]{3,2,1,0:T(8,128)(2,1)} %get-tuple-element.240, bf16[640,8,1,7,2]{0,3,4,1,2:T(8,128)(2,1)} %slice.38, bf16[640,8,1,8,33]{0,3,4,1,2:T(8,128)(2,1)} %copy-done.10), kind=kOutput, calls=%fused_computation.54 | convolution fusion | flops 11688130560 | bytes 12247304 | tf_op jit(solution)/shard_map/conv_general_dilated | solution.py:199
  140.1 4.1 %reshape.110 = bf16[6,1,264,640]{3,2,0,1:T(8,128)(2,1)} reshape(bf16[6,8,33,640]{3,2,1,0:T(8,128)(2,1)} %copy.87) | data formatting | bytes 4055040 | tf_op jit(solution)/shard_map/conv_general_dilated | solution.py:199
  158.5 7.3 %collective-permute-start.17 = (bf16[640,6,128]{2,0,1:T(8,128)(2,1)}, bf16[640,6,128]{2,0,1:T(8,128)(2,1)}, u32[]{:S(2)}, u32[]{:S(2)}) collective-permute-start(bf16[640,6,128]{2,0,1:T(8,128)(2,1)} %get-tuple-element.233), channel_id=1, source_target_pairs={{0,1},{3,2},{1,3},{2,0},{4,5},{7,6},{5,7},{6,4},{8,9},{11,10},{9,1... | collective-permute-start | bytes 2949128 | tf_op jit(solution)/shard_map/ppermute | solution.py:217
  172.6 17.7 %collective-permute-done.17 = bf16[640,6,128]{2,0,1:T(8,128)(2,1)} collective-permute-done((bf16[640,6,128]{2,0,1:T(8,128)(2,1)}, bf16[640,6,128]{2,0,1:T(8,128)(2,1)}, u32[]{:S(2)}, u32[]{:S(2)}) %collective-permute-start.17) | collective-permute-done | bytes 983072 | tf_op jit(solution)/shard_map/ppermute | solution.py:217
  195.1 7.9 %collective-permute-start.19 = (f32[2,16]{1,0:T(2,128)S(1)}, f32[2,16]{1,0:T(2,128)S(1)}, u32[]{:S(2)}, u32[]{:S(2)}) collective-permute-start(f32[2,16]{1,0:T(2,128)S(1)} %fusion.65), channel_id=1, source_target_pairs={{0,4},{4,0},{8,12},{12,8},{1,5},{5,1},{9,13},{13,9},{2,6},{6,2},{1... | collective-permute-start | bytes 392 | tf_op jit(solution)/shard_map/ppermute | solution.py:39
  206.4 6.4 %collective-permute-start.20 = (f32[2,16]{1,0:T(2,128)S(1)}, f32[2,16]{1,0:T(2,128)S(1)}, u32[]{:S(2)}, u32[]{:S(2)}) collective-permute-start(f32[2,16]{1,0:T(2,128)S(1)} %fusion.72), channel_id=1, source_target_pairs={{0,8},{4,12},{8,0},{12,4},{1,9},{5,13},{9,1},{13,5},{2,10},{6,14},... | collective-permute-start | bytes 392 | tf_op jit(solution)/shard_map/ppermute | solution.py:39
  231.5 7.4 %conditional.3 = (bf16[3,3,640,640]{3,2,1,0:T(8,128)(2,1)}) conditional(s32[]{:T(128)} %clamp.4, (bf16[9,160,640]{2,1,0:T(8,128)(2,1)}, bf16[9,160,640]{2,1,0:T(8,128)(2,1)S(1)}, bf16[9,160,640]{2,1,0:T(8,128)(2,1)}, bf16[9,160,640]{2,1,0:T(8,128)(2,1)}) %tuple.75, (bf16[9,160,640]{2,1,0:T(8,128)(2,1)}, ...), branch_computations={%region_16.0_spmd, %region_17.0_spmd, %region_18.19_spmd, %region_... | conditional | flops 29491200 | bytes 14745608 | solution.py:186
  231.5 7.4 %pad_maximum_fusion.8 = bf16[9,640,640]{2,1,0:T(8,128)(2,1)} fusion(bf16[9,160,640]{2,1,0:T(8,128)(2,1)} %get-tuple-element.188, bf16[9,160,640]{2,1,0:T(8,128)(2,1)} %get-tuple-element.187, bf16[9,160,640]{2,1,0:T(8,128)(2,1)S(1)} %get-tuple-element.186, bf16[9,160,640]{2,1,0:T(8,128)(2,1)} %get-tuple-element.185), kind=kLoop, calls=%fused_computation.8 | loop fusion | flops 29491200 | bytes 14745600 | tf_op jit(solution)/shard_map/cond/branch_0_fun/concatenate | solution.py:181
  244.4 5.9 %copy.95 = bf16[640,8,1,258]{0,1,3,2:T(8,128)(2,1)} copy(bf16[640,8,1,258]{3,0,1,2:T(8,128)(2,1)} %fusion.5) | data formatting | bytes 5283840
  252.6 17.4 %broadcast_select_fusion = bf16[6,8,33,640]{3,1,2,0:T(8,128)(2,1)S(1)} fusion(pred[8,33]{0,1:T(8,128)(4,1)S(1)} %copy-done.21, bf16[3,3,640,640]{3,2,1,0:T(8,128)(2,1)} %get-tuple-element.241, bf16[640,8,1,7,2]{0,3,4,1,2:T(8,128)(2,1)S(1)} %slice.42, bf16[640,8,1,8,33]{0,3,4,1,2:T(8,128)(2,1)S(1)} %copy.91), kind=kOutput, calls=%fused_computation.53 | convolution fusion | flops 11688130560 | bytes 12247304 | tf_op jit(solution)/shard_map/conv_general_dilated | solution.py:199
  271.9 4.1 %reshape.117 = bf16[6,1,264,640]{3,2,0,1:T(8,128)(2,1)} reshape(bf16[6,8,33,640]{3,2,1,0:T(8,128)(2,1)} %copy.92) | data formatting | bytes 4055040 | tf_op jit(solution)/shard_map/conv_general_dilated | solution.py:199
  287.1 38.0 %collective-permute-start.37 = (bf16[640,6,128]{2,0,1:T(8,128)(2,1)S(1)}, bf16[640,6,128]{2,0,1:T(8,128)(2,1)S(1)}, u32[]{:S(2)}, u32[]{:S(2)}) collective-permute-start(bf16[640,6,128]{2,0,1:T(8,128)(2,1)S(1)} %get-tuple-element.231), channel_id=1, source_target_pairs={{0,1},{3,2},{1,3},{2,0},{4,5},{7,6},{5,7},{6,4},{8,9},{11,10},{9,1... | collective-permute-start | bytes 2949128 | tf_op jit(solution)/shard_map/ppermute | solution.py:217
  325.1 24.2 %collective-permute-done.37 = bf16[640,6,128]{2,0,1:T(8,128)(2,1)S(1)} collective-permute-done((bf16[640,6,128]{2,0,1:T(8,128)(2,1)S(1)}, bf16[640,6,128]{2,0,1:T(8,128)(2,1)S(1)}, u32[]{:S(2)}, u32[]{:S(2)}) %collective-permute-start.37) | collective-permute-done | bytes 983072 | tf_op jit(solution)/shard_map/ppermute | solution.py:217
  (170 shorter events, 113.7 us)
Async XLA Ops:
  3.8 34.9 %collective-permute-start.4 = (bf16[9,160,640]{2,1,0:T(8,128)(2,1)S(1)}, bf16[9,160,640]{2,1,0:T(8,128)(2,1)}, u32[]{:S(2)}, u32[]{:S(2)}) collective-permute-start(bf16[9,160,640]{2,1,0:T(8,128)(2,1)S(1)} %get-tuple-element.223), channel_id=1, source_target_pairs={{4,0},{9,5},{13,9},{6,2},{11,7},{15,11},{20,16},{25,21},{29,25},{2... | collective-permute-start | bytes 5529608 | tf_op jit(solution)/shard_map/ppermute | solution.py:157
  5.1 35.5 %collective-permute-start.10 = (bf16[9,160,640]{2,1,0:T(8,128)(2,1)S(1)}, bf16[9,160,640]{2,1,0:T(8,128)(2,1)}, u32[]{:S(2)}, u32[]{:S(2)}) collective-permute-start(bf16[9,160,640]{2,1,0:T(8,128)(2,1)S(1)} %get-tuple-element.223), channel_id=1, source_target_pairs={{0,4},{4,8},{9,13},{2,6},{6,10},{11,15},{16,20},{20,24},{25,29},{1... | collective-permute-start | bytes 5529608 | tf_op jit(solution)/shard_map/ppermute | solution.py:157
  14.6 17.5 %collective-permute-start.1 = (f32[2,16]{1,0:T(2,128)S(1)}, f32[2,16]{1,0:T(2,128)S(1)}, u32[]{:S(2)}, u32[]{:S(2)}) collective-permute-start(f32[2,16]{1,0:T(2,128)S(1)} %fusion.66), channel_id=1, source_target_pairs={{0,4},{4,0},{8,12},{12,8},{1,5},{5,1},{9,13},{13,9},{2,6},{6,2},{1... | collective-permute-start | bytes 392 | tf_op jit(solution)/shard_map/ppermute | solution.py:39
  38.7 22.4 %collective-permute-start.6 = (bf16[9,160,640]{2,1,0:T(8,128)(2,1)}, bf16[9,160,640]{2,1,0:T(8,128)(2,1)}, u32[]{:S(2)}, u32[]{:S(2)}) collective-permute-start(bf16[9,160,640]{2,1,0:T(8,128)(2,1)} %collective-permute-done.4), channel_id=1, source_target_pairs={{5,1},{9,5},{7,3},{11,7},{21,17},{25,21},{23,19},{27,23}} | collective-permute-start | bytes 5529608 | tf_op jit(solution)/shard_map/ppermute | solution.py:157
  40.6 22.4 %collective-permute-start.12 = (bf16[9,160,640]{2,1,0:T(8,128)(2,1)}, bf16[9,160,640]{2,1,0:T(8,128)(2,1)}, u32[]{:S(2)}, u32[]{:S(2)}) collective-permute-start(bf16[9,160,640]{2,1,0:T(8,128)(2,1)} %collective-permute-done.10), channel_id=1, source_target_pairs={{4,8},{8,12},{6,10},{10,14},{20,24},{24,28},{22,26},{26,30}} | collective-permute-start | bytes 5529608 | tf_op jit(solution)/shard_map/ppermute | solution.py:157
  47.3 26.2 %collective-permute-start.30 = (bf16[9,160,640]{2,1,0:T(8,128)(2,1)}, bf16[9,160,640]{2,1,0:T(8,128)(2,1)}, u32[]{:S(2)}, u32[]{:S(2)}) collective-permute-start(bf16[9,160,640]{2,1,0:T(8,128)(2,1)} %get-tuple-element.225), channel_id=1, source_target_pairs={{0,4},{4,8},{9,13},{2,6},{6,10},{11,15},{16,20},{20,24},{25,29},{1... | collective-permute-start | bytes 5529608 | tf_op jit(solution)/shard_map/ppermute | solution.py:157
  53.6 33.4 %collective-permute-start.5 = (bf16[9,160,640]{2,1,0:T(8,128)(2,1)}, bf16[9,160,640]{2,1,0:T(8,128)(2,1)}, u32[]{:S(2)}, u32[]{:S(2)}) collective-permute-start(bf16[9,160,640]{2,1,0:T(8,128)(2,1)} %collective-permute-done.4), channel_id=1, source_target_pairs={{0,16},{5,21},{9,25},{16,0},{21,5},{25,9},{2,18},{7,23},{11,27},{1... | collective-permute-start | bytes 5529608 | tf_op jit(solution)/shard_map/ppermute | solution.py:164
  59.2 29.7 %collective-permute-start.11 = (bf16[9,160,640]{2,1,0:T(8,128)(2,1)}, bf16[9,160,640]{2,1,0:T(8,128)(2,1)}, u32[]{:S(2)}, u32[]{:S(2)}) collective-permute-start(bf16[9,160,640]{2,1,0:T(8,128)(2,1)} %collective-permute-done.10), channel_id=1, source_target_pairs={{4,20},{8,24},{13,29},{20,4},{24,8},{29,13},{6,22},{10,26},{15,31}... | collective-permute-start | bytes 5529608 | tf_op jit(solution)/shard_map/ppermute | solution.py:164
  61.1 29.9 %collective-permute-start.8 = (bf16[9,160,640]{2,1,0:T(8,128)(2,1)}, bf16[9,160,640]{2,1,0:T(8,128)(2,1)}, u32[]{:S(2)}, u32[]{:S(2)}) collective-permute-start(bf16[9,160,640]{2,1,0:T(8,128)(2,1)} %collective-permute-done.6), channel_id=1, source_target_pairs={{5,1},{7,3},{21,17},{23,19}} | collective-permute-start | bytes 5529608 | tf_op jit(solution)/shard_map/ppermute | solution.py:157
  63.0 29.8 %collective-permute-start.14 = (bf16[9,160,640]{2,1,0:T(8,128)(2,1)}, bf16[9,160,640]{2,1,0:T(8,128)(2,1)}, u32[]{:S(2)}, u32[]{:S(2)}) collective-permute-start(bf16[9,160,640]{2,1,0:T(8,128)(2,1)} %collective-permute-done.12), channel_id=1, source_target_pairs={{8,12},{10,14},{24,28},{26,30}} | collective-permute-start | bytes 5529608 | tf_op jit(solution)/shard_map/ppermute | solution.py:157
  73.5 36.0 %collective-permute-start.24 = (bf16[9,160,640]{2,1,0:T(8,128)(2,1)}, bf16[9,160,640]{2,1,0:T(8,128)(2,1)}, u32[]{:S(2)}, u32[]{:S(2)}) collective-permute-start(bf16[9,160,640]{2,1,0:T(8,128)(2,1)} %get-tuple-element.225), channel_id=1, source_target_pairs={{4,0},{9,5},{13,9},{6,2},{11,7},{15,11},{20,16},{25,21},{29,25},{2... | collective-permute-start | bytes 5529608 | tf_op jit(solution)/shard_map/ppermute | solution.py:157
  87.0 24.6 %collective-permute-start.7 = (bf16[9,160,640]{2,1,0:T(8,128)(2,1)}, bf16[9,160,640]{2,1,0:T(8,128)(2,1)}, u32[]{:S(2)}, u32[]{:S(2)}) collective-permute-start(bf16[9,160,640]{2,1,0:T(8,128)(2,1)} %collective-permute-done.6), channel_id=1, source_target_pairs={{1,17},{5,21},{17,1},{21,5},{3,19},{7,23},{19,3},{23,7}} | collective-permute-start | bytes 5529608 | tf_op jit(solution)/shard_map/ppermute | solution.py:164
  88.9 24.5 %collective-permute-start.13 = (bf16[9,160,640]{2,1,0:T(8,128)(2,1)}, bf16[9,160,640]{2,1,0:T(8,128)(2,1)}, u32[]{:S(2)}, u32[]{:S(2)}) collective-permute-start(bf16[9,160,640]{2,1,0:T(8,128)(2,1)} %collective-permute-done.12), channel_id=1, source_target_pairs={{8,24},{12,28},{24,8},{28,12},{10,26},{14,30},{26,10},{30,14}} | collective-permute-start | bytes 5529608 | tf_op jit(solution)/shard_map/ppermute | solution.py:164
  90.9 22.5 %collective-permute-start.9 = (bf16[9,160,640]{2,1,0:T(8,128)(2,1)}, bf16[9,160,640]{2,1,0:T(8,128)(2,1)}, u32[]{:S(2)}, u32[]{:S(2)}) collective-permute-start(bf16[9,160,640]{2,1,0:T(8,128)(2,1)} %collective-permute-done.8), channel_id=1, source_target_pairs={{1,17},{17,1},{3,19},{19,3}} | collective-permute-start | bytes 5529608 | tf_op jit(solution)/shard_map/ppermute | solution.py:164
  92.8 20.6 %collective-permute-start.15 = (bf16[9,160,640]{2,1,0:T(8,128)(2,1)}, bf16[9,160,640]{2,1,0:T(8,128)(2,1)}, u32[]{:S(2)}, u32[]{:S(2)}) collective-permute-start(bf16[9,160,640]{2,1,0:T(8,128)(2,1)} %collective-permute-done.14), channel_id=1, source_target_pairs={{12,28},{28,12},{14,30},{30,14}} | collective-permute-start | bytes 5529608 | tf_op jit(solution)/shard_map/ppermute | solution.py:164
  109.5 59.3 %collective-permute-start.32 = (bf16[9,160,640]{2,1,0:T(8,128)(2,1)}, bf16[9,160,640]{2,1,0:T(8,128)(2,1)}, u32[]{:S(2)}, u32[]{:S(2)}) collective-permute-start(bf16[9,160,640]{2,1,0:T(8,128)(2,1)} %collective-permute-done.30), channel_id=1, source_target_pairs={{4,8},{8,12},{6,10},{10,14},{20,24},{24,28},{22,26},{26,30}} | collective-permute-start | bytes 5529608 | tf_op jit(solution)/shard_map/ppermute | solution.py:157
  111.5 59.2 %collective-permute-start.26 = (bf16[9,160,640]{2,1,0:T(8,128)(2,1)}, bf16[9,160,640]{2,1,0:T(8,128)(2,1)}, u32[]{:S(2)}, u32[]{:S(2)}) collective-permute-start(bf16[9,160,640]{2,1,0:T(8,128)(2,1)} %collective-permute-done.24), channel_id=1, source_target_pairs={{5,1},{9,5},{7,3},{11,7},{21,17},{25,21},{23,19},{27,23}} | collective-permute-start | bytes 5529608 | tf_op jit(solution)/shard_map/ppermute | solution.py:157
  158.5 31.8 %collective-permute-start.17 = (bf16[640,6,128]{2,0,1:T(8,128)(2,1)}, bf16[640,6,128]{2,0,1:T(8,128)(2,1)}, u32[]{:S(2)}, u32[]{:S(2)}) collective-permute-start(bf16[640,6,128]{2,0,1:T(8,128)(2,1)} %get-tuple-element.233), channel_id=1, source_target_pairs={{0,1},{3,2},{1,3},{2,0},{4,5},{7,6},{5,7},{6,4},{8,9},{11,10},{9,1... | collective-permute-start | bytes 2949128 | tf_op jit(solution)/shard_map/ppermute | solution.py:217
  166.9 53.5 %collective-permute-start.31 = (bf16[9,160,640]{2,1,0:T(8,128)(2,1)}, bf16[9,160,640]{2,1,0:T(8,128)(2,1)}, u32[]{:S(2)}, u32[]{:S(2)}) collective-permute-start(bf16[9,160,640]{2,1,0:T(8,128)(2,1)} %collective-permute-done.30), channel_id=1, source_target_pairs={{4,20},{8,24},{13,29},{20,4},{24,8},{29,13},{6,22},{10,26},{15,31}... | collective-permute-start | bytes 5529608 | tf_op jit(solution)/shard_map/ppermute | solution.py:164
  168.8 52.9 %collective-permute-start.34 = (bf16[9,160,640]{2,1,0:T(8,128)(2,1)}, bf16[9,160,640]{2,1,0:T(8,128)(2,1)}, u32[]{:S(2)}, u32[]{:S(2)}) collective-permute-start(bf16[9,160,640]{2,1,0:T(8,128)(2,1)} %collective-permute-done.32), channel_id=1, source_target_pairs={{8,12},{10,14},{24,28},{26,30}} | collective-permute-start | bytes 5529608 | tf_op jit(solution)/shard_map/ppermute | solution.py:157
  170.7 52.9 %collective-permute-start.28 = (bf16[9,160,640]{2,1,0:T(8,128)(2,1)}, bf16[9,160,640]{2,1,0:T(8,128)(2,1)}, u32[]{:S(2)}, u32[]{:S(2)}) collective-permute-start(bf16[9,160,640]{2,1,0:T(8,128)(2,1)} %collective-permute-done.26), channel_id=1, source_target_pairs={{5,1},{7,3},{21,17},{23,19}} | collective-permute-start | bytes 5529608 | tf_op jit(solution)/shard_map/ppermute | solution.py:157
  202.9 28.5 %collective-permute-start.25 = (bf16[9,160,640]{2,1,0:T(8,128)(2,1)}, bf16[9,160,640]{2,1,0:T(8,128)(2,1)}, u32[]{:S(2)}, u32[]{:S(2)}) collective-permute-start(bf16[9,160,640]{2,1,0:T(8,128)(2,1)} %collective-permute-done.24), channel_id=1, source_target_pairs={{0,16},{5,21},{9,25},{16,0},{21,5},{25,9},{2,18},{7,23},{11,27},{1... | collective-permute-start | bytes 5529608 | tf_op jit(solution)/shard_map/ppermute | solution.py:164
  286.2 38.9 %collective-permute-start.36 = (bf16[640,6,128]{2,0,1:T(8,128)(2,1)S(1)}, bf16[640,6,128]{2,0,1:T(8,128)(2,1)S(1)}, u32[]{:S(2)}, u32[]{:S(2)}) collective-permute-start(bf16[640,6,128]{2,0,1:T(8,128)(2,1)S(1)} %get-tuple-element.230), channel_id=1, source_target_pairs={{1,2},{2,1},{5,6},{6,5},{9,10},{10,9},{13,14},{14,13},{17,18},{18,... | collective-permute-start | bytes 2949128 | tf_op jit(solution)/shard_map/ppermute | solution.py:218
  287.1 62.2 %collective-permute-start.37 = (bf16[640,6,128]{2,0,1:T(8,128)(2,1)S(1)}, bf16[640,6,128]{2,0,1:T(8,128)(2,1)S(1)}, u32[]{:S(2)}, u32[]{:S(2)}) collective-permute-start(bf16[640,6,128]{2,0,1:T(8,128)(2,1)S(1)} %get-tuple-element.231), channel_id=1, source_target_pairs={{0,1},{3,2},{1,3},{2,0},{4,5},{7,6},{5,7},{6,4},{8,9},{11,10},{9,1... | collective-permute-start | bytes 2949128 | tf_op jit(solution)/shard_map/ppermute | solution.py:217
  (36 other events, 838.4 us)

commit v5 on v0

--- a/solution.py
+++ b/solution.py
@@ -191,7 +191,7 @@
     c = lax.axis_index("col")
     left = jnp.where(c == 0, block, other)
     right = jnp.where(c == 0, other, block)
-    return jnp.pad(jnp.concatenate([left, right], axis=2), ((0, 0), (0, 0), (1, 1)))
+    return jnp.concatenate([left, right], axis=2)
 
 
 def conv_full(padded, weight):
@@ -200,7 +200,7 @@
         padded[None],
         kernel,
         window_strides=(1, 1),
-        padding="VALID",
+        padding=((0, 0), (1, 1)),
         dimension_numbers=("NCHW", "HWOI", "NCHW"),
         preferred_element_type=jnp.float32,
     )[0]

time: 339 us -> 332 us (0.979)
  other arithmetic: 39.2 us -> 33.3 us
  local copies, waits for them, and re-layouts: 54.1 us -> 50.7 us
    broadcast_in_dim x2, other arithmetic: 7.91 us -> 2.08 us  [conv_full(): padded[None]]
    unnamed x56 -> x52, local copies, waits for them, and re-layouts: 29.9 us -> 26.5 us
  transfers between devices with their start and end apart: 38 -> 38, of which waited for: 10 -> 11; matrix products, arithmetic and copies ran while one was open for 24% -> 24% of each run, Pallas kernels for 0% -> 0%
where the time goes in v5:
time: 332 us; the launch traced here: 330 us
  starting transfers between devices  125 us (38%)
  waiting for transfers between devices  82.9 us (25%)
  local copies, waits for them, and re-layouts  50.7 us (15%)
  matrix products  35.9 us (11%)
  other arithmetic  33.3 us (10%)
    ppermute x2, starting transfers between devices, reduce_cores(): lax.ppermute(send_a, ('chan', 'col'), [(0, 1), (3, 2), (1, 3), (2, 0)])  44 us
    conv_general_dilated x2, matrix products, conv_full(): lax.conv_general_dilated(padded[None], kernel, window_strides=(1, 1), pad...  35.6 us
    ppermute x2, waiting for transfers between devices, reduce_cores(): lax.ppermute(send_a, ('chan', 'col'), [(0, 1), (3, 2), (1, 3), (2, 0)])  33.8 us
    ppermute x12, starting transfers between devices, line_weights(): got = lax.ppermute(last[d], ('patch', 'col'), pairs)  31.7 us
    ppermute x12, starting transfers between devices, line_weights(): bufs[t, d, 'o'] = lax.ppermute(got, ('groups', 'patch', 'col'), trade)  27.1 us
    unnamed x52, local copies, waits for them, and re-layouts  26.5 us
    ppermute x4, waiting for transfers between devices, group_moments(): lax.ppermute(summed, 'patch', [(i, i ^ step) for i in range(n_p)])  23.4 us
    ppermute x4, starting transfers between devices, group_moments(): lax.ppermute(summed, 'patch', [(i, i ^ step) for i in range(n_p)])  14.3 us
  transfers between devices with their start and end apart: 38, of which 11 were waited for; matrix products, arithmetic and copies ran while one was open for 24% of the time, Pallas kernels for 0%

profile of v5, /device:TPU:0, one launch (start us, length us, event | category | flops | bytes accessed | tf_op | source)
XLA Modules:
  0.0 329.8 jit_solution(8721194212849172358)
XLA Ops:
  0.0 3.8 %constant_dynamic-slice_fusion.8 = (bf16[9,160,640]{2,1,0:T(8,128)(2,1)}, bf16[9,160,640]{2,1,0:T(8,128)(2,1)S(1)}) fusion(bf16[9,320,640]{2,1,0:T(8,128)(2,1)} %bitcast.138, s32[]{:T(128)S(6)} %select_n.62, s32[]{:T(128)S(6)} %select_n.61), kind=kLoop, calls=%fused_computation.109 | loop fusion | bytes 7372808 | tf_op jit(solution)/shard_map/dynamic_slice | solution.py:144
  5.1 7.5 %collective-permute-start.10 = (bf16[9,160,640]{2,1,0:T(8,128)(2,1)S(1)}, bf16[9,160,640]{2,1,0:T(8,128)(2,1)}, u32[]{:S(2)}, u32[]{:S(2)}) collective-permute-start(bf16[9,160,640]{2,1,0:T(8,128)(2,1)S(1)} %get-tuple-element.431), channel_id=1, source_target_pairs={{0,4},{4,8},{9,13},{2,6},{6,10},{11,15},{16,20},{20,24},{25,29},{1... | collective-permute-start | bytes 5529608 | tf_op jit(solution)/shard_map/ppermute | solution.py:157
  14.7 17.4 %collective-permute-done.1 = f32[2,16]{1,0:T(2,128)S(1)} collective-permute-done((f32[2,16]{1,0:T(2,128)S(1)}, f32[2,16]{1,0:T(2,128)S(1)}, u32[]{:S(2)}, u32[]{:S(2)}) %collective-permute-start.1) | collective-permute-done | bytes 160 | tf_op jit(solution)/shard_map/ppermute | solution.py:39
  32.2 4.5 %collective-permute-done.2 = f32[2,16]{1,0:T(2,128)S(1)} collective-permute-done((f32[2,16]{1,0:T(2,128)S(1)}, f32[2,16]{1,0:T(2,128)S(1)}, u32[]{:S(2)}, u32[]{:S(2)}) %collective-permute-start.2) | collective-permute-done | bytes 160 | tf_op jit(solution)/shard_map/ppermute | solution.py:39
  47.3 6.3 %collective-permute-start.30 = (bf16[9,160,640]{2,1,0:T(8,128)(2,1)}, bf16[9,160,640]{2,1,0:T(8,128)(2,1)}, u32[]{:S(2)}, u32[]{:S(2)}) collective-permute-start(bf16[9,160,640]{2,1,0:T(8,128)(2,1)} %get-tuple-element.433), channel_id=1, source_target_pairs={{0,4},{4,8},{9,13},{2,6},{6,10},{11,15},{16,20},{20,24},{25,29},{1... | collective-permute-start | bytes 5529608 | tf_op jit(solution)/shard_map/ppermute | solution.py:157
  53.6 4.5 %collective-permute-start.5 = (bf16[9,160,640]{2,1,0:T(8,128)(2,1)}, bf16[9,160,640]{2,1,0:T(8,128)(2,1)}, u32[]{:S(2)}, u32[]{:S(2)}) collective-permute-start(bf16[9,160,640]{2,1,0:T(8,128)(2,1)} %collective-permute-done.4), channel_id=1, source_target_pairs={{0,16},{5,21},{9,25},{16,0},{21,5},{25,9},{2,18},{7,23},{11,27},{1... | collective-permute-start | bytes 5529608 | tf_op jit(solution)/shard_map/ppermute | solution.py:164
  65.0 8.5 %collective-permute-done.30 = bf16[9,160,640]{2,1,0:T(8,128)(2,1)} collective-permute-done((bf16[9,160,640]{2,1,0:T(8,128)(2,1)}, bf16[9,160,640]{2,1,0:T(8,128)(2,1)}, u32[]{:S(2)}, u32[]{:S(2)}) %collective-permute-start.30) | collective-permute-done | bytes 1843232 | tf_op jit(solution)/shard_map/ppermute | solution.py:157
  74.8 12.2 %collective-permute-done.5 = bf16[9,160,640]{2,1,0:T(8,128)(2,1)} collective-permute-done((bf16[9,160,640]{2,1,0:T(8,128)(2,1)}, bf16[9,160,640]{2,1,0:T(8,128)(2,1)}, u32[]{:S(2)}, u32[]{:S(2)}) %collective-permute-start.5) | collective-permute-done | bytes 1843232 | tf_op jit(solution)/shard_map/ppermute | solution.py:164
  98.3 4.9 %copy.86 = bf16[640,8,1,256]{0,1,3,2:T(8,128)(2,1)} copy(bf16[640,8,1,256]{3,0,1,2:T(8,128)(2,1)} %maximum_bitcast_fusion) | data formatting | bytes 5242880
  112.2 6.6 %conditional.2 = (bf16[3,3,640,640]{3,2,1,0:T(8,128)(2,1)}) conditional(s32[]{:T(128)} %clamp.4, (bf16[9,160,640]{2,1,0:T(8,128)(2,1)S(1)}, bf16[9,160,640]{2,1,0:T(8,128)(2,1)S(1)}, bf16[9,160,640]{2,1,0:T(8,128)(2,1)}, bf16[9,160,640]{2,1,0:T(8,128)(2,1)}) %tuple.211, (bf16[9,160,640]{2,1,0:T(8,128)(2,1)}, ...), branch_computations={%region_4.0_spmd, %region_5.0_spmd, %region_6.0_spmd, %region_7.0_... | conditional | flops 29491200 | bytes 14745608 | solution.py:186
  112.2 6.6 %pad_maximum_fusion = bf16[9,640,640]{2,1,0:T(8,128)(2,1)} fusion(bf16[9,160,640]{2,1,0:T(8,128)(2,1)} %get-tuple-element.273, bf16[9,160,640]{2,1,0:T(8,128)(2,1)} %get-tuple-element.272, bf16[9,160,640]{2,1,0:T(8,128)(2,1)S(1)} %get-tuple-element.271, bf16[9,160,640]{2,1,0:T(8,128)(2,1)S(1)} %get-tuple-element.270), kind=kLoop, calls=%fused_computation | loop fusion | flops 29491200 | bytes 14745600 | tf_op jit(solution)/shard_map/cond/branch_0_fun/concatenate | solution.py:181
  118.8 18.2 %select_convert_fusion.1 = bf16[6,8,33,640]{3,1,2,0:T(8,128)(2,1)S(1)} fusion(pred[8,33]{0,1:T(8,128)(4,1)S(1)} %copy-done.20, bf16[3,3,640,640]{3,2,1,0:T(8,128)(2,1)} %get-tuple-element.450, bf16[640,8,1,7,2]{0,3,4,1,2:T(8,128)(2,1)} %slice.38, bf16[640,8,1,8,33]{0,3,4,1,2:T(8,128)(2,1)} %copy-done.9), kind=kOutput, calls=%fused_computation.36 | convolution fusion | flops 11689144320 | bytes 12247304 | tf_op jit(solution)/shard_map/conv_general_dilated | solution.py:199
  138.8 4.1 %reshape.162 = bf16[6,1,264,640]{3,2,0,1:T(8,128)(2,1)} reshape(bf16[6,8,33,640]{3,2,1,0:T(8,128)(2,1)} %copy.71) | data formatting | bytes 4055040 | tf_op jit(solution)/shard_map/convert_element_type | solution.py:207
  152.5 8.7 %collective-permute-start.17 = (bf16[640,6,128]{2,0,1:T(8,128)(2,1)}, bf16[640,6,128]{2,0,1:T(8,128)(2,1)}, u32[]{:S(2)}, u32[]{:S(2)}) collective-permute-start(bf16[640,6,128]{2,0,1:T(8,128)(2,1)} %bitcast.141), channel_id=1, source_target_pairs={{0,1},{3,2},{1,3},{2,0},{4,5},{7,6},{5,7},{6,4},{8,9},{11,10},{9,1... | collective-permute-start | bytes 2949128 | tf_op jit(solution)/shard_map/ppermute | solution.py:215
  169.6 13.8 %collective-permute-done.17 = bf16[640,6,128]{2,0,1:T(8,128)(2,1)} collective-permute-done((bf16[640,6,128]{2,0,1:T(8,128)(2,1)}, bf16[640,6,128]{2,0,1:T(8,128)(2,1)}, u32[]{:S(2)}, u32[]{:S(2)}) %collective-permute-start.17) | collective-permute-done | bytes 983072 | tf_op jit(solution)/shard_map/ppermute | solution.py:215
  187.9 4.5 %collective-permute-start.19 = (f32[2,16]{1,0:T(2,128)S(1)}, f32[2,16]{1,0:T(2,128)S(1)}, u32[]{:S(2)}, u32[]{:S(2)}) collective-permute-start(f32[2,16]{1,0:T(2,128)S(1)} %fusion.57), channel_id=1, source_target_pairs={{0,4},{4,0},{8,12},{12,8},{1,5},{5,1},{9,13},{13,9},{2,6},{6,2},{1... | collective-permute-start | bytes 392 | tf_op jit(solution)/shard_map/ppermute | solution.py:39
  195.8 9.7 %collective-permute-start.20 = (f32[2,16]{1,0:T(2,128)S(1)}, f32[2,16]{1,0:T(2,128)S(1)}, u32[]{:S(2)}, u32[]{:S(2)}) collective-permute-start(f32[2,16]{1,0:T(2,128)S(1)} %fusion.64), channel_id=1, source_target_pairs={{0,8},{4,12},{8,0},{12,4},{1,9},{5,13},{9,1},{13,5},{2,10},{6,14},... | collective-permute-start | bytes 392 | tf_op jit(solution)/shard_map/ppermute | solution.py:39
  209.5 3.6 %collective-permute-start.21 = (bf16[640,1,128]{2,0,1:T(8,128)(2,1)S(1)}, bf16[640,1,128]{2,0,1:T(8,128)(2,1)S(1)}, u32[]{:S(2)}, u32[]{:S(2)}) collective-permute-start(bf16[640,1,128]{2,0,1:T(8,128)(2,1)S(1)} %get-tuple-element.444), channel_id=1, source_target_pairs={{0,4},{4,8},{8,12},{1,5},{5,9},{9,13},{2,6},{6,10},{10,14},{3,7},{... | collective-permute-start | bytes 491528 | tf_op jit(solution)/shard_map/ppermute | solution.py:21
  224.2 7.4 %conditional.3 = (bf16[3,3,640,640]{3,2,1,0:T(8,128)(2,1)}) conditional(s32[]{:T(128)} %clamp.4, (bf16[9,160,640]{2,1,0:T(8,128)(2,1)}, bf16[9,160,640]{2,1,0:T(8,128)(2,1)S(1)}, bf16[9,160,640]{2,1,0:T(8,128)(2,1)}, bf16[9,160,640]{2,1,0:T(8,128)(2,1)}) %tuple.145, (bf16[9,160,640]{2,1,0:T(8,128)(2,1)}, ...), branch_computations={%region_24.0_spmd, %region_25.0_spmd, %region_26.0_spmd, %region_2... | conditional | flops 29491200 | bytes 14745608 | solution.py:186
  224.2 7.4 %pad_maximum_fusion.16 = bf16[9,640,640]{2,1,0:T(8,128)(2,1)} fusion(bf16[9,160,640]{2,1,0:T(8,128)(2,1)} %get-tuple-element.364, bf16[9,160,640]{2,1,0:T(8,128)(2,1)} %get-tuple-element.363, bf16[9,160,640]{2,1,0:T(8,128)(2,1)S(1)} %get-tuple-element.362, bf16[9,160,640]{2,1,0:T(8,128)(2,1)} %get-tuple-element.361), kind=kLoop, calls=%fused_computation.16 | loop fusion | flops 29491200 | bytes 14745600 | tf_op jit(solution)/shard_map/cond/branch_0_fun/concatenate | solution.py:181
  233.5 3.5 %copy.87 = bf16[640,8,1,256]{0,1,3,2:T(8,128)(2,1)} copy(bf16[640,8,1,256]{3,0,1,2:T(8,128)(2,1)S(1)} %maximum_bitcast_fusion.1) | data formatting | bytes 5242880
  239.4 17.4 %select_convert_fusion = bf16[6,8,33,640]{3,1,2,0:T(8,128)(2,1)S(1)} fusion(pred[8,33]{0,1:T(8,128)(4,1)S(1)} %copy-done.20, bf16[3,3,640,640]{3,2,1,0:T(8,128)(2,1)} %get-tuple-element.451, bf16[640,8,1,7,2]{0,3,4,1,2:T(8,128)(2,1)S(1)} %slice.42, bf16[640,8,1,8,33]{0,3,4,1,2:T(8,128)(2,1)S(1)} %copy.75), kind=kOutput, calls=%fused_computation.35 | convolution fusion | flops 11689144320 | bytes 12247304 | tf_op jit(solution)/shard_map/conv_general_dilated | solution.py:199
  269.1 35.4 %collective-permute-start.37 = (bf16[640,6,128]{2,0,1:T(8,128)(2,1)}, bf16[640,6,128]{2,0,1:T(8,128)(2,1)}, u32[]{:S(2)}, u32[]{:S(2)}) collective-permute-start(bf16[640,6,128]{2,0,1:T(8,128)(2,1)} %bitcast.143), channel_id=1, source_target_pairs={{0,1},{3,2},{1,3},{2,0},{4,5},{7,6},{5,7},{6,4},{8,9},{11,10},{9,1... | collective-permute-start | bytes 2949128 | tf_op jit(solution)/shard_map/ppermute | solution.py:215
  306.7 20.0 %collective-permute-done.37 = bf16[640,6,128]{2,0,1:T(8,128)(2,1)} collective-permute-done((bf16[640,6,128]{2,0,1:T(8,128)(2,1)}, bf16[640,6,128]{2,0,1:T(8,128)(2,1)}, u32[]{:S(2)}, u32[]{:S(2)}) %collective-permute-start.37) | collective-permute-done | bytes 983072 | tf_op jit(solution)/shard_map/ppermute | solution.py:215
  (170 shorter events, 106.0 us)
Async XLA Ops:
  3.8 34.9 %collective-permute-start.4 = (bf16[9,160,640]{2,1,0:T(8,128)(2,1)S(1)}, bf16[9,160,640]{2,1,0:T(8,128)(2,1)}, u32[]{:S(2)}, u32[]{:S(2)}) collective-permute-start(bf16[9,160,640]{2,1,0:T(8,128)(2,1)S(1)} %get-tuple-element.431), channel_id=1, source_target_pairs={{4,0},{9,5},{13,9},{6,2},{11,7},{15,11},{20,16},{25,21},{29,25},{2... | collective-permute-start | bytes 5529608 | tf_op jit(solution)/shard_map/ppermute | solution.py:157
  5.1 35.6 %collective-permute-start.10 = (bf16[9,160,640]{2,1,0:T(8,128)(2,1)S(1)}, bf16[9,160,640]{2,1,0:T(8,128)(2,1)}, u32[]{:S(2)}, u32[]{:S(2)}) collective-permute-start(bf16[9,160,640]{2,1,0:T(8,128)(2,1)S(1)} %get-tuple-element.431), channel_id=1, source_target_pairs={{0,4},{4,8},{9,13},{2,6},{6,10},{11,15},{16,20},{20,24},{25,29},{1... | collective-permute-start | bytes 5529608 | tf_op jit(solution)/shard_map/ppermute | solution.py:157
  38.7 22.4 %collective-permute-start.6 = (bf16[9,160,640]{2,1,0:T(8,128)(2,1)}, bf16[9,160,640]{2,1,0:T(8,128)(2,1)}, u32[]{:S(2)}, u32[]{:S(2)}) collective-permute-start(bf16[9,160,640]{2,1,0:T(8,128)(2,1)} %collective-permute-done.4), channel_id=1, source_target_pairs={{5,1},{9,5},{7,3},{11,7},{21,17},{25,21},{23,19},{27,23}} | collective-permute-start | bytes 5529608 | tf_op jit(solution)/shard_map/ppermute | solution.py:157
  40.6 22.5 %collective-permute-start.12 = (bf16[9,160,640]{2,1,0:T(8,128)(2,1)}, bf16[9,160,640]{2,1,0:T(8,128)(2,1)}, u32[]{:S(2)}, u32[]{:S(2)}) collective-permute-start(bf16[9,160,640]{2,1,0:T(8,128)(2,1)} %collective-permute-done.10), channel_id=1, source_target_pairs={{4,8},{8,12},{6,10},{10,14},{20,24},{24,28},{22,26},{26,30}} | collective-permute-start | bytes 5529608 | tf_op jit(solution)/shard_map/ppermute | solution.py:157
  47.3 26.2 %collective-permute-start.30 = (bf16[9,160,640]{2,1,0:T(8,128)(2,1)}, bf16[9,160,640]{2,1,0:T(8,128)(2,1)}, u32[]{:S(2)}, u32[]{:S(2)}) collective-permute-start(bf16[9,160,640]{2,1,0:T(8,128)(2,1)} %get-tuple-element.433), channel_id=1, source_target_pairs={{0,4},{4,8},{9,13},{2,6},{6,10},{11,15},{16,20},{20,24},{25,29},{1... | collective-permute-start | bytes 5529608 | tf_op jit(solution)/shard_map/ppermute | solution.py:157
  53.6 33.4 %collective-permute-start.5 = (bf16[9,160,640]{2,1,0:T(8,128)(2,1)}, bf16[9,160,640]{2,1,0:T(8,128)(2,1)}, u32[]{:S(2)}, u32[]{:S(2)}) collective-permute-start(bf16[9,160,640]{2,1,0:T(8,128)(2,1)} %collective-permute-done.4), channel_id=1, source_target_pairs={{0,16},{5,21},{9,25},{16,0},{21,5},{25,9},{2,18},{7,23},{11,27},{1... | collective-permute-start | bytes 5529608 | tf_op jit(solution)/shard_map/ppermute | solution.py:164
  59.2 29.7 %collective-permute-start.11 = (bf16[9,160,640]{2,1,0:T(8,128)(2,1)}, bf16[9,160,640]{2,1,0:T(8,128)(2,1)}, u32[]{:S(2)}, u32[]{:S(2)}) collective-permute-start(bf16[9,160,640]{2,1,0:T(8,128)(2,1)} %collective-permute-done.10), channel_id=1, source_target_pairs={{4,20},{8,24},{13,29},{20,4},{24,8},{29,13},{6,22},{10,26},{15,31}... | collective-permute-start | bytes 5529608 | tf_op jit(solution)/shard_map/ppermute | solution.py:164
  61.2 29.8 %collective-permute-start.8 = (bf16[9,160,640]{2,1,0:T(8,128)(2,1)}, bf16[9,160,640]{2,1,0:T(8,128)(2,1)}, u32[]{:S(2)}, u32[]{:S(2)}) collective-permute-start(bf16[9,160,640]{2,1,0:T(8,128)(2,1)} %collective-permute-done.6), channel_id=1, source_target_pairs={{5,1},{7,3},{21,17},{23,19}} | collective-permute-start | bytes 5529608 | tf_op jit(solution)/shard_map/ppermute | solution.py:157
  63.1 29.7 %collective-permute-start.14 = (bf16[9,160,640]{2,1,0:T(8,128)(2,1)}, bf16[9,160,640]{2,1,0:T(8,128)(2,1)}, u32[]{:S(2)}, u32[]{:S(2)}) collective-permute-start(bf16[9,160,640]{2,1,0:T(8,128)(2,1)} %collective-permute-done.12), channel_id=1, source_target_pairs={{8,12},{10,14},{24,28},{26,30}} | collective-permute-start | bytes 5529608 | tf_op jit(solution)/shard_map/ppermute | solution.py:157
  73.5 34.7 %collective-permute-start.24 = (bf16[9,160,640]{2,1,0:T(8,128)(2,1)}, bf16[9,160,640]{2,1,0:T(8,128)(2,1)}, u32[]{:S(2)}, u32[]{:S(2)}) collective-permute-start(bf16[9,160,640]{2,1,0:T(8,128)(2,1)} %get-tuple-element.433), channel_id=1, source_target_pairs={{4,0},{9,5},{13,9},{6,2},{11,7},{15,11},{20,16},{25,21},{29,25},{2... | collective-permute-start | bytes 5529608 | tf_op jit(solution)/shard_map/ppermute | solution.py:157
  87.0 23.2 %collective-permute-start.7 = (bf16[9,160,640]{2,1,0:T(8,128)(2,1)}, bf16[9,160,640]{2,1,0:T(8,128)(2,1)}, u32[]{:S(2)}, u32[]{:S(2)}) collective-permute-start(bf16[9,160,640]{2,1,0:T(8,128)(2,1)} %collective-permute-done.6), channel_id=1, source_target_pairs={{1,17},{5,21},{17,1},{21,5},{3,19},{7,23},{19,3},{23,7}} | collective-permute-start | bytes 5529608 | tf_op jit(solution)/shard_map/ppermute | solution.py:164
  88.9 23.2 %collective-permute-start.13 = (bf16[9,160,640]{2,1,0:T(8,128)(2,1)}, bf16[9,160,640]{2,1,0:T(8,128)(2,1)}, u32[]{:S(2)}, u32[]{:S(2)}) collective-permute-start(bf16[9,160,640]{2,1,0:T(8,128)(2,1)} %collective-permute-done.12), channel_id=1, source_target_pairs={{8,24},{12,28},{24,8},{28,12},{10,26},{14,30},{26,10},{30,14}} | collective-permute-start | bytes 5529608 | tf_op jit(solution)/shard_map/ppermute | solution.py:164
  90.9 21.2 %collective-permute-start.9 = (bf16[9,160,640]{2,1,0:T(8,128)(2,1)}, bf16[9,160,640]{2,1,0:T(8,128)(2,1)}, u32[]{:S(2)}, u32[]{:S(2)}) collective-permute-start(bf16[9,160,640]{2,1,0:T(8,128)(2,1)} %collective-permute-done.8), channel_id=1, source_target_pairs={{1,17},{17,1},{3,19},{19,3}} | collective-permute-start | bytes 5529608 | tf_op jit(solution)/shard_map/ppermute | solution.py:164
  92.8 19.3 %collective-permute-start.15 = (bf16[9,160,640]{2,1,0:T(8,128)(2,1)}, bf16[9,160,640]{2,1,0:T(8,128)(2,1)}, u32[]{:S(2)}, u32[]{:S(2)}) collective-permute-start(bf16[9,160,640]{2,1,0:T(8,128)(2,1)} %collective-permute-done.14), channel_id=1, source_target_pairs={{12,28},{28,12},{14,30},{30,14}} | collective-permute-start | bytes 5529608 | tf_op jit(solution)/shard_map/ppermute | solution.py:164
  108.2 56.0 %collective-permute-start.32 = (bf16[9,160,640]{2,1,0:T(8,128)(2,1)}, bf16[9,160,640]{2,1,0:T(8,128)(2,1)}, u32[]{:S(2)}, u32[]{:S(2)}) collective-permute-start(bf16[9,160,640]{2,1,0:T(8,128)(2,1)} %collective-permute-done.30), channel_id=1, source_target_pairs={{4,8},{8,12},{6,10},{10,14},{20,24},{24,28},{22,26},{26,30}} | collective-permute-start | bytes 5529608 | tf_op jit(solution)/shard_map/ppermute | solution.py:157
  110.2 55.9 %collective-permute-start.26 = (bf16[9,160,640]{2,1,0:T(8,128)(2,1)}, bf16[9,160,640]{2,1,0:T(8,128)(2,1)}, u32[]{:S(2)}, u32[]{:S(2)}) collective-permute-start(bf16[9,160,640]{2,1,0:T(8,128)(2,1)} %collective-permute-done.24), channel_id=1, source_target_pairs={{5,1},{9,5},{7,3},{11,7},{21,17},{25,21},{23,19},{27,23}} | collective-permute-start | bytes 5529608 | tf_op jit(solution)/shard_map/ppermute | solution.py:157
  148.6 21.0 %collective-permute-start.16 = (bf16[640,6,128]{2,0,1:T(8,128)(2,1)}, bf16[640,6,128]{2,0,1:T(8,128)(2,1)}, u32[]{:S(2)}, u32[]{:S(2)}) collective-permute-start(bf16[640,6,128]{2,0,1:T(8,128)(2,1)} %bitcast.140), channel_id=1, source_target_pairs={{1,2},{2,1},{5,6},{6,5},{9,10},{10,9},{13,14},{14,13},{17,18},{18,... | collective-permute-start | bytes 2949128 | tf_op jit(solution)/shard_map/ppermute | solution.py:216
  152.5 30.9 %collective-permute-start.17 = (bf16[640,6,128]{2,0,1:T(8,128)(2,1)}, bf16[640,6,128]{2,0,1:T(8,128)(2,1)}, u32[]{:S(2)}, u32[]{:S(2)}) collective-permute-start(bf16[640,6,128]{2,0,1:T(8,128)(2,1)} %bitcast.141), channel_id=1, source_target_pairs={{0,1},{3,2},{1,3},{2,0},{4,5},{7,6},{5,7},{6,4},{8,9},{11,10},{9,1... | collective-permute-start | bytes 2949128 | tf_op jit(solution)/shard_map/ppermute | solution.py:215
  162.2 50.9 %collective-permute-start.31 = (bf16[9,160,640]{2,1,0:T(8,128)(2,1)}, bf16[9,160,640]{2,1,0:T(8,128)(2,1)}, u32[]{:S(2)}, u32[]{:S(2)}) collective-permute-start(bf16[9,160,640]{2,1,0:T(8,128)(2,1)} %collective-permute-done.30), channel_id=1, source_target_pairs={{4,20},{8,24},{13,29},{20,4},{24,8},{29,13},{6,22},{10,26},{15,31}... | collective-permute-start | bytes 5529608 | tf_op jit(solution)/shard_map/ppermute | solution.py:164
  164.2 50.3 %collective-permute-start.34 = (bf16[9,160,640]{2,1,0:T(8,128)(2,1)}, bf16[9,160,640]{2,1,0:T(8,128)(2,1)}, u32[]{:S(2)}, u32[]{:S(2)}) collective-permute-start(bf16[9,160,640]{2,1,0:T(8,128)(2,1)} %collective-permute-done.32), channel_id=1, source_target_pairs={{8,12},{10,14},{24,28},{26,30}} | collective-permute-start | bytes 5529608 | tf_op jit(solution)/shard_map/ppermute | solution.py:157
  166.1 50.3 %collective-permute-start.28 = (bf16[9,160,640]{2,1,0:T(8,128)(2,1)}, bf16[9,160,640]{2,1,0:T(8,128)(2,1)}, u32[]{:S(2)}, u32[]{:S(2)}) collective-permute-start(bf16[9,160,640]{2,1,0:T(8,128)(2,1)} %collective-permute-done.26), channel_id=1, source_target_pairs={{5,1},{7,3},{21,17},{23,19}} | collective-permute-start | bytes 5529608 | tf_op jit(solution)/shard_map/ppermute | solution.py:157
  192.3 31.8 %collective-permute-start.25 = (bf16[9,160,640]{2,1,0:T(8,128)(2,1)}, bf16[9,160,640]{2,1,0:T(8,128)(2,1)}, u32[]{:S(2)}, u32[]{:S(2)}) collective-permute-start(bf16[9,160,640]{2,1,0:T(8,128)(2,1)} %collective-permute-done.24), channel_id=1, source_target_pairs={{0,16},{5,21},{9,25},{16,0},{21,5},{25,9},{2,18},{7,23},{11,27},{1... | collective-permute-start | bytes 5529608 | tf_op jit(solution)/shard_map/ppermute | solution.py:164
  265.2 41.5 %collective-permute-start.36 = (bf16[640,6,128]{2,0,1:T(8,128)(2,1)}, bf16[640,6,128]{2,0,1:T(8,128)(2,1)}, u32[]{:S(2)}, u32[]{:S(2)}) collective-permute-start(bf16[640,6,128]{2,0,1:T(8,128)(2,1)} %bitcast.142), channel_id=1, source_target_pairs={{1,2},{2,1},{5,6},{6,5},{9,10},{10,9},{13,14},{14,13},{17,18},{18,... | collective-permute-start | bytes 2949128 | tf_op jit(solution)/shard_map/ppermute | solution.py:216
  269.1 57.6 %collective-permute-start.37 = (bf16[640,6,128]{2,0,1:T(8,128)(2,1)}, bf16[640,6,128]{2,0,1:T(8,128)(2,1)}, u32[]{:S(2)}, u32[]{:S(2)}) collective-permute-start(bf16[640,6,128]{2,0,1:T(8,128)(2,1)} %bitcast.143), channel_id=1, source_target_pairs={{0,1},{3,2},{1,3},{2,0},{4,5},{7,6},{5,7},{6,4},{8,9},{11,10},{9,1... | collective-permute-start | bytes 2949128 | tf_op jit(solution)/shard_map/ppermute | solution.py:215
  (35 other events, 857.3 us)

commit v6 on v5

--- a/solution.py
+++ b/solution.py
@@ -189,8 +189,9 @@
 def full_width(block):
     other = swap(block, "col")
     c = lax.axis_index("col")
-    left = jnp.where(c == 0, block, other)
-    right = jnp.where(c == 0, other, block)
+    pair = jnp.stack([block, other])
+    left = lax.dynamic_index_in_dim(pair, c, axis=0, keepdims=False)
+    right = lax.dynamic_index_in_dim(pair, 1 - c, axis=0, keepdims=False)
     return jnp.concatenate([left, right], axis=2)
 
 

time: 332 us -> 353 us (1.063); the launches traced: 330 us -> 347 us
  waiting for transfers between devices: 82.9 us -> 92.4 us
  loops' own time: 0.05 us -> 8.89 us
  local copies, waits for them, and re-layouts: 50.7 us -> 45.9 us
    unnamed x52 -> x43, local copies, waits for them, and re-layouts: 26.5 us -> 10.7 us
    another operation x2, loops' own time: 0.05 us -> 8.89 us  [line_weights(): return (lax.switch(index, cases, *operands), lines)]
    ppermute x2, waiting for transfers between devices: 33.8 us -> 41.8 us  [reduce_cores(): lax.ppermute(send_a, ('chan', 'col'), [(0, 1), (3, 2), (1, 3), (2, 0)])]
    ppermute x12, waiting for transfers between devices: 10.3 us -> 17.6 us  [line_weights(): got = lax.ppermute(last[d], ('patch', 'col'), pairs)]
    dynamic_slice x0 -> x5, local copies, waits for them, and re-layouts: none -> 5.83 us  [the longest x2 2.25 us: full_width(): left = lax.dynamic_index_in_dim(pair, c, axis=0, keepdims=False)]
    another operation x2 -> x4, other arithmetic: 2.11 us -> 6.5 us  [the longest x2 4.56 us: full_width(): pair = jnp.stack([block, other])]
    ppermute x4, waiting for transfers between devices: 23.4 us -> 19.3 us  [group_moments(): lax.ppermute(summed, 'patch', [(i, i ^ step) for i in range(n_p)])]
  transfers between devices with their start and end apart: 38 -> 38, of which waited for: 11 -> 10; matrix products, arithmetic and copies ran while one was open for 24% -> 20% of each run, Pallas kernels for 0% -> 0%
where the time goes in v6:
time: 353 us; the launch traced here: 347 us
  starting transfers between devices  125 us (35%)
  waiting for transfers between devices  92.4 us (26%)
  local copies, waits for them, and re-layouts  45.9 us (13%)
  other arithmetic  36.6 us (10%)
  matrix products  35.9 us (10%)
  loops' own time  8.89 us (3%)
    ppermute x2, starting transfers between devices, reduce_cores(): lax.ppermute(send_a, ('chan', 'col'), [(0, 1), (3, 2), (1, 3), (2, 0)])  43.4 us
    ppermute x2, waiting for transfers between devices, reduce_cores(): lax.ppermute(send_a, ('chan', 'col'), [(0, 1), (3, 2), (1, 3), (2, 0)])  41.8 us
    conv_general_dilated x2, matrix products, conv_full(): lax.conv_general_dilated(padded[None], kernel, window_strides=(1, 1), pad...  35.6 us
    ppermute x12, starting transfers between devices, line_weights(): got = lax.ppermute(last[d], ('patch', 'col'), pairs)  31.7 us
    ppermute x12, starting transfers between devices, line_weights(): bufs[t, d, 'o'] = lax.ppermute(got, ('groups', 'patch', 'col'), trade)  27 us
    ppermute x4, waiting for transfers between devices, group_moments(): lax.ppermute(summed, 'patch', [(i, i ^ step) for i in range(n_p)])  19.3 us
    ppermute x12, waiting for transfers between devices, line_weights(): got = lax.ppermute(last[d], ('patch', 'col'), pairs)  17.6 us
    ppermute x4, starting transfers between devices, group_moments(): lax.ppermute(summed, 'patch', [(i, i ^ step) for i in range(n_p)])  15.9 us
  transfers between devices with their start and end apart: 38, of which 10 were waited for; matrix products, arithmetic and copies ran while one was open for 20% of the time, Pallas kernels for 0%

profile of v6, /device:TPU:0, one launch (start us, length us, event | category | flops | bytes accessed | tf_op | source)
XLA Modules:
  0.0 346.8 jit_solution(9377638562413190014)
XLA Ops:
  0.0 3.8 %constant_dynamic-slice_fusion.2 = (bf16[9,160,640]{2,1,0:T(8,128)(2,1)}, bf16[9,160,640]{2,1,0:T(8,128)(2,1)S(1)}) fusion(bf16[9,320,640]{2,1,0:T(8,128)(2,1)} %bitcast.158, s32[]{:T(128)S(6)} %select_n.50, s32[]{:T(128)S(6)} %select_n.49), kind=kLoop, calls=%fused_computation.112 | loop fusion | bytes 7372808 | tf_op jit(solution)/shard_map/dynamic_slice | solution.py:144
  5.1 7.5 %collective-permute-start.10 = (bf16[9,160,640]{2,1,0:T(8,128)(2,1)S(1)}, bf16[9,160,640]{2,1,0:T(8,128)(2,1)}, u32[]{:S(2)}, u32[]{:S(2)}) collective-permute-start(bf16[9,160,640]{2,1,0:T(8,128)(2,1)S(1)} %get-tuple-element.431), channel_id=1, source_target_pairs={{0,4},{4,8},{9,13},{2,6},{6,10},{11,15},{16,20},{20,24},{25,29},{1... | collective-permute-start | bytes 5529608 | tf_op jit(solution)/shard_map/ppermute | solution.py:157
  18.8 13.3 %collective-permute-done.1 = f32[2,16]{1,0:T(2,128)S(1)} collective-permute-done((f32[2,16]{1,0:T(2,128)S(1)}, f32[2,16]{1,0:T(2,128)S(1)}, u32[]{:S(2)}, u32[]{:S(2)}) %collective-permute-start.1) | collective-permute-done | bytes 160 | tf_op jit(solution)/shard_map/ppermute | solution.py:39
  32.3 4.5 %collective-permute-done.2 = f32[2,16]{1,0:T(2,128)S(1)} collective-permute-done((f32[2,16]{1,0:T(2,128)S(1)}, f32[2,16]{1,0:T(2,128)S(1)}, u32[]{:S(2)}, u32[]{:S(2)}) %collective-permute-start.2) | collective-permute-done | bytes 160 | tf_op jit(solution)/shard_map/ppermute | solution.py:39
  46.5 6.3 %collective-permute-start.30 = (bf16[9,160,640]{2,1,0:T(8,128)(2,1)}, bf16[9,160,640]{2,1,0:T(8,128)(2,1)}, u32[]{:S(2)}, u32[]{:S(2)}) collective-permute-start(bf16[9,160,640]{2,1,0:T(8,128)(2,1)} %get-tuple-element.433), channel_id=1, source_target_pairs={{0,4},{4,8},{9,13},{2,6},{6,10},{11,15},{16,20},{20,24},{25,29},{1... | collective-permute-start | bytes 5529608 | tf_op jit(solution)/shard_map/ppermute | solution.py:157
  52.8 4.5 %collective-permute-start.5 = (bf16[9,160,640]{2,1,0:T(8,128)(2,1)}, bf16[9,160,640]{2,1,0:T(8,128)(2,1)}, u32[]{:S(2)}, u32[]{:S(2)}) collective-permute-start(bf16[9,160,640]{2,1,0:T(8,128)(2,1)} %collective-permute-done.4), channel_id=1, source_target_pairs={{0,16},{5,21},{9,25},{16,0},{21,5},{25,9},{2,18},{7,23},{11,27},{1... | collective-permute-start | bytes 5529608 | tf_op jit(solution)/shard_map/ppermute | solution.py:164
  63.0 9.7 %collective-permute-done.30 = bf16[9,160,640]{2,1,0:T(8,128)(2,1)} collective-permute-done((bf16[9,160,640]{2,1,0:T(8,128)(2,1)}, bf16[9,160,640]{2,1,0:T(8,128)(2,1)}, u32[]{:S(2)}, u32[]{:S(2)}) %collective-permute-start.30) | collective-permute-done | bytes 1843232 | tf_op jit(solution)/shard_map/ppermute | solution.py:157
  74.0 11.5 %collective-permute-done.5 = bf16[9,160,640]{2,1,0:T(8,128)(2,1)} collective-permute-done((bf16[9,160,640]{2,1,0:T(8,128)(2,1)}, bf16[9,160,640]{2,1,0:T(8,128)(2,1)}, u32[]{:S(2)}, u32[]{:S(2)}) %collective-permute-start.5) | collective-permute-done | bytes 1843232 | tf_op jit(solution)/shard_map/ppermute | solution.py:164
  100.4 7.9 %collective-permute-done.24 = bf16[9,160,640]{2,1,0:T(8,128)(2,1)} collective-permute-done((bf16[9,160,640]{2,1,0:T(8,128)(2,1)}, bf16[9,160,640]{2,1,0:T(8,128)(2,1)}, u32[]{:S(2)}, u32[]{:S(2)}) %collective-permute-start.24) | collective-permute-done | bytes 1843232 | tf_op jit(solution)/shard_map/ppermute | solution.py:157
  112.1 15.4 %conditional.2 = (bf16[3,3,640,640]{3,2,1,0:T(8,128)(2,1)}) conditional(s32[]{:T(128)} %clamp.4, (bf16[9,160,640]{2,1,0:T(8,128)(2,1)S(1)}, bf16[9,160,640]{2,1,0:T(8,128)(2,1)S(1)}, bf16[9,160,640]{2,1,0:T(8,128)(2,1)}, bf16[9,160,640]{2,1,0:T(8,128)(2,1)}) %tuple.211, (bf16[9,160,640]{2,1,0:T(8,128)(2,1)}, ...), branch_computations={%region_4.0_spmd, %region_5.0_spmd, %region_6.0_spmd, %region_7.0_... | conditional | flops 29491200 | bytes 14745608 | solution.py:186
  112.1 6.5 %pad_maximum_fusion = bf16[9,640,640]{2,1,0:T(8,128)(2,1)} fusion(bf16[9,160,640]{2,1,0:T(8,128)(2,1)} %get-tuple-element.273, bf16[9,160,640]{2,1,0:T(8,128)(2,1)} %get-tuple-element.272, bf16[9,160,640]{2,1,0:T(8,128)(2,1)S(1)} %get-tuple-element.271, bf16[9,160,640]{2,1,0:T(8,128)(2,1)S(1)} %get-tuple-element.270), kind=kLoop, calls=%fused_computation | loop fusion | flops 29491200 | bytes 14745600 | tf_op jit(solution)/shard_map/cond/branch_0_fun/concatenate | solution.py:181
  127.5 18.2 %select_convert_fusion.1 = bf16[6,8,33,640]{3,1,2,0:T(8,128)(2,1)S(1)} fusion(pred[8,33]{0,1:T(8,128)(4,1)S(1)} %copy-done.19, bf16[3,3,640,640]{3,2,1,0:T(8,128)(2,1)} %get-tuple-element.452, bf16[640,8,1,7,2]{0,3,4,1,2:T(8,128)(2,1)} %slice.38, bf16[640,8,1,8,33]{0,3,4,1,2:T(8,128)(2,1)} %copy-done.8), kind=kOutput, calls=%fused_computation.36 | convolution fusion | flops 11689144320 | bytes 12247304 | tf_op jit(solution)/shard_map/conv_general_dilated | solution.py:200
  147.5 4.1 %reshape.207 = bf16[6,1,264,640]{3,2,0,1:T(8,128)(2,1)} reshape(bf16[6,8,33,640]{3,2,1,0:T(8,128)(2,1)} %copy.46) | data formatting | bytes 4055040 | tf_op jit(solution)/shard_map/convert_element_type | solution.py:208
  157.8 8.0 %collective-permute-start.17 = (bf16[640,6,128]{0,2,1:T(8,128)(2,1)}, bf16[640,6,128]{0,2,1:T(8,128)(2,1)}, u32[]{:S(2)}, u32[]{:S(2)}) collective-permute-start(bf16[640,6,128]{0,2,1:T(8,128)(2,1)} %get-tuple-element.441), channel_id=1, source_target_pairs={{0,1},{3,2},{1,3},{2,0},{4,5},{7,6},{5,7},{6,4},{8,9},{11,10},{9,1... | collective-permute-start | bytes 2949128 | tf_op jit(solution)/shard_map/ppermute | solution.py:216
  172.6 17.6 %collective-permute-done.17 = bf16[640,6,128]{0,2,1:T(8,128)(2,1)} collective-permute-done((bf16[640,6,128]{0,2,1:T(8,128)(2,1)}, bf16[640,6,128]{0,2,1:T(8,128)(2,1)}, u32[]{:S(2)}, u32[]{:S(2)}) %collective-permute-start.17) | collective-permute-done | bytes 983072 | tf_op jit(solution)/shard_map/ppermute | solution.py:216
  201.7 12.5 %collective-permute-start.20 = (f32[2,16]{1,0:T(2,128)S(1)}, f32[2,16]{1,0:T(2,128)S(1)}, u32[]{:S(2)}, u32[]{:S(2)}) collective-permute-start(f32[2,16]{1,0:T(2,128)S(1)} %fusion.67), channel_id=1, source_target_pairs={{0,8},{4,12},{8,0},{12,4},{1,9},{5,13},{9,1},{13,5},{2,10},{6,14},... | collective-permute-start | bytes 392 | tf_op jit(solution)/shard_map/ppermute | solution.py:39
  218.1 3.5 %collective-permute-start.21 = (bf16[640,1,128]{0,2,1:T(8,128)(2,1)S(1)}, bf16[640,1,128]{0,2,1:T(8,128)(2,1)S(1)}, u32[]{:S(2)}, u32[]{:S(2)}) collective-permute-start(bf16[640,1,128]{0,2,1:T(8,128)(2,1)S(1)} %get-tuple-element.444), channel_id=1, source_target_pairs={{0,4},{4,8},{8,12},{1,5},{5,9},{9,13},{2,6},{6,10},{10,14},{3,7},{... | collective-permute-start | bytes 491528 | tf_op jit(solution)/shard_map/ppermute | solution.py:21
  233.3 7.4 %conditional.3 = (bf16[3,3,640,640]{3,2,1,0:T(8,128)(2,1)}) conditional(s32[]{:T(128)} %clamp.4, (bf16[9,160,640]{2,1,0:T(8,128)(2,1)}, bf16[9,160,640]{2,1,0:T(8,128)(2,1)S(1)}, bf16[9,160,640]{2,1,0:T(8,128)(2,1)}, bf16[9,160,640]{2,1,0:T(8,128)(2,1)}) %tuple.145, (bf16[9,160,640]{2,1,0:T(8,128)(2,1)}, ...), branch_computations={%region_24.0_spmd, %region_25.0_spmd, %region_26.0_spmd, %region_2... | conditional | flops 29491200 | bytes 14745608 | solution.py:186
  233.3 7.4 %pad_maximum_fusion.16 = bf16[9,640,640]{2,1,0:T(8,128)(2,1)} fusion(bf16[9,160,640]{2,1,0:T(8,128)(2,1)} %get-tuple-element.364, bf16[9,160,640]{2,1,0:T(8,128)(2,1)} %get-tuple-element.363, bf16[9,160,640]{2,1,0:T(8,128)(2,1)S(1)} %get-tuple-element.362, bf16[9,160,640]{2,1,0:T(8,128)(2,1)} %get-tuple-element.361), kind=kLoop, calls=%fused_computation.16 | loop fusion | flops 29491200 | bytes 14745600 | tf_op jit(solution)/shard_map/cond/branch_0_fun/concatenate | solution.py:181
  250.4 4.0 %copy.54 = bf16[640,8,1,256]{0,1,3,2:T(8,128)(2,1)} copy(bf16[640,8,1,256]{3,1,0,2:T(8,128)(2,1)S(1)} %maximum_bitcast_fusion.1) | data formatting | bytes 5242880
  256.8 17.4 %select_convert_fusion = bf16[6,8,33,640]{3,1,2,0:T(8,128)(2,1)S(1)} fusion(pred[8,33]{0,1:T(8,128)(4,1)S(1)} %copy-done.19, bf16[3,3,640,640]{3,2,1,0:T(8,128)(2,1)} %get-tuple-element.453, bf16[640,8,1,7,2]{0,3,4,1,2:T(8,128)(2,1)S(1)} %slice.42, bf16[640,8,1,8,33]{0,3,4,1,2:T(8,128)(2,1)S(1)} %copy.51), kind=kOutput, calls=%fused_computation.35 | convolution fusion | flops 11689144320 | bytes 12247304 | tf_op jit(solution)/shard_map/conv_general_dilated | solution.py:200
  276.1 4.2 %reshape.214 = bf16[6,1,264,640]{3,2,0,1:T(8,128)(2,1)} reshape(bf16[6,8,33,640]{3,2,1,0:T(8,128)(2,1)} %copy.52) | data formatting | bytes 4055040 | tf_op jit(solution)/shard_map/convert_element_type | solution.py:208
  283.0 35.4 %collective-permute-start.37 = (bf16[640,6,128]{0,2,1:T(8,128)(2,1)S(1)}, bf16[640,6,128]{0,2,1:T(8,128)(2,1)S(1)}, u32[]{:S(2)}, u32[]{:S(2)}) collective-permute-start(bf16[640,6,128]{0,2,1:T(8,128)(2,1)S(1)} %get-tuple-element.439), channel_id=1, source_target_pairs={{0,1},{3,2},{1,3},{2,0},{4,5},{7,6},{5,7},{6,4},{8,9},{11,10},{9,1... | collective-permute-start | bytes 2949128 | tf_op jit(solution)/shard_map/ppermute | solution.py:216
  318.4 24.2 %collective-permute-done.37 = bf16[640,6,128]{0,2,1:T(8,128)(2,1)S(1)} collective-permute-done((bf16[640,6,128]{0,2,1:T(8,128)(2,1)S(1)}, bf16[640,6,128]{0,2,1:T(8,128)(2,1)S(1)}, u32[]{:S(2)}, u32[]{:S(2)}) %collective-permute-start.37) | collective-permute-done | bytes 983072 | tf_op jit(solution)/shard_map/ppermute | solution.py:216
  (169 shorter events, 104.2 us)
Async XLA Ops:
  3.8 34.8 %collective-permute-start.4 = (bf16[9,160,640]{2,1,0:T(8,128)(2,1)S(1)}, bf16[9,160,640]{2,1,0:T(8,128)(2,1)}, u32[]{:S(2)}, u32[]{:S(2)}) collective-permute-start(bf16[9,160,640]{2,1,0:T(8,128)(2,1)S(1)} %get-tuple-element.431), channel_id=1, source_target_pairs={{4,0},{9,5},{13,9},{6,2},{11,7},{15,11},{20,16},{25,21},{29,25},{2... | collective-permute-start | bytes 5529608 | tf_op jit(solution)/shard_map/ppermute | solution.py:157
  5.1 35.5 %collective-permute-start.10 = (bf16[9,160,640]{2,1,0:T(8,128)(2,1)S(1)}, bf16[9,160,640]{2,1,0:T(8,128)(2,1)}, u32[]{:S(2)}, u32[]{:S(2)}) collective-permute-start(bf16[9,160,640]{2,1,0:T(8,128)(2,1)S(1)} %get-tuple-element.431), channel_id=1, source_target_pairs={{0,4},{4,8},{9,13},{2,6},{6,10},{11,15},{16,20},{20,24},{25,29},{1... | collective-permute-start | bytes 5529608 | tf_op jit(solution)/shard_map/ppermute | solution.py:157
  38.6 20.6 %collective-permute-start.6 = (bf16[9,160,640]{2,1,0:T(8,128)(2,1)}, bf16[9,160,640]{2,1,0:T(8,128)(2,1)}, u32[]{:S(2)}, u32[]{:S(2)}) collective-permute-start(bf16[9,160,640]{2,1,0:T(8,128)(2,1)} %collective-permute-done.4), channel_id=1, source_target_pairs={{5,1},{9,5},{7,3},{11,7},{21,17},{25,21},{23,19},{27,23}} | collective-permute-start | bytes 5529608 | tf_op jit(solution)/shard_map/ppermute | solution.py:157
  40.6 20.5 %collective-permute-start.12 = (bf16[9,160,640]{2,1,0:T(8,128)(2,1)}, bf16[9,160,640]{2,1,0:T(8,128)(2,1)}, u32[]{:S(2)}, u32[]{:S(2)}) collective-permute-start(bf16[9,160,640]{2,1,0:T(8,128)(2,1)} %collective-permute-done.10), channel_id=1, source_target_pairs={{4,8},{8,12},{6,10},{10,14},{20,24},{24,28},{22,26},{26,30}} | collective-permute-start | bytes 5529608 | tf_op jit(solution)/shard_map/ppermute | solution.py:157
  46.5 26.2 %collective-permute-start.30 = (bf16[9,160,640]{2,1,0:T(8,128)(2,1)}, bf16[9,160,640]{2,1,0:T(8,128)(2,1)}, u32[]{:S(2)}, u32[]{:S(2)}) collective-permute-start(bf16[9,160,640]{2,1,0:T(8,128)(2,1)} %get-tuple-element.433), channel_id=1, source_target_pairs={{0,4},{4,8},{9,13},{2,6},{6,10},{11,15},{16,20},{20,24},{25,29},{1... | collective-permute-start | bytes 5529608 | tf_op jit(solution)/shard_map/ppermute | solution.py:157
  52.8 32.7 %collective-permute-start.5 = (bf16[9,160,640]{2,1,0:T(8,128)(2,1)}, bf16[9,160,640]{2,1,0:T(8,128)(2,1)}, u32[]{:S(2)}, u32[]{:S(2)}) collective-permute-start(bf16[9,160,640]{2,1,0:T(8,128)(2,1)} %collective-permute-done.4), channel_id=1, source_target_pairs={{0,16},{5,21},{9,25},{16,0},{21,5},{25,9},{2,18},{7,23},{11,27},{1... | collective-permute-start | bytes 5529608 | tf_op jit(solution)/shard_map/ppermute | solution.py:164
  57.3 30.1 %collective-permute-start.11 = (bf16[9,160,640]{2,1,0:T(8,128)(2,1)}, bf16[9,160,640]{2,1,0:T(8,128)(2,1)}, u32[]{:S(2)}, u32[]{:S(2)}) collective-permute-start(bf16[9,160,640]{2,1,0:T(8,128)(2,1)} %collective-permute-done.10), channel_id=1, source_target_pairs={{4,20},{8,24},{13,29},{20,4},{24,8},{29,13},{6,22},{10,26},{15,31}... | collective-permute-start | bytes 5529608 | tf_op jit(solution)/shard_map/ppermute | solution.py:164
  59.3 30.1 %collective-permute-start.8 = (bf16[9,160,640]{2,1,0:T(8,128)(2,1)}, bf16[9,160,640]{2,1,0:T(8,128)(2,1)}, u32[]{:S(2)}, u32[]{:S(2)}) collective-permute-start(bf16[9,160,640]{2,1,0:T(8,128)(2,1)} %collective-permute-done.6), channel_id=1, source_target_pairs={{5,1},{7,3},{21,17},{23,19}} | collective-permute-start | bytes 5529608 | tf_op jit(solution)/shard_map/ppermute | solution.py:157
  61.2 30.1 %collective-permute-start.14 = (bf16[9,160,640]{2,1,0:T(8,128)(2,1)}, bf16[9,160,640]{2,1,0:T(8,128)(2,1)}, u32[]{:S(2)}, u32[]{:S(2)}) collective-permute-start(bf16[9,160,640]{2,1,0:T(8,128)(2,1)} %collective-permute-done.12), channel_id=1, source_target_pairs={{8,12},{10,14},{24,28},{26,30}} | collective-permute-start | bytes 5529608 | tf_op jit(solution)/shard_map/ppermute | solution.py:157
  72.7 35.5 %collective-permute-start.24 = (bf16[9,160,640]{2,1,0:T(8,128)(2,1)}, bf16[9,160,640]{2,1,0:T(8,128)(2,1)}, u32[]{:S(2)}, u32[]{:S(2)}) collective-permute-start(bf16[9,160,640]{2,1,0:T(8,128)(2,1)} %get-tuple-element.433), channel_id=1, source_target_pairs={{4,0},{9,5},{13,9},{6,2},{11,7},{15,11},{20,16},{25,21},{29,25},{2... | collective-permute-start | bytes 5529608 | tf_op jit(solution)/shard_map/ppermute | solution.py:157
  85.6 24.6 %collective-permute-start.7 = (bf16[9,160,640]{2,1,0:T(8,128)(2,1)}, bf16[9,160,640]{2,1,0:T(8,128)(2,1)}, u32[]{:S(2)}, u32[]{:S(2)}) collective-permute-start(bf16[9,160,640]{2,1,0:T(8,128)(2,1)} %collective-permute-done.6), channel_id=1, source_target_pairs={{1,17},{5,21},{17,1},{21,5},{3,19},{7,23},{19,3},{23,7}} | collective-permute-start | bytes 5529608 | tf_op jit(solution)/shard_map/ppermute | solution.py:164
  87.4 24.6 %collective-permute-start.13 = (bf16[9,160,640]{2,1,0:T(8,128)(2,1)}, bf16[9,160,640]{2,1,0:T(8,128)(2,1)}, u32[]{:S(2)}, u32[]{:S(2)}) collective-permute-start(bf16[9,160,640]{2,1,0:T(8,128)(2,1)} %collective-permute-done.12), channel_id=1, source_target_pairs={{8,24},{12,28},{24,8},{28,12},{10,26},{14,30},{26,10},{30,14}} | collective-permute-start | bytes 5529608 | tf_op jit(solution)/shard_map/ppermute | solution.py:164
  89.4 22.7 %collective-permute-start.9 = (bf16[9,160,640]{2,1,0:T(8,128)(2,1)}, bf16[9,160,640]{2,1,0:T(8,128)(2,1)}, u32[]{:S(2)}, u32[]{:S(2)}) collective-permute-start(bf16[9,160,640]{2,1,0:T(8,128)(2,1)} %collective-permute-done.8), channel_id=1, source_target_pairs={{1,17},{17,1},{3,19},{19,3}} | collective-permute-start | bytes 5529608 | tf_op jit(solution)/shard_map/ppermute | solution.py:164
  91.2 20.8 %collective-permute-start.15 = (bf16[9,160,640]{2,1,0:T(8,128)(2,1)}, bf16[9,160,640]{2,1,0:T(8,128)(2,1)}, u32[]{:S(2)}, u32[]{:S(2)}) collective-permute-start(bf16[9,160,640]{2,1,0:T(8,128)(2,1)} %collective-permute-done.14), channel_id=1, source_target_pairs={{12,28},{28,12},{14,30},{30,14}} | collective-permute-start | bytes 5529608 | tf_op jit(solution)/shard_map/ppermute | solution.py:164
  108.2 60.6 %collective-permute-start.32 = (bf16[9,160,640]{2,1,0:T(8,128)(2,1)}, bf16[9,160,640]{2,1,0:T(8,128)(2,1)}, u32[]{:S(2)}, u32[]{:S(2)}) collective-permute-start(bf16[9,160,640]{2,1,0:T(8,128)(2,1)} %collective-permute-done.30), channel_id=1, source_target_pairs={{4,8},{8,12},{6,10},{10,14},{20,24},{24,28},{22,26},{26,30}} | collective-permute-start | bytes 5529608 | tf_op jit(solution)/shard_map/ppermute | solution.py:157
  110.1 60.6 %collective-permute-start.26 = (bf16[9,160,640]{2,1,0:T(8,128)(2,1)}, bf16[9,160,640]{2,1,0:T(8,128)(2,1)}, u32[]{:S(2)}, u32[]{:S(2)}) collective-permute-start(bf16[9,160,640]{2,1,0:T(8,128)(2,1)} %collective-permute-done.24), channel_id=1, source_target_pairs={{5,1},{9,5},{7,3},{11,7},{21,17},{25,21},{23,19},{27,23}} | collective-permute-start | bytes 5529608 | tf_op jit(solution)/shard_map/ppermute | solution.py:157
  156.2 16.5 %collective-permute-start.16 = (bf16[640,6,128]{0,2,1:T(8,128)(2,1)}, bf16[640,6,128]{0,2,1:T(8,128)(2,1)}, u32[]{:S(2)}, u32[]{:S(2)}) collective-permute-start(bf16[640,6,128]{0,2,1:T(8,128)(2,1)} %get-tuple-element.440), channel_id=1, source_target_pairs={{1,2},{2,1},{5,6},{6,5},{9,10},{10,9},{13,14},{14,13},{17,18},{18,... | collective-permute-start | bytes 2949128 | tf_op jit(solution)/shard_map/ppermute | solution.py:217
  157.8 32.5 %collective-permute-start.17 = (bf16[640,6,128]{0,2,1:T(8,128)(2,1)}, bf16[640,6,128]{0,2,1:T(8,128)(2,1)}, u32[]{:S(2)}, u32[]{:S(2)}) collective-permute-start(bf16[640,6,128]{0,2,1:T(8,128)(2,1)} %get-tuple-element.441), channel_id=1, source_target_pairs={{0,1},{3,2},{1,3},{2,0},{4,5},{7,6},{5,7},{6,4},{8,9},{11,10},{9,1... | collective-permute-start | bytes 2949128 | tf_op jit(solution)/shard_map/ppermute | solution.py:216
  166.8 54.8 %collective-permute-start.31 = (bf16[9,160,640]{2,1,0:T(8,128)(2,1)}, bf16[9,160,640]{2,1,0:T(8,128)(2,1)}, u32[]{:S(2)}, u32[]{:S(2)}) collective-permute-start(bf16[9,160,640]{2,1,0:T(8,128)(2,1)} %collective-permute-done.30), channel_id=1, source_target_pairs={{4,20},{8,24},{13,29},{20,4},{24,8},{29,13},{6,22},{10,26},{15,31}... | collective-permute-start | bytes 5529608 | tf_op jit(solution)/shard_map/ppermute | solution.py:164
  168.8 54.2 %collective-permute-start.34 = (bf16[9,160,640]{2,1,0:T(8,128)(2,1)}, bf16[9,160,640]{2,1,0:T(8,128)(2,1)}, u32[]{:S(2)}, u32[]{:S(2)}) collective-permute-start(bf16[9,160,640]{2,1,0:T(8,128)(2,1)} %collective-permute-done.32), channel_id=1, source_target_pairs={{8,12},{10,14},{24,28},{26,30}} | collective-permute-start | bytes 5529608 | tf_op jit(solution)/shard_map/ppermute | solution.py:157
  170.7 54.2 %collective-permute-start.28 = (bf16[9,160,640]{2,1,0:T(8,128)(2,1)}, bf16[9,160,640]{2,1,0:T(8,128)(2,1)}, u32[]{:S(2)}, u32[]{:S(2)}) collective-permute-start(bf16[9,160,640]{2,1,0:T(8,128)(2,1)} %collective-permute-done.26), channel_id=1, source_target_pairs={{5,1},{7,3},{21,17},{23,19}} | collective-permute-start | bytes 5529608 | tf_op jit(solution)/shard_map/ppermute | solution.py:157
  198.3 34.9 %collective-permute-start.25 = (bf16[9,160,640]{2,1,0:T(8,128)(2,1)}, bf16[9,160,640]{2,1,0:T(8,128)(2,1)}, u32[]{:S(2)}, u32[]{:S(2)}) collective-permute-start(bf16[9,160,640]{2,1,0:T(8,128)(2,1)} %collective-permute-done.24), channel_id=1, source_target_pairs={{0,16},{5,21},{9,25},{16,0},{21,5},{25,9},{2,18},{7,23},{11,27},{1... | collective-permute-start | bytes 5529608 | tf_op jit(solution)/shard_map/ppermute | solution.py:164
  282.2 36.2 %collective-permute-start.36 = (bf16[640,6,128]{0,2,1:T(8,128)(2,1)S(1)}, bf16[640,6,128]{0,2,1:T(8,128)(2,1)S(1)}, u32[]{:S(2)}, u32[]{:S(2)}) collective-permute-start(bf16[640,6,128]{0,2,1:T(8,128)(2,1)S(1)} %get-tuple-element.438), channel_id=1, source_target_pairs={{1,2},{2,1},{5,6},{6,5},{9,10},{10,9},{13,14},{14,13},{17,18},{18,... | collective-permute-start | bytes 2949128 | tf_op jit(solution)/shard_map/ppermute | solution.py:217
  283.0 59.6 %collective-permute-start.37 = (bf16[640,6,128]{0,2,1:T(8,128)(2,1)S(1)}, bf16[640,6,128]{0,2,1:T(8,128)(2,1)S(1)}, u32[]{:S(2)}, u32[]{:S(2)}) collective-permute-start(bf16[640,6,128]{0,2,1:T(8,128)(2,1)S(1)} %get-tuple-element.439), channel_id=1, source_target_pairs={{0,1},{3,2},{1,3},{2,0},{4,5},{7,6},{5,7},{6,4},{8,9},{11,10},{9,1... | collective-permute-start | bytes 2949128 | tf_op jit(solution)/shard_map/ppermute | solution.py:216
  (34 other events, 881.8 us)
